TPU v7x, 256 devices: a whole 4x4x8 slice. The times are simulated.
256 devices in a mesh: expert: 8 (over z), mp: 32 (over x, y, core).
Axes of the slice: x: 4, y: 4, z: 8, core: 2. Of those that a mesh axis runs over, the one named last changes fastest.
Arguments:
- tokens: bfloat16 [4096, 2048], P('expert', 'mp'), may hold values from -6 to 6
- expert_route: int32 [4096, 2], P('expert'), may hold values from 0 to 7, all different within a row; in each aligned block of 512 rows (0 to 511, 512 to 1023, ...) at most 256 rows name the same one
- route_gate: float32 [4096, 2], P('expert'), may hold values from 0.05 to 1
- request_lengths: int32 [32], replicated, may hold values from 1 to 1024, 4096 in all
- request_adapter: int32 [32], replicated, may hold values from 0 to 63, as said below
- request_order: int32 [32], replicated, may hold values from 0 to 31, each once
- gate_weight: bfloat16 [8, 5632, 2048], P('expert', 'mp'), may hold values from -0.125 to 0.125
- up_weight: bfloat16 [8, 5632, 2048], P('expert', 'mp'), may hold values from -0.125 to 0.125
- down_weight: bfloat16 [8, 5632, 2048], P('expert', 'mp'), may hold values from -0.15625 to 0.15625
- adapter_in: bfloat16 [8, 1024, 2048], P('expert', 'mp'), may hold values from -0.125 to 0.125
- adapter_out: bfloat16 [8, 5632, 1024], P('expert', 'mp'), may hold values from -1.5 to 1.5
Outputs:
- mixed: bfloat16 [4096, 2048], P('expert', 'mp')
Inputs may be any that keep to these rules, and one draw needn't show every extreme that they name: `expert_route`: the two entries of a row differ; within each aligned block of 512 rows (the tokens held at one position along `expert`) no expert is named by more than 256 rows, and in some block some expert is named by exactly 256 rows. `request_lengths`: they sum to 4096; the largest is 1024. `request_order`: each request index appears once. `request_adapter`: exactly 16 different adapters appear.
All inputs are finite; a program needn't handle non-finite values.
Results may differ from a plain program's by a relative error of at most 0.035.
Values may be sent and summed in bfloat16 or wider, within the bound.
No kernel may reach another device: no remote copies, remote signals or barrier semaphores. Data moves between devices by JAX's collectives and lax.ppermute only.
A program may use at most 64 MiB of HBM per device.

v0:
```python
import jax
import jax.numpy as jnp
from jax import lax
from jax.sharding import PartitionSpec as P

RANK = 16
ADAPTERS = 64


def token_adapters(request_lengths, request_adapter, request_order, first_token, token_count):
    request_ids = jnp.arange(request_lengths.shape[0], dtype=jnp.int32)
    chosen = (request_order[:, None] == request_ids[None, :]).astype(jnp.int32)
    packed_lengths = jnp.sum(chosen * request_lengths[None, :], axis=1, dtype=jnp.int32)
    packed_adapters = jnp.sum(chosen * request_adapter[None, :], axis=1, dtype=jnp.int32)
    boundary = jnp.cumsum(packed_lengths, dtype=jnp.int32)
    positions = first_token + jnp.arange(token_count, dtype=jnp.int32)
    packed_index = jnp.sum(
        (boundary[None, :] <= positions[:, None]).astype(jnp.int32), axis=1, dtype=jnp.int32
    )
    matches = (packed_index[:, None] == request_ids[None, :]).astype(jnp.int32)
    return jnp.sum(matches * packed_adapters[None, :], axis=1, dtype=jnp.int32)


def expert_slots(routes, groups, capacity):
    flat_routes = routes.reshape(-1)
    one_hot = (flat_routes[:, None] == jnp.arange(groups, dtype=jnp.int32)[None, :]).astype(
        jnp.int32
    )
    before = jnp.cumsum(one_hot, axis=0, dtype=jnp.int32) - one_hot
    seat_index = jnp.sum(before * one_hot, axis=1, dtype=jnp.int32)
    return (flat_routes * capacity + seat_index).reshape(routes.shape)


def contract_last(left, right):
    return lax.dot_general(
        left, right, (((1,), (1,)), ((), ())), preferred_element_type=jnp.float32
    )


def on_device(
    tokens,
    expert_route,
    route_gate,
    request_lengths,
    request_adapter,
    request_order,
    gate_weight,
    up_weight,
    down_weight,
    adapter_in,
    adapter_out,
):
    tok_rows = tokens.shape[0]
    groups = lax.axis_size("expert")
    capacity = 4 * tok_rows // groups
    total_slots = groups * capacity
    source_group = lax.axis_index("expert")
    adapter_of = token_adapters(
        request_lengths, request_adapter, request_order, source_group * tok_rows, tok_rows
    )
    slot_index = expert_slots(expert_route, groups, capacity)
    flat_slots = slot_index.reshape(-1)
    flat_tokens = jnp.broadcast_to(
        jnp.arange(tok_rows, dtype=jnp.int32)[:, None], slot_index.shape
    ).reshape(-1)
    slot_token = jnp.zeros((total_slots,), jnp.int32).at[flat_slots].set(flat_tokens)
    filled = jnp.zeros((total_slots,), jnp.bool_).at[flat_slots].set(True)
    slot_adapter = jnp.where(filled, adapter_of[slot_token], -1)
    gate_w = gate_weight[0]
    up_w = up_weight[0]
    rank_w = adapter_in[0]
    blank = jnp.zeros((), tokens.dtype)
    full_rows = lax.all_gather(tokens, "mp", axis=1, tiled=True)
    send_rows = jnp.where(filled[:, None], full_rows[slot_token], blank)
    arrived, arrived_adapter = (
        lax.all_to_all(send_rows, "expert", split_axis=0, concat_axis=0, tiled=True),
        lax.all_to_all(slot_adapter, "expert", split_axis=0, concat_axis=0, tiled=True),
    )
    gate_pre = contract_last(arrived, gate_w)
    up_base = contract_last(arrived, up_w)
    rank_cols = contract_last(arrived, rank_w)
    row_count = arrived.shape[0]
    per_device = rank_w.shape[0] // RANK
    local_adapter = arrived_adapter - lax.axis_index("mp") * per_device
    local_pick = (
        local_adapter[:, None] == jnp.arange(per_device, dtype=jnp.int32)[None, :]
    ).astype(jnp.float32)
    rank_part = jnp.sum(
        rank_cols.reshape(row_count, per_device, RANK) * local_pick[:, :, None], axis=1
    )
    rank = lax.psum(rank_part.astype(jnp.bfloat16), "mp")
    chosen = (arrived_adapter[:, None] == jnp.arange(ADAPTERS, dtype=jnp.int32)[None, :]).astype(
        jnp.bfloat16
    )
    expanded = (rank[:, None, :] * chosen[:, :, None]).reshape(row_count, ADAPTERS * RANK)
    up = up_base + contract_last(expanded, adapter_out[0])
    hidden = (jax.nn.silu(gate_pre) * up).astype(jnp.bfloat16)
    down_w = down_weight[0]
    scattered = lax.psum_scatter(
        lax.dot_general(
            down_w, hidden, (((0,), (1,)), ((), ())), preferred_element_type=jnp.float32
        ).astype(jnp.bfloat16),
        "mp",
        scatter_dimension=0,
        tiled=True,
    )
    returned = lax.all_to_all(scattered, "expert", split_axis=1, concat_axis=1, tiled=True)
    returned_rows = jnp.transpose(returned)
    picked = returned_rows[slot_index].astype(jnp.float32)
    mixed = jnp.sum(route_gate[:, :, None] * picked, axis=1)
    return mixed.astype(jnp.bfloat16)


def solution(mesh):
    in_specs = (
        P("expert", "mp"),
        P("expert", None),
        P("expert", None),
        P(),
        P(),
        P(),
        P("expert", "mp", None),
        P("expert", "mp", None),
        P("expert", "mp", None),
        P("expert", "mp", None),
        P("expert", "mp", None),
    )
    out_specs = P("expert", "mp")
    return jax.shard_map(
        on_device, mesh=mesh, in_specs=in_specs, out_specs=out_specs, check_vma=False
    )
```

profile of v0, /device:TPU:1, one launch (start us, length us, event | category | flops | bytes accessed | tf_op | source)
XLA Modules:
  0.0 540.4 jit_solution(17868920710652745654)
XLA Ops:
  6.5 0.7 all-gather.2.cloned.1.call-update
  7.3 0.8 copy.42
  8.4 2.3 reduce-window.18
  10.7 0.3 slice_reduce_fusion
  11.9 0.9 select_reduce_fusion.2
  13.1 4.3 scatter_custom_fusion.1
  17.4 4.3 scatter_custom_fusion
  22.0 13.2 %gather_fusion.1 = s32[2048]{0:T(1024)S(1)} fusion(s32[512]{0:T(512)S(1)} %select_reduce_fusion, s32[2048]{0:T(1024)S(1)} %fusion.20), kind=kCustom, calls=%fused_computation.1 | custom fusion | bytes 24576 | tf_op jit(solution)/shard_map/gather | solution.py:68
  35.2 0.6 broadcast_select_fusion.1
  35.8 9.0 %all-to-all-start.1 = ((s32[8,256,1]{1,2,0:T(1,128)}), s32[8,256,1]{1,2,0:T(1,128)S(1)}, u32[]{:S(2)}, u32[]{:S(2)}) async-start(s32[8,256,1]{1,2,0:T(1,128)} %bitcast.10), calls=%async_computation.1 | async-start | bytes 16384 | tf_op jit(solution)/shard_map/all_to_all | solution.py:77
  44.8 18.0 %all-gather.2.cloned.1.call-done = bf16[512,2048]{0,1:T(8,128)(2,1)} async-done(((bf16[512,64]{0,1:T(8,128)(2,1)}), bf16[512,2048]{0,1:T(8,128)(2,1)}) %all-gather.2.cloned.1.call-update) | async-done | bytes 2097168 | tf_op jit(solution)/shard_map/all_gather | solution.py:73
  62.7 2.9 copy.45
  65.7 11.0 %gather_fusion = bf16[2048,2048]{1,0:T(8,128)(2,1)} fusion(bf16[512,2048]{1,0:T(8,128)(2,1)S(1)} %copy.45, s32[2048]{0:T(1024)S(1)} %fusion.20), kind=kCustom, calls=%fused_computation | custom fusion | bytes 16785408 | tf_op jit(solution)/shard_map/gather | solution.py:74
  76.7 7.2 %broadcast_select_fusion = bf16[8,256,2048]{2,1,0:T(8,128)(2,1)} fusion(bf16[8,256,2048]{2,1,0:T(8,128)(2,1)} %bitcast.57, pred[8,256]{1,0:T(8,128)(4,1)S(1)} %broadcast_in_dim.26), kind=kLoop, calls=%fused_computation.6 | loop fusion | flops 4194304 | bytes 16779264 | tf_op jit(solution)/shard_map/jit(_where)/select_n | solution.py:74
  83.9 6.9 %all-to-all-start = ((bf16[8,256,2048]{2,1,0:T(8,128)(2,1)}), bf16[8,256,2048]{2,1,0:T(8,128)(2,1)}, u32[]{:S(2)}, u32[]{:S(2)}) async-start(bf16[8,256,2048]{2,1,0:T(8,128)(2,1)} %broadcast_select_fusion), calls=%async_computation | async-start | bytes 16777216 | tf_op jit(solution)/shard_map/all_to_all | solution.py:76
  90.9 186.9 %all-to-all-done = bf16[8,256,2048]{2,1,0:T(8,128)(2,1)} async-done(((bf16[8,256,2048]{2,1,0:T(8,128)(2,1)}), bf16[8,256,2048]{2,1,0:T(8,128)(2,1)}, u32[]{:S(2)}, u32[]{:S(2)}) %all-to-all-start) | async-done | bytes 8388640 | tf_op jit(solution)/shard_map/all_to_all | solution.py:76
  277.9 6.7 %fusion.5 = bf16[2048,16]{0,1:T(8,128)(2,1)} fusion(bf16[2048,2048,1]{1,0,2:T(8,128)(2,1)} %bitcast.7, bf16[2,16,2048]{2,1,0:T(8,128)(2,1)S(1)} %bitcast.69, f32[2048,2]{0,1:T(2,128)S(1)} %compare_convert_fusion), kind=kOutput, calls=%fused_computation.15 | convolution fusion | flops 268533760 | bytes 8601600 | tf_op jit(solution)/shard_map/dot_general | solution.py:35
  284.8 7.5 %fusion.7 = f32[2048,176]{0,1:T(8,128)} fusion(bf16[2048,2048]{1,0:T(8,128)(2,1)} %bitcast.4, bf16[1,176,2048]{2,1,0:T(8,128)(2,1)S(1)} %copy-done.2), kind=kOutput, calls=%fused_computation.18 | convolution fusion | flops 1476395008 | bytes 10551296 | tf_op jit(solution)/shard_map/dot_general | solution.py:35
  292.3 7.5 %fusion.9 = f32[2048,176]{0,1:T(8,128)} fusion(bf16[2048,2048]{1,0:T(8,128)(2,1)} %bitcast.4, bf16[1,176,2048]{2,1,0:T(8,128)(2,1)S(1)} %copy-done.3), kind=kOutput, calls=%fused_computation.20 | convolution fusion | flops 1476395008 | bytes 10551296 | tf_op jit(solution)/shard_map/dot_general | solution.py:35
  299.8 86.5 %all-reduce.2.cloned.1.call-done = bf16[2048,16]{0,1:T(8,128)(2,1)} async-done(((bf16[2048,16]{0,1:T(8,128)(2,1)}), bf16[2048,16]{0,1:T(8,128)(2,1)}) %all-reduce.2.cloned.1.call-update) | async-done | bytes 65552 | tf_op jit(solution)/shard_map/psum | solution.py:91
  386.3 3.2 broadcast_multiply_fusion
  389.5 9.2 %convert_bitcast_fusion = bf16[2048,2048]{0,1:T(8,128)(2,1)} fusion(f32[2048,176]{0,1:T(8,128)S(1)} %copy-done.6, bf16[2048,1024]{0,1:T(8,128)(2,1)} %bitcast.59, f32[2048,176]{0,1:T(8,128)} %fusion.9, bf16[1,176,2048]{2,1,0:T(8,128)(2,1)S(1)} %copy-done, bf16[1,176,1024]{2,1,0:T(8,128)(2,1)S(1)} %copy-done.4), kind=kOutput, calls=%fused_computation.5 | convolution fusion | flops 2221309952 | bytes 16547840 | tf_op jit(solution)/shard_map/dot_general | solution.py:100
  398.7 12.3 %copy.51 = bf16[2048,2048]{1,0:T(8,128)(2,1)} copy(bf16[2048,2048]{0,1:T(8,128)(2,1)} %convert_bitcast_fusion) | data formatting | bytes 16777216
  411.1 97.4 %reduce-scatter.4.cloned.1.call-done = bf16[64,2048]{1,0:T(8,128)(2,1)} async-done(((bf16[2048,2048]{1,0:T(8,128)(2,1)}), bf16[64,2048]{1,0:T(8,128)(2,1)}) %reduce-scatter.4.cloned.1.call-update) | async-done | bytes 262160
  508.5 1.2 copy.52
  509.8 0.9 copy.48
  510.6 6.7 %all-to-all-start.2 = ((bf16[64,8,256]{2,0,1:T(8,128)(2,1)}), bf16[64,8,256]{2,0,1:T(8,128)(2,1)S(1)}, u32[]{:S(2)}, u32[]{:S(2)}) async-start(bf16[64,8,256]{2,0,1:T(8,128)(2,1)} %copy.48), calls=%async_computation.2 | async-start | bytes 524288 | tf_op jit(solution)/shard_map/all_to_all | solution.py:107
  517.7 9.1 %all-to-all-done.2 = bf16[64,8,256]{2,0,1:T(8,128)(2,1)S(1)} async-done(((bf16[64,8,256]{2,0,1:T(8,128)(2,1)}), bf16[64,8,256]{2,0,1:T(8,128)(2,1)S(1)}, u32[]{:S(2)}, u32[]{:S(2)}) %all-to-all-start.2) | async-done | bytes 262176 | tf_op jit(solution)/shard_map/all_to_all | solution.py:107
  526.8 0.3 copy.49
  527.1 3.2 gather_fusion.2
  530.3 2.8 fusion.12
  533.1 0.7 copy.50
  (47 shorter events, 2.4 us)
Async XLA Ops:
  6.5 383.0 %copy-start = (bf16[1,176,2048]{2,1,0:T(8,128)(2,1)S(1)}, bf16[1,176,2048]{2,1,0:T(8,128)(2,1)}, u32[]{:S(2)}) copy-start(bf16[1,176,2048]{2,1,0:T(8,128)(2,1)} %param.19) | copy-start | bytes 2162692
  6.5 56.2 %all-gather.2.cloned.1.call-start = ((), (), s32[]{:S(2)}) async-start(), calls=%async_computation.4 | async-start | bytes 2162688 | tf_op jit(solution)/shard_map/all_gather | solution.py:73
  35.8 48.2 %all-to-all-start.1 = ((s32[8,256,1]{1,2,0:T(1,128)}), s32[8,256,1]{1,2,0:T(1,128)S(1)}, u32[]{:S(2)}, u32[]{:S(2)}) async-start(s32[8,256,1]{1,2,0:T(1,128)} %bitcast.10), calls=%async_computation.1 | async-start | bytes 16384 | tf_op jit(solution)/shard_map/all_to_all | solution.py:77
  83.9 194.0 %copy-start.5 = (bf16[1,32,2048]{2,1,0:T(8,128)(2,1)S(1)}, bf16[1,32,2048]{2,1,0:T(8,128)(2,1)}, u32[]{:S(2)}) copy-start(bf16[1,32,2048]{2,1,0:T(8,128)(2,1)} %param.20) | copy-start | bytes 393220
  83.9 193.9 %all-to-all-start = ((bf16[8,256,2048]{2,1,0:T(8,128)(2,1)}), bf16[8,256,2048]{2,1,0:T(8,128)(2,1)}, u32[]{:S(2)}, u32[]{:S(2)}) async-start(bf16[8,256,2048]{2,1,0:T(8,128)(2,1)} %broadcast_select_fusion), calls=%async_computation | async-start | bytes 16777216 | tf_op jit(solution)/shard_map/all_to_all | solution.py:76
  90.8 295.5 %all-reduce.2.cloned.1.call-start = ((), (), s32[]{:S(2)}) async-start(), calls=%async_computation.5 | async-start | bytes 131072 | tf_op jit(solution)/shard_map/psum | solution.py:91
  277.9 6.9 %copy-start.2 = (bf16[1,176,2048]{2,1,0:T(8,128)(2,1)S(1)}, bf16[1,176,2048]{2,1,0:T(8,128)(2,1)}, u32[]{:S(2)}) copy-start(bf16[1,176,2048]{2,1,0:T(8,128)(2,1)} %param.18) | copy-start | bytes 2162692
  284.6 223.9 %reduce-scatter.4.cloned.1.call-start = ((), (), s32[]{:S(2)}) async-start(), calls=%async_computation.6 | async-start | bytes 8650752
  284.8 7.5 %copy-start.3 = (bf16[1,176,2048]{2,1,0:T(8,128)(2,1)S(1)}, bf16[1,176,2048]{2,1,0:T(8,128)(2,1)}, u32[]{:S(2)}) copy-start(bf16[1,176,2048]{2,1,0:T(8,128)(2,1)} %param.17) | copy-start | bytes 2162692
  299.8 89.7 %copy-start.4 = (bf16[1,176,1024]{2,1,0:T(8,128)(2,1)S(1)}, bf16[1,176,1024]{2,1,0:T(8,128)(2,1)}, u32[]{:S(2)}) copy-start(bf16[1,176,1024]{2,1,0:T(8,128)(2,1)} %param.21) | copy-start | bytes 1081348
  299.8 89.7 %copy-start.6 = (f32[2048,176]{0,1:T(8,128)S(1)}, f32[2048,176]{0,1:T(8,128)}, u32[]{:S(2)}) copy-start(f32[2048,176]{0,1:T(8,128)} %fusion.7) | copy-start | bytes 4325380
  411.1 106.5 %copy-start.1 = (f32[512,2]{0,1:T(2,128)S(1)}, f32[512,2]{0,1:T(2,128)}, u32[]{:S(2)}) copy-start(f32[512,2]{0,1:T(2,128)} %param.13) | copy-start | bytes 12292
  510.6 16.1 %all-to-all-start.2 = ((bf16[64,8,256]{2,0,1:T(8,128)(2,1)}), bf16[64,8,256]{2,0,1:T(8,128)(2,1)S(1)}, u32[]{:S(2)}, u32[]{:S(2)}) async-start(bf16[64,8,256]{2,0,1:T(8,128)(2,1)} %copy.48), calls=%async_computation.2 | async-start | bytes 524288 | tf_op jit(solution)/shard_map/all_to_all | solution.py:107
Sparse Core Ops, SparseCore 0:
  9.9 52.8 all-gather.1
  284.7 101.5 all-reduce.1
  411.2 97.2 reduce-scatter.3
where the time goes:
time: 543 us; the launch traced here: 540 us
  waiting for transfers between devices  399 us (73%)
  local copies, waits for them, and re-layouts  56.9 us (10%)
  matrix products  30.9 us (6%)
  starting transfers between devices  22.9 us (4%)
  other arithmetic  17.7 us (3%)
  between operations  13.3 us (2%)
    all_to_all x1, waiting for transfers between devices, on_device(): lax.all_to_all(send_rows, 'expert', split_axis=0, concat_axis=0, tiled=True)  187 us
    unnamed x4, waiting for transfers between devices  98.2 us
    psum x1, waiting for transfers between devices, on_device(): rank = lax.psum(rank_part.astype(jnp.bfloat16), 'mp')  86.5 us
    dot_general x3, matrix products, contract_last(): lax.dot_general(left, right, (((1,), (1,)), ((), ())), preferred_element_...  21.7 us
    all_gather x1, waiting for transfers between devices, on_device(): full_rows = lax.all_gather(tokens, 'mp', axis=1, tiled=True)  18 us
    unnamed x18, local copies, waits for them, and re-layouts  14.6 us
    gather x1, local copies, waits for them, and re-layouts, on_device(): slot_adapter = jnp.where(filled, adapter_of[slot_token], -1)  13.2 us
    gather x1, local copies, waits for them, and re-layouts, on_device(): send_rows = jnp.where(filled[:, None], full_rows[slot_token], blank)  11 us
  transfers between devices with their start and end apart: 6, of which 5 were waited for; matrix products, arithmetic and copies ran while one was open for 12% of the time, Pallas kernels for 0%

commit v1 on v0

--- a/solution.py
+++ b/solution.py
@@ -50,11 +50,16 @@
     adapter_in,
     adapter_out,
 ):
-    tok_rows = tokens.shape[0]
+    tok_rows, local_feat = tokens.shape
     groups = lax.axis_size("expert")
+    n_mp = lax.axis_size("mp")
     capacity = 4 * tok_rows // groups
     total_slots = groups * capacity
     source_group = lax.axis_index("expert")
+
+    rank_w = adapter_in[0]
+    rank_cols_w = lax.all_to_all(rank_w, "mp", split_axis=1, concat_axis=0, tiled=True)
+
     adapter_of = token_adapters(
         request_lengths, request_adapter, request_order, source_group * tok_rows, tok_rows
     )
@@ -66,32 +71,25 @@
     slot_token = jnp.zeros((total_slots,), jnp.int32).at[flat_slots].set(flat_tokens)
     filled = jnp.zeros((total_slots,), jnp.bool_).at[flat_slots].set(True)
     slot_adapter = jnp.where(filled, adapter_of[slot_token], -1)
-    gate_w = gate_weight[0]
-    up_w = up_weight[0]
-    rank_w = adapter_in[0]
     blank = jnp.zeros((), tokens.dtype)
-    full_rows = lax.all_gather(tokens, "mp", axis=1, tiled=True)
-    send_rows = jnp.where(filled[:, None], full_rows[slot_token], blank)
-    arrived, arrived_adapter = (
-        lax.all_to_all(send_rows, "expert", split_axis=0, concat_axis=0, tiled=True),
-        lax.all_to_all(slot_adapter, "expert", split_axis=0, concat_axis=0, tiled=True),
+    send_rows = jnp.where(filled[:, None], tokens[slot_token], blank)
+    arrived_local = lax.all_to_all(send_rows, "expert", split_axis=0, concat_axis=0, tiled=True)
+    arrived_adapter = lax.all_to_all(slot_adapter, "expert", split_axis=0, concat_axis=0, tiled=True)
+    row_count = arrived_local.shape[0]
+
+    part_all = contract_last(arrived_local, rank_cols_w)
+    pick = (arrived_adapter[:, None] == jnp.arange(ADAPTERS, dtype=jnp.int32)[None, :]).astype(
+        jnp.float32
     )
-    gate_pre = contract_last(arrived, gate_w)
-    up_base = contract_last(arrived, up_w)
-    rank_cols = contract_last(arrived, rank_w)
-    row_count = arrived.shape[0]
-    per_device = rank_w.shape[0] // RANK
-    local_adapter = arrived_adapter - lax.axis_index("mp") * per_device
-    local_pick = (
-        local_adapter[:, None] == jnp.arange(per_device, dtype=jnp.int32)[None, :]
-    ).astype(jnp.float32)
-    rank_part = jnp.sum(
-        rank_cols.reshape(row_count, per_device, RANK) * local_pick[:, :, None], axis=1
-    )
-    rank = lax.psum(rank_part.astype(jnp.bfloat16), "mp")
-    chosen = (arrived_adapter[:, None] == jnp.arange(ADAPTERS, dtype=jnp.int32)[None, :]).astype(
-        jnp.bfloat16
-    )
+    part_rank = jnp.sum(part_all.reshape(row_count, ADAPTERS, RANK) * pick[:, :, None], axis=1)
+
+    arrived = lax.all_gather(arrived_local, "mp", axis=1, tiled=True)
+    parts = lax.all_gather(part_rank.astype(jnp.bfloat16), "mp", axis=0, tiled=False)
+    rank = jnp.sum(parts.astype(jnp.float32), axis=0).astype(jnp.bfloat16)
+
+    gate_pre = contract_last(arrived, gate_weight[0])
+    up_base = contract_last(arrived, up_weight[0])
+    chosen = pick.astype(jnp.bfloat16)
     expanded = (rank[:, None, :] * chosen[:, :, None]).reshape(row_count, ADAPTERS * RANK)
     up = up_base + contract_last(expanded, adapter_out[0])
     hidden = (jax.nn.silu(gate_pre) * up).astype(jnp.bfloat16)

time: 543 us -> 354 us (0.65)
  waiting for transfers between devices: 399 us -> 220 us
  matrix products: 30.9 us -> 20.8 us
  starting transfers between devices: 22.9 us -> 31 us
  other arithmetic: 17.7 us -> 11.1 us
    all_to_all x1, waiting for transfers between devices: 187 us -> 10.7 us  [on_device(): lax.all_to_all(send_rows, 'expert', split_axis=0, concat_axis=0, tiled=True)]
    psum x1 -> x0, waiting for transfers between devices: 86.5 us -> none  [on_device(): rank = lax.psum(rank_part.astype(jnp.bfloat16), 'mp')]
    all_gather x1 -> x2, waiting for transfers between devices: 18 us -> 95.7 us  [the longest x1 54 us: on_device(): arrived = lax.all_gather(arrived_local, 'mp', axis=1, tiled=True)]
    dot_general x3, matrix products: 21.7 us -> 11.1 us  [contract_last(): lax.dot_general(left, right, (((1,), (1,)), ((), ())), preferred_element_...]
    all_to_all x0 -> x1, starting transfers between devices: none -> 8.04 us  [on_device(): lax.all_to_all(rank_w, 'mp', split_axis=1, concat_axis=0, tiled=True)]
    all_to_all x0 -> x1, waiting for transfers between devices: none -> 6.96 us  [on_device(): lax.all_to_all(rank_w, 'mp', split_axis=1, concat_axis=0, tiled=True)]
    select_n x1, other arithmetic: 7.24 us -> 0.72 us  [on_device(): send_rows = jnp.where(filled[:, None], tokens[slot_token], blank)]
    gather x1 -> x2, local copies, waits for them, and re-layouts: 11 us -> 6.39 us  [on_device(): send_rows = jnp.where(filled[:, None], tokens[slot_token], blank)]
  transfers between devices with their start and end apart: 6 -> 7, of which waited for: 5 -> 6; matrix products, arithmetic and copies ran while one was open for 12% -> 4% of each run, Pallas kernels for 0% -> 0%
where the time goes in v1:
time: 354 us; the launch traced here: 352 us
  waiting for transfers between devices  220 us (62%)
  local copies, waits for them, and re-layouts  54.8 us (15%)
  starting transfers between devices  31 us (9%)
  matrix products  20.8 us (6%)
  between operations  13.4 us (4%)
  other arithmetic  11.1 us (3%)
    unnamed x4, waiting for transfers between devices  98 us
    all_gather x1, waiting for transfers between devices, on_device(): arrived = lax.all_gather(arrived_local, 'mp', axis=1, tiled=True)  54 us
    all_gather x1, waiting for transfers between devices, on_device(): lax.all_gather(part_rank.astype(jnp.bfloat16), 'mp', axis=0, tiled=False)  41.7 us
    unnamed x24, local copies, waits for them, and re-layouts  18.6 us
    gather x1, local copies, waits for them, and re-layouts, on_device(): slot_adapter = jnp.where(filled, adapter_of[slot_token], -1)  13.2 us
    dot_general x3, matrix products, contract_last(): lax.dot_general(left, right, (((1,), (1,)), ((), ())), preferred_element_...  11.1 us
    all_to_all x1, waiting for transfers between devices, on_device(): lax.all_to_all(send_rows, 'expert', split_axis=0, concat_axis=0, tiled=True)  10.7 us
    dot_general x1, matrix products, on_device(): lax.dot_general(down_w, hidden, (((0,), (1,)), ((), ())), preferred_eleme...  9.66 us
  transfers between devices with their start and end apart: 7, of which 6 were waited for; matrix products, arithmetic and copies ran while one was open for 4% of the time, Pallas kernels for 0%

profile of v1, /device:TPU:1, one launch (start us, length us, event | category | flops | bytes accessed | tf_op | source)
XLA Modules:
  0.0 351.5 jit_solution(11466283499831162084)
XLA Ops:
  6.5 0.9 copy.63
  7.8 2.3 reduce-window.18
  11.3 4.3 %scatter_custom_fusion.1 = s32[2048]{0:T(1024)S(1)} fusion(s32[1024]{0:T(1024)S(1)} %bitcast.81, s32[1024]{0:T(1024)S(1)} %reshape.215, s32[]{:T(128)} %constant.14.clone.1), kind=kCustom, calls=%fused_computation.50 | custom fusion | bytes 8196 | tf_op jit(solution)/shard_map/scatter | solution.py:71
  15.6 0.9 select_reduce_fusion.2
  17.0 13.2 %gather_fusion.1 = s32[2048]{0:T(1024)S(1)} fusion(s32[512]{0:T(512)S(1)} %select_reduce_fusion, s32[2048]{0:T(1024)S(1)} %fusion.21), kind=kCustom, calls=%fused_computation.1 | custom fusion | bytes 24576 | tf_op jit(solution)/shard_map/gather | solution.py:73
  30.2 4.3 %scatter_custom_fusion = pred[2048]{0:T(1024)(128)(4,1)S(1)} fusion(s32[1024]{0:T(1024)S(1)} %bitcast.82, pred[1024]{0:T(1024)(128)(4,1)S(1)} %broadcast.114, pred[]{:T(512)} %constant.12.clone.1), kind=kCustom, calls=%fused_computation.52 | custom fusion | bytes 2049 | tf_op jit(solution)/shard_map/scatter | solution.py:72
  35.1 9.0 %all-to-all-start.2 = ((s32[8,256,1]{1,2,0:T(1,128)}), s32[8,256,1]{1,2,0:T(1,128)S(1)}, u32[]{:S(2)}, u32[]{:S(2)}) async-start(s32[8,256,1]{1,2,0:T(1,128)} %bitcast.9), calls=%async_computation.2 | async-start | bytes 16384 | tf_op jit(solution)/shard_map/all_to_all | solution.py:77
  44.3 6.2 %gather_fusion = bf16[2048,64]{1,0:T(8,128)(2,1)S(1)} fusion(bf16[512,64]{1,0:T(8,128)(2,1)S(1)} %copy.66, s32[2048]{0:T(1024)S(1)} %fusion.21), kind=kCustom, calls=%fused_computation | custom fusion | bytes 532480 | tf_op jit(solution)/shard_map/gather | solution.py:75
  51.1 0.9 reshape.235
  51.9 8.0 %all-to-all-start.1 = ((bf16[32,2,1024]{2,1,0:T(2,128)(2,1)}), bf16[32,2,1024]{2,1,0:T(2,128)(2,1)S(1)}, u32[]{:S(2)}, u32[]{:S(2)}) async-start(bf16[32,2,1024]{2,1,0:T(2,128)(2,1)} %reshape.235), calls=%async_computation.1 | async-start | bytes 262144 | tf_op jit(solution)/shard_map/all_to_all | solution.py:61
  60.0 0.7 broadcast_select_fusion
  60.7 7.0 %all-to-all-done.1 = bf16[32,2,1024]{2,1,0:T(2,128)(2,1)S(1)} async-done(((bf16[32,2,1024]{2,1,0:T(2,128)(2,1)}), bf16[32,2,1024]{2,1,0:T(2,128)(2,1)S(1)}, u32[]{:S(2)}, u32[]{:S(2)}) %all-to-all-start.1) | async-done | bytes 131104 | tf_op jit(solution)/shard_map/all_to_all | solution.py:61
  67.6 6.9 %all-to-all-start = ((bf16[8,256,64]{1,2,0:T(8,128)(2,1)}), bf16[8,256,64]{1,2,0:T(8,128)(2,1)S(1)}, u32[]{:S(2)}, u32[]{:S(2)}) async-start(bf16[8,256,64]{1,2,0:T(8,128)(2,1)} %broadcast_select_fusion), calls=%async_computation | async-start | bytes 524288 | tf_op jit(solution)/shard_map/all_to_all | solution.py:76
  74.9 10.7 %all-to-all-done = bf16[8,256,64]{1,2,0:T(8,128)(2,1)S(1)} async-done(((bf16[8,256,64]{1,2,0:T(8,128)(2,1)}), bf16[8,256,64]{1,2,0:T(8,128)(2,1)S(1)}, u32[]{:S(2)}, u32[]{:S(2)}) %all-to-all-start) | async-done | bytes 262176 | tf_op jit(solution)/shard_map/all_to_all | solution.py:76
  85.9 1.9 multiply_reduce_fusion
  87.9 0.7 copy.78
  88.9 41.7 %all-gather.6.cloned.1.call-done = bf16[65536,16]{0,1:T(8,128)(2,1)} async-done(((bf16[2048,16]{0,1:T(8,128)(2,1)}), bf16[65536,16]{0,1:T(8,128)(2,1)}) %all-gather.6.cloned.1.call-update) | async-done | bytes 2097168 | tf_op jit(solution)/shard_map/all_gather | solution.py:87
  130.6 2.7 copy.80
  134.0 2.3 broadcast_multiply_fusion
  136.4 54.0 %all-gather.4.cloned.1.call-done = bf16[2048,2048]{0,1:T(8,128)(2,1)} async-done(((bf16[2048,64]{0,1:T(8,128)(2,1)}), bf16[2048,2048]{0,1:T(8,128)(2,1)}) %all-gather.4.cloned.1.call-update) | async-done | bytes 8388624 | tf_op jit(solution)/shard_map/all_gather | solution.py:86
  190.4 6.4 %fusion.6 = f32[2048,176]{0,1:T(8,128)} fusion(bf16[2048,2048]{0,1:T(8,128)(2,1)} %all-gather.4.cloned.1.call-done, bf16[1,176,2048]{2,1,0:T(8,128)(2,1)S(1)} %copy-done.5), kind=kOutput, calls=%fused_computation.17 | convolution fusion | flops 1476395008 | bytes 10551296 | tf_op jit(solution)/shard_map/dot_general | solution.py:35
  196.7 2.9 fusion.8
  199.6 9.7 %convert_bitcast_fusion = bf16[2048,2048]{0,1:T(8,128)(2,1)} fusion(f32[2048,176]{0,1:T(8,128)} %fusion.6, bf16[2048,1024]{0,1:T(8,128)(2,1)} %bitcast.69, f32[2048,176]{0,1:T(8,128)} %fusion.8, bf16[1,176,2048]{2,1,0:T(8,128)(2,1)S(1)} %copy-done, bf16[1,176,1024]{2,1,0:T(8,128)(2,1)S(1)} %copy-done.7), kind=kOutput, calls=%fused_computation.5 | convolution fusion | flops 2221309952 | bytes 16547840 | tf_op jit(solution)/shard_map/dot_general | solution.py:98
  209.3 12.3 %copy.76 = bf16[2048,2048]{1,0:T(8,128)(2,1)} copy(bf16[2048,2048]{0,1:T(8,128)(2,1)} %convert_bitcast_fusion) | data formatting | bytes 16777216
  221.7 98.0 %reduce-scatter.4.cloned.1.call-done = bf16[64,2048]{1,0:T(8,128)(2,1)} async-done(((bf16[2048,2048]{1,0:T(8,128)(2,1)}), bf16[64,2048]{1,0:T(8,128)(2,1)}) %reduce-scatter.4.cloned.1.call-update) | async-done | bytes 262160
  319.6 1.2 copy.77
  320.9 0.9 copy.73
  321.8 6.8 %all-to-all-start.3 = ((bf16[64,8,256]{2,0,1:T(8,128)(2,1)}), bf16[64,8,256]{2,0,1:T(8,128)(2,1)S(1)}, u32[]{:S(2)}, u32[]{:S(2)}) async-start(bf16[64,8,256]{2,0,1:T(8,128)(2,1)} %copy.73), calls=%async_computation.3 | async-start | bytes 524288 | tf_op jit(solution)/shard_map/all_to_all | solution.py:105
  328.9 9.1 %all-to-all-done.3 = bf16[64,8,256]{2,0,1:T(8,128)(2,1)S(1)} async-done(((bf16[64,8,256]{2,0,1:T(8,128)(2,1)}), bf16[64,8,256]{2,0,1:T(8,128)(2,1)S(1)}, u32[]{:S(2)}, u32[]{:S(2)}) %all-to-all-start.3) | async-done | bytes 262176 | tf_op jit(solution)/shard_map/all_to_all | solution.py:105
  338.2 3.2 gather_fusion.2
  341.4 2.8 fusion.11
  344.3 0.7 copy.75
  (59 shorter events, 5.5 us)
Async XLA Ops:
  6.5 193.1 %copy-start = (bf16[1,176,2048]{2,1,0:T(8,128)(2,1)S(1)}, bf16[1,176,2048]{2,1,0:T(8,128)(2,1)}, u32[]{:S(2)}) copy-start(bf16[1,176,2048]{2,1,0:T(8,128)(2,1)} %param.19) | copy-start | bytes 2162692
  16.9 27.2 %copy-start.2 = (bf16[512,64]{0,1:T(8,128)(2,1)S(1)}, bf16[512,64]{0,1:T(8,128)(2,1)}, u32[]{:S(2)}) copy-start(bf16[512,64]{0,1:T(8,128)(2,1)} %param.11) | copy-start | bytes 196612
  30.2 20.5 %copy-start.1 = (bf16[1,32,2048]{2,1,0:T(8,128)(2,1)S(1)}, bf16[1,32,2048]{2,1,0:T(8,128)(2,1)}, u32[]{:S(2)}) copy-start(bf16[1,32,2048]{2,1,0:T(8,128)(2,1)} %param.20) | copy-start | bytes 393220
  35.1 16.8 %all-to-all-start.2 = ((s32[8,256,1]{1,2,0:T(1,128)}), s32[8,256,1]{1,2,0:T(1,128)S(1)}, u32[]{:S(2)}, u32[]{:S(2)}) async-start(s32[8,256,1]{1,2,0:T(1,128)} %bitcast.9), calls=%async_computation.2 | async-start | bytes 16384 | tf_op jit(solution)/shard_map/all_to_all | solution.py:77
  51.9 15.7 %all-to-all-start.1 = ((bf16[32,2,1024]{2,1,0:T(2,128)(2,1)}), bf16[32,2,1024]{2,1,0:T(2,128)(2,1)S(1)}, u32[]{:S(2)}, u32[]{:S(2)}) async-start(bf16[32,2,1024]{2,1,0:T(2,128)(2,1)} %reshape.235), calls=%async_computation.1 | async-start | bytes 262144 | tf_op jit(solution)/shard_map/all_to_all | solution.py:61
  67.6 18.0 %all-to-all-start = ((bf16[8,256,64]{1,2,0:T(8,128)(2,1)}), bf16[8,256,64]{1,2,0:T(8,128)(2,1)S(1)}, u32[]{:S(2)}, u32[]{:S(2)}) async-start(bf16[8,256,64]{1,2,0:T(8,128)(2,1)} %broadcast_select_fusion), calls=%async_computation | async-start | bytes 524288 | tf_op jit(solution)/shard_map/all_to_all | solution.py:76
  74.6 56.0 %all-gather.6.cloned.1.call-start = ((), (), s32[]{:S(2)}) async-start(), calls=%async_computation.6 | async-start | bytes 2162688 | tf_op jit(solution)/shard_map/all_gather | solution.py:87
  87.8 102.5 %all-gather.4.cloned.1.call-start = ((), (), s32[]{:S(2)}) async-start(), calls=%async_computation.5 | async-start | bytes 8650752 | tf_op jit(solution)/shard_map/all_gather | solution.py:86
  88.6 231.0 %reduce-scatter.4.cloned.1.call-start = ((), (), s32[]{:S(2)}) async-start(), calls=%async_computation.7 | async-start | bytes 8650752
  133.3 57.0 %copy-start.5 = (bf16[1,176,2048]{2,1,0:T(8,128)(2,1)S(1)}, bf16[1,176,2048]{2,1,0:T(8,128)(2,1)}, u32[]{:S(2)}) copy-start(bf16[1,176,2048]{2,1,0:T(8,128)(2,1)} %param.18) | copy-start | bytes 2162692
  136.4 60.4 %copy-start.6 = (bf16[1,176,2048]{2,1,0:T(8,128)(2,1)S(1)}, bf16[1,176,2048]{2,1,0:T(8,128)(2,1)}, u32[]{:S(2)}) copy-start(bf16[1,176,2048]{2,1,0:T(8,128)(2,1)} %param.17) | copy-start | bytes 2162692
  190.4 6.4 %copy-start.4 = (bf16[2048,2048]{0,1:T(8,128)(2,1)S(1)}, bf16[2048,2048]{0,1:T(8,128)(2,1)}, u32[]{:S(2)}) copy-start(bf16[2048,2048]{0,1:T(8,128)(2,1)} %all-gather.4.cloned.1.call-done) | copy-start | bytes 25165828
  196.7 2.9 copy-start.7
  221.6 107.1 %copy-start.3 = (f32[512,2]{0,1:T(2,128)S(1)}, f32[512,2]{0,1:T(2,128)}, u32[]{:S(2)}) copy-start(f32[512,2]{0,1:T(2,128)} %param.13) | copy-start | bytes 12292
  321.8 16.1 %all-to-all-start.3 = ((bf16[64,8,256]{2,0,1:T(8,128)(2,1)}), bf16[64,8,256]{2,0,1:T(8,128)(2,1)S(1)}, u32[]{:S(2)}, u32[]{:S(2)}) async-start(bf16[64,8,256]{2,0,1:T(8,128)(2,1)} %copy.73), calls=%async_computation.3 | async-start | bytes 524288 | tf_op jit(solution)/shard_map/all_to_all | solution.py:105
Sparse Core Ops, SparseCore 0:
  87.9 42.5 all-gather.5
  133.1 57.1 all-gather.3
  221.8 97.8 reduce-scatter.3

commit v2 on v1

--- a/solution.py
+++ b/solution.py
@@ -64,17 +64,27 @@
         request_lengths, request_adapter, request_order, source_group * tok_rows, tok_rows
     )
     slot_index = expert_slots(expert_route, groups, capacity)
-    flat_slots = slot_index.reshape(-1)
-    flat_tokens = jnp.broadcast_to(
-        jnp.arange(tok_rows, dtype=jnp.int32)[:, None], slot_index.shape
-    ).reshape(-1)
-    slot_token = jnp.zeros((total_slots,), jnp.int32).at[flat_slots].set(flat_tokens)
-    filled = jnp.zeros((total_slots,), jnp.bool_).at[flat_slots].set(True)
-    slot_adapter = jnp.where(filled, adapter_of[slot_token], -1)
-    blank = jnp.zeros((), tokens.dtype)
-    send_rows = jnp.where(filled[:, None], tokens[slot_token], blank)
-    arrived_local = lax.all_to_all(send_rows, "expert", split_axis=0, concat_axis=0, tiled=True)
-    arrived_adapter = lax.all_to_all(slot_adapter, "expert", split_axis=0, concat_axis=0, tiled=True)
+    slot_ids = jnp.arange(total_slots, dtype=jnp.int32)[:, None]
+    seat = (
+        (slot_index[None, :, 0] == slot_ids) | (slot_index[None, :, 1] == slot_ids)
+    ).astype(tokens.dtype)
+    send_rows = jnp.dot(seat, tokens, preferred_element_type=jnp.float32).astype(tokens.dtype)
+    id_plus = jnp.dot(
+        seat, (adapter_of + 1).astype(tokens.dtype), preferred_element_type=jnp.float32
+    ) - 1.0
+    payload = jnp.concatenate(
+        [
+            send_rows.reshape(groups, capacity, local_feat),
+            id_plus.astype(tokens.dtype).reshape(groups, capacity // local_feat, local_feat),
+        ],
+        axis=1,
+    )
+    chunk = payload.shape[1]
+    received = lax.all_to_all(
+        payload.reshape(groups * chunk, local_feat), "expert", split_axis=0, concat_axis=0, tiled=True
+    ).reshape(groups, chunk, local_feat)
+    arrived_local = received[:, :capacity].reshape(total_slots, local_feat)
+    arrived_adapter = received[:, capacity:].reshape(total_slots).astype(jnp.int32)
     row_count = arrived_local.shape[0]
 
     part_all = contract_last(arrived_local, rank_cols_w)
@@ -82,10 +92,19 @@
         jnp.float32
     )
     part_rank = jnp.sum(part_all.reshape(row_count, ADAPTERS, RANK) * pick[:, :, None], axis=1)
-
-    arrived = lax.all_gather(arrived_local, "mp", axis=1, tiled=True)
-    parts = lax.all_gather(part_rank.astype(jnp.bfloat16), "mp", axis=0, tiled=False)
-    rank = jnp.sum(parts.astype(jnp.float32), axis=0).astype(jnp.bfloat16)
+    part_rows = row_count * RANK // local_feat
+    payload2 = jnp.concatenate(
+        [arrived_local, part_rank.astype(tokens.dtype).reshape(part_rows, local_feat)], axis=0
+    )
+    gathered = lax.all_gather(payload2, "mp", axis=1, tiled=True)
+    arrived = gathered[:row_count]
+    rank = (
+        jnp.sum(
+            gathered[row_count:].reshape(part_rows, n_mp, local_feat).astype(jnp.float32), axis=1
+        )
+        .reshape(row_count, RANK)
+        .astype(jnp.bfloat16)
+    )
 
     gate_pre = contract_last(arrived, gate_weight[0])
     up_base = contract_last(arrived, up_weight[0])

time: 354 us -> 285 us (0.81)
  waiting for transfers between devices: 220 us -> 181 us
  local copies, waits for them, and re-layouts: 54.8 us -> 27.1 us
  starting transfers between devices: 31 us -> 23.8 us
  matrix products: 20.8 us -> 25.4 us
    all_gather x2 -> x1, waiting for transfers between devices: 95.7 us -> 59.1 us  [on_device(): gathered = lax.all_gather(payload2, 'mp', axis=1, tiled=True)]
    gather x3 -> x0, local copies, waits for them, and re-layouts: 19.6 us -> none  [the longest x1 13.2 us: on_device(): slot_adapter = jnp.where(filled, adapter_of[slot_token], -1)]
    scatter x2 -> x0, local copies, waits for them, and re-layouts: 8.66 us -> none  [the longest x1 4.34 us: on_device(): filled = jnp.zeros((total_slots,), jnp.bool_).at[flat_slots].set(True)]
    all_to_all x2 -> x1, starting transfers between devices: 15.9 us -> 8.18 us  [on_device(): lax.all_to_all(payload.reshape(groups * chunk, local_feat), 'expert', spl...]
    all_to_all x1, waiting for transfers between devices: 6.96 us -> 0.01 us  [on_device(): lax.all_to_all(rank_w, 'mp', split_axis=1, concat_axis=0, tiled=True)]
    all_to_all x2 -> x1, waiting for transfers between devices: 10.7 us -> 14.9 us  [on_device(): lax.all_to_all(payload.reshape(groups * chunk, local_feat), 'expert', spl...]
    unnamed x24 -> x20, local copies, waits for them, and re-layouts: 18.6 us -> 15.8 us
    unnamed x4 -> x3, waiting for transfers between devices: 98 us -> 98 us
  transfers between devices with their start and end apart: 7 -> 5, of which waited for: 6 -> 4; matrix products, arithmetic and copies ran while one was open for 4% -> 4% of each run, Pallas kernels for 0% -> 0%
where the time goes in v2:
time: 285 us; the launch traced here: 282 us
  waiting for transfers between devices  181 us (64%)
  local copies, waits for them, and re-layouts  27.1 us (10%)
  matrix products  25.4 us (9%)
  starting transfers between devices  23.8 us (8%)
  between operations  13.7 us (5%)
  other arithmetic  11.7 us (4%)
    unnamed x3, waiting for transfers between devices  98 us
    all_gather x1, waiting for transfers between devices, on_device(): gathered = lax.all_gather(payload2, 'mp', axis=1, tiled=True)  59.1 us
    unnamed x20, local copies, waits for them, and re-layouts  15.8 us
    all_to_all x1, waiting for transfers between devices, on_device(): lax.all_to_all(payload.reshape(groups * chunk, local_feat), 'expert', spl...  14.9 us
    dot_general x3, matrix products, contract_last(): lax.dot_general(left, right, (((1,), (1,)), ((), ())), preferred_element_...  13.7 us
    dot_general x1, matrix products, on_device(): lax.dot_general(down_w, hidden, (((0,), (1,)), ((), ())), preferred_eleme...  9.67 us
    all_to_all x1, waiting for transfers between devices, on_device(): lax.all_to_all(scattered, 'expert', split_axis=1, concat_axis=1, tiled=True)  8.89 us
    all_to_all x1, starting transfers between devices, on_device(): lax.all_to_all(rank_w, 'mp', split_axis=1, concat_axis=0, tiled=True)  8.58 us
  transfers between devices with their start and end apart: 5, of which 4 were waited for; matrix products, arithmetic and copies ran while one was open for 4% of the time, Pallas kernels for 0%

profile of v2, /device:TPU:1, one launch (start us, length us, event | category | flops | bytes accessed | tf_op | source)
XLA Modules:
  0.0 282.5 jit_solution(9148846674152353136)
XLA Ops:
  6.5 1.2 all_to_all.25
  7.9 0.8 reshape.180
  8.7 8.6 %all-to-all-start.1 = ((bf16[32,2,1024]{2,1,0:T(2,128)(2,1)}), bf16[32,2,1024]{2,1,0:T(2,128)(2,1)S(1)}, u32[]{:S(2)}, u32[]{:S(2)}) async-start(bf16[32,2,1024]{2,1,0:T(2,128)(2,1)} %reshape.180), calls=%async_computation.1 | async-start | bytes 262144 | tf_op jit(solution)/shard_map/all_to_all | solution.py:61
  17.3 0.8 copy.77
  18.5 0.9 select_reduce_fusion.2
  19.9 2.3 reduce-window.18
  23.0 0.7 compare_select_fusion
  23.7 0.9 fusion.5
  24.7 1.1 fusion.11
  26.0 0.8 pad_maximum_fusion
  26.8 8.2 %all-to-all-start = ((bf16[8,260,64]{1,2,0:T(8,128)(2,1)}), bf16[8,260,64]{1,2,0:T(8,128)(2,1)S(1)}, u32[]{:S(2)}, u32[]{:S(2)}) async-start(bf16[8,260,64]{1,2,0:T(8,128)(2,1)} %pad_maximum_fusion), calls=%async_computation | async-start | bytes 786432 | tf_op jit(solution)/shard_map/all_to_all | solution.py:83
  35.3 14.9 %all-to-all-done = bf16[8,260,64]{1,2,0:T(8,128)(2,1)S(1)} async-done(((bf16[8,260,64]{1,2,0:T(8,128)(2,1)}), bf16[8,260,64]{1,2,0:T(8,128)(2,1)S(1)}, u32[]{:S(2)}, u32[]{:S(2)}) %all-to-all-start) | async-done | bytes 266272 | tf_op jit(solution)/shard_map/all_to_all | solution.py:83
  50.9 1.3 multiply_reduce_fusion
  52.4 0.3 convert_element_type.97
  52.8 0.8 pad_maximum_fusion.1
  53.8 59.1 %all-gather.2.cloned.1.call-done = bf16[2560,2048]{0,1:T(8,128)(2,1)} async-done(((bf16[2560,64]{0,1:T(8,128)(2,1)}), bf16[2560,2048]{0,1:T(8,128)(2,1)}) %all-gather.2.cloned.1.call-update) | async-done | bytes 10485776 | tf_op jit(solution)/shard_map/all_gather | solution.py:99
  112.9 1.6 slice-done
  114.5 0.3 reduce
  115.4 2.4 broadcast_multiply_fusion
  117.8 6.2 %fusion = f32[2048,176]{0,1:T(8,128)} fusion(bf16[2560,2048]{0,1:T(8,128)(2,1)} %all-gather.2.cloned.1.call-done, bf16[1,176,2048]{2,1,0:T(8,128)(2,1)S(1)} %copy-done.2), kind=kOutput, calls=%fused_computation.3 | convolution fusion | flops 1476395008 | bytes 10551296 | tf_op jit(solution)/shard_map/dot_general | solution.py:35
  124.0 6.2 %fusion.2 = f32[2048,176]{0,1:T(8,128)} fusion(bf16[2560,2048]{0,1:T(8,128)(2,1)} %all-gather.2.cloned.1.call-done, bf16[1,176,2048]{2,1,0:T(8,128)(2,1)S(1)} %copy-done.3), kind=kOutput, calls=%fused_computation.5 | convolution fusion | flops 1476395008 | bytes 10551296 | tf_op jit(solution)/shard_map/dot_general | solution.py:35
  130.3 9.7 %convert_bitcast_fusion = bf16[2048,2048]{0,1:T(8,128)(2,1)} fusion(f32[2048,176]{0,1:T(8,128)} %fusion.2, bf16[2048,1024]{0,1:T(8,128)(2,1)} %bitcast.69, f32[2048,176]{0,1:T(8,128)} %fusion, bf16[1,176,2048]{2,1,0:T(8,128)(2,1)S(1)} %copy-done, bf16[1,176,1024]{2,1,0:T(8,128)(2,1)S(1)} %copy-done.4), kind=kOutput, calls=%fused_computation.1 | convolution fusion | flops 2221309952 | bytes 16547840 | tf_op jit(solution)/shard_map/dot_general | solution.py:117
  139.9 12.3 %copy.96 = bf16[2048,2048]{1,0:T(8,128)(2,1)} copy(bf16[2048,2048]{0,1:T(8,128)(2,1)} %convert_bitcast_fusion) | data formatting | bytes 16777216
  152.3 98.0 %reduce-scatter.4.cloned.1.call-done = bf16[64,2048]{1,0:T(8,128)(2,1)} async-done(((bf16[2048,2048]{1,0:T(8,128)(2,1)}), bf16[64,2048]{1,0:T(8,128)(2,1)}) %reduce-scatter.4.cloned.1.call-update) | async-done | bytes 262160
  250.3 1.2 copy.97
  251.5 0.9 copy.92
  252.4 6.8 %all-to-all-start.2 = ((bf16[64,8,256]{2,0,1:T(8,128)(2,1)}), bf16[64,8,256]{2,0,1:T(8,128)(2,1)S(1)}, u32[]{:S(2)}, u32[]{:S(2)}) async-start(bf16[64,8,256]{2,0,1:T(8,128)(2,1)} %copy.92), calls=%async_computation.2 | async-start | bytes 524288 | tf_op jit(solution)/shard_map/all_to_all | solution.py:124
  259.6 8.9 %all-to-all-done.2 = bf16[64,8,256]{2,0,1:T(8,128)(2,1)S(1)} async-done(((bf16[64,8,256]{2,0,1:T(8,128)(2,1)}), bf16[64,8,256]{2,0,1:T(8,128)(2,1)S(1)}, u32[]{:S(2)}, u32[]{:S(2)}) %all-to-all-start.2) | async-done | bytes 262176 | tf_op jit(solution)/shard_map/all_to_all | solution.py:124
  268.5 0.3 copy.93
  268.8 3.2 %gather_fusion = bf16[1024,64]{1,0:T(8,128)(2,1)S(1)} fusion(bf16[2048,64]{1,0:T(8,128)(2,1)S(1)} %bitcast.67, s32[1024]{0:T(1024)S(1)} %broadcast_clamp_fusion), kind=kCustom, calls=%fused_computation | custom fusion | bytes 266240 | tf_op jit(solution)/shard_map/gather | solution.py:126
  272.0 2.8 %fusion.25 = bf16[512,64]{1,0:T(8,128)(2,1)S(1)} fusion(bf16[512,2,64]{2,1,0:T(2,128)(2,1)S(1)} %bitcast.71, f32[512,2]{1,0:T(8,128)S(1)} %copy.76), kind=kLoop, calls=%fused_computation.29 | loop fusion | flops 163840 | bytes 200704 | tf_op jit(solution)/shard_map/reduce_sum | solution.py:127
  274.9 0.7 copy.95
  (61 shorter events, 4.6 us)
Async XLA Ops:
  6.5 123.7 %copy-start = (bf16[1,176,2048]{2,1,0:T(8,128)(2,1)S(1)}, bf16[1,176,2048]{2,1,0:T(8,128)(2,1)}, u32[]{:S(2)}) copy-start(bf16[1,176,2048]{2,1,0:T(8,128)(2,1)} %param.19) | copy-start | bytes 2162692
  6.5 18.1 %copy-start.5 = (bf16[512,64]{0,1:T(8,128)(2,1)S(1)}, bf16[512,64]{0,1:T(8,128)(2,1)}, u32[]{:S(2)}) copy-start(bf16[512,64]{0,1:T(8,128)(2,1)} %param.11) | copy-start | bytes 196612
  8.7 18.1 %all-to-all-start.1 = ((bf16[32,2,1024]{2,1,0:T(2,128)(2,1)}), bf16[32,2,1024]{2,1,0:T(2,128)(2,1)S(1)}, u32[]{:S(2)}, u32[]{:S(2)}) async-start(bf16[32,2,1024]{2,1,0:T(2,128)(2,1)} %reshape.180), calls=%async_computation.1 | async-start | bytes 262144 | tf_op jit(solution)/shard_map/all_to_all | solution.py:61
  26.8 23.3 %all-to-all-start = ((bf16[8,260,64]{1,2,0:T(8,128)(2,1)}), bf16[8,260,64]{1,2,0:T(8,128)(2,1)S(1)}, u32[]{:S(2)}, u32[]{:S(2)}) async-start(bf16[8,260,64]{1,2,0:T(8,128)(2,1)} %pad_maximum_fusion), calls=%async_computation | async-start | bytes 786432 | tf_op jit(solution)/shard_map/all_to_all | solution.py:83
  35.0 77.9 %all-gather.2.cloned.1.call-start = ((), (), s32[]{:S(2)}) async-start(), calls=%async_computation.4 | async-start | bytes 10813440 | tf_op jit(solution)/shard_map/all_gather | solution.py:99
  53.6 196.7 %reduce-scatter.4.cloned.1.call-start = ((), (), s32[]{:S(2)}) async-start(), calls=%async_computation.5 | async-start | bytes 8650752
  112.9 1.6 slice-start
  114.8 3.0 %copy-start.2 = (bf16[1,176,2048]{2,1,0:T(8,128)(2,1)S(1)}, bf16[1,176,2048]{2,1,0:T(8,128)(2,1)}, u32[]{:S(2)}) copy-start(bf16[1,176,2048]{2,1,0:T(8,128)(2,1)} %param.17) | copy-start | bytes 2162692
  117.8 6.2 %copy-start.3 = (bf16[1,176,2048]{2,1,0:T(8,128)(2,1)S(1)}, bf16[1,176,2048]{2,1,0:T(8,128)(2,1)}, u32[]{:S(2)}) copy-start(bf16[1,176,2048]{2,1,0:T(8,128)(2,1)} %param.18) | copy-start | bytes 2162692
  124.0 6.2 %copy-start.4 = (bf16[1,176,1024]{2,1,0:T(8,128)(2,1)S(1)}, bf16[1,176,1024]{2,1,0:T(8,128)(2,1)}, u32[]{:S(2)}) copy-start(bf16[1,176,1024]{2,1,0:T(8,128)(2,1)} %param.21) | copy-start | bytes 1081348
  152.3 107.2 %copy-start.1 = (f32[512,2]{0,1:T(2,128)S(1)}, f32[512,2]{0,1:T(2,128)}, u32[]{:S(2)}) copy-start(f32[512,2]{0,1:T(2,128)} %param.13) | copy-start | bytes 12292
  252.4 16.1 %all-to-all-start.2 = ((bf16[64,8,256]{2,0,1:T(8,128)(2,1)}), bf16[64,8,256]{2,0,1:T(8,128)(2,1)S(1)}, u32[]{:S(2)}, u32[]{:S(2)}) async-start(bf16[64,8,256]{2,0,1:T(8,128)(2,1)} %copy.92), calls=%async_computation.2 | async-start | bytes 524288 | tf_op jit(solution)/shard_map/all_to_all | solution.py:124
Sparse Core Ops, SparseCore 0:
  53.7 59.1 all-gather.1
  152.4 97.8 reduce-scatter.3

commit v3 on v2

--- a/solution.py
+++ b/solution.py
@@ -59,6 +59,7 @@
 
     rank_w = adapter_in[0]
     rank_cols_w = lax.all_to_all(rank_w, "mp", split_axis=1, concat_axis=0, tiled=True)
+    down_cols_w = lax.all_to_all(down_weight[0], "mp", split_axis=1, concat_axis=0, tiled=True)
 
     adapter_of = token_adapters(
         request_lengths, request_adapter, request_order, source_group * tok_rows, tok_rows
@@ -112,17 +113,11 @@
     expanded = (rank[:, None, :] * chosen[:, :, None]).reshape(row_count, ADAPTERS * RANK)
     up = up_base + contract_last(expanded, adapter_out[0])
     hidden = (jax.nn.silu(gate_pre) * up).astype(jnp.bfloat16)
-    down_w = down_weight[0]
-    scattered = lax.psum_scatter(
-        lax.dot_general(
-            down_w, hidden, (((0,), (1,)), ((), ())), preferred_element_type=jnp.float32
-        ).astype(jnp.bfloat16),
-        "mp",
-        scatter_dimension=0,
-        tiled=True,
+    hidden_full = lax.all_gather(hidden, "mp", axis=1, tiled=True)
+    down_local = jnp.dot(hidden_full, down_cols_w, preferred_element_type=jnp.float32).astype(
+        jnp.bfloat16
     )
-    returned = lax.all_to_all(scattered, "expert", split_axis=1, concat_axis=1, tiled=True)
-    returned_rows = jnp.transpose(returned)
+    returned_rows = lax.all_to_all(down_local, "expert", split_axis=0, concat_axis=0, tiled=True)
     picked = returned_rows[slot_index].astype(jnp.float32)
     mixed = jnp.sum(route_gate[:, :, None] * picked, axis=1)
     return mixed.astype(jnp.bfloat16)

time: 285 us -> 267 us (0.937)
  waiting for transfers between devices: 181 us -> 152 us
  blocking collectives: 0 us -> 25.8 us
  local copies, waits for them, and re-layouts: 27.1 us -> 16.4 us
    unnamed x3 -> x2, waiting for transfers between devices: 98 us -> 0.03 us
    all_gather x0 -> x1, waiting for transfers between devices: none -> 66.8 us  [on_device(): hidden_full = lax.all_gather(hidden, 'mp', axis=1, tiled=True)]
    all_to_all x0 -> x1, blocking collectives: none -> 25.8 us  [on_device(): lax.all_to_all(down_weight[0], 'mp', split_axis=1, concat_axis=0, tiled=T...]
    unnamed x20 -> x19, local copies, waits for them, and re-layouts: 15.8 us -> 2.74 us
    dot_general x3 -> x4, matrix products: 13.7 us -> 13.7 us  [contract_last(): lax.dot_general(left, right, (((1,), (1,)), ((), ())), preferred_element_...]
where the time goes in v3:
time: 267 us
  waiting for transfers between devices  152 us (57%)
  blocking collectives  25.8 us (10%)
  matrix products  25.5 us (10%)
  starting transfers between devices  23.8 us (9%)
  local copies, waits for them, and re-layouts  16.4 us (6%)
  between operations  13.8 us (5%)
  other arithmetic  9.58 us (4%)
    all_gather x1, waiting for transfers between devices, on_device(): hidden_full = lax.all_gather(hidden, 'mp', axis=1, tiled=True)  66.8 us
    all_gather x1, waiting for transfers between devices, on_device(): gathered = lax.all_gather(payload2, 'mp', axis=1, tiled=True)  59.1 us
    all_to_all x1, blocking collectives, on_device(): lax.all_to_all(down_weight[0], 'mp', split_axis=1, concat_axis=0, tiled=T...  25.8 us
    all_to_all x1, waiting for transfers between devices, on_device(): lax.all_to_all(payload.reshape(groups * chunk, local_feat), 'expert', spl...  14.9 us
    dot_general x4, matrix products, contract_last(): lax.dot_general(left, right, (((1,), (1,)), ((), ())), preferred_element_...  13.7 us
    all_to_all x1, waiting for transfers between devices, on_device(): lax.all_to_all(down_local, 'expert', split_axis=0, concat_axis=0, tiled=T...  11.3 us
    dot_general x1, matrix products, on_device(): jnp.dot(hidden_full, down_cols_w, preferred_element_type=jnp.float32)  9.78 us
    all_to_all x1, starting transfers between devices, on_device(): lax.all_to_all(rank_w, 'mp', split_axis=1, concat_axis=0, tiled=True)  8.58 us
  transfers between devices with their start and end apart: 5, of which 4 were waited for; matrix products, arithmetic and copies ran while one was open for 4% of the time, Pallas kernels for 0%

profile of v3, /device:TPU:1, one launch (start us, length us, event | category | flops | bytes accessed | tf_op | source)
XLA Modules:
  0.0 266.8 jit_solution(568058251567174584)
XLA Ops:
  6.5 1.2 all_to_all.39
  7.9 0.8 reshape.182
  8.7 8.6 %all-to-all-start.1 = ((bf16[32,2,1024]{2,1,0:T(2,128)(2,1)}), bf16[32,2,1024]{2,1,0:T(2,128)(2,1)S(1)}, u32[]{:S(2)}, u32[]{:S(2)}) async-start(bf16[32,2,1024]{2,1,0:T(2,128)(2,1)} %reshape.182), calls=%async_computation.1 | async-start | bytes 262144 | tf_op jit(solution)/shard_map/all_to_all | solution.py:61
  17.3 0.8 copy.88
  18.5 0.9 select_reduce_fusion.2
  19.9 2.3 reduce-window.18
  23.0 0.7 compare_select_fusion
  23.7 0.9 fusion.5
  24.7 1.1 fusion.11
  26.0 0.8 pad_maximum_fusion
  26.8 8.2 %all-to-all-start = ((bf16[8,260,64]{1,2,0:T(8,128)(2,1)}), bf16[8,260,64]{1,2,0:T(8,128)(2,1)S(1)}, u32[]{:S(2)}, u32[]{:S(2)}) async-start(bf16[8,260,64]{1,2,0:T(8,128)(2,1)} %pad_maximum_fusion), calls=%async_computation | async-start | bytes 786432 | tf_op jit(solution)/shard_map/all_to_all | solution.py:84
  35.3 14.9 %all-to-all-done = bf16[8,260,64]{1,2,0:T(8,128)(2,1)S(1)} async-done(((bf16[8,260,64]{1,2,0:T(8,128)(2,1)}), bf16[8,260,64]{1,2,0:T(8,128)(2,1)S(1)}, u32[]{:S(2)}, u32[]{:S(2)}) %all-to-all-start) | async-done | bytes 266272 | tf_op jit(solution)/shard_map/all_to_all | solution.py:84
  50.8 1.3 multiply_reduce_fusion
  52.8 0.8 pad_maximum_fusion.1
  53.8 59.1 %all-gather.3.cloned.1.call-done = bf16[2560,2048]{0,1:T(8,128)(2,1)} async-done(((bf16[2560,64]{0,1:T(8,128)(2,1)}), bf16[2560,2048]{0,1:T(8,128)(2,1)}) %all-gather.3.cloned.1.call-update) | async-done | bytes 10485776 | tf_op jit(solution)/shard_map/all_gather | solution.py:100
  112.9 1.6 slice-done
  115.4 0.3 broadcast_multiply_fusion
  115.7 5.1 %fusion.2 = f32[2048,176]{0,1:T(8,128)S(1)} fusion(bf16[2560,2048]{0,1:T(8,128)(2,1)} %all-gather.3.cloned.1.call-done, bf16[1,176,2048]{2,1,0:T(8,128)(2,1)S(1)} %copy-done), kind=kOutput, calls=%fused_computation.4 | convolution fusion | flops 1476395008 | bytes 10551296 | tf_op jit(solution)/shard_map/dot_general | solution.py:35
  120.9 5.1 %fusion = f32[2048,176]{0,1:T(8,128)S(1)} fusion(bf16[2560,2048]{0,1:T(8,128)(2,1)} %all-gather.3.cloned.1.call-done, bf16[1,176,2048]{2,1,0:T(8,128)(2,1)S(1)} %copy-done.3), kind=kOutput, calls=%fused_computation.2 | convolution fusion | flops 1476395008 | bytes 10551296 | tf_op jit(solution)/shard_map/dot_general | solution.py:35
  126.0 2.2 fusion.10
  128.2 0.5 copy.103
  128.8 25.8 %all_to_all.53 = bf16[176,32,64]{0,2,1:T(8,128)(2,1)S(1)} all-to-all(bf16[176,32,64]{0,2,1:T(8,128)(2,1)S(1)} %bitcast.69), channel_id=1, replica_groups=mesh['expert'=8,'mp'=32] {'mp'}, dimensions={1} | all-to-all | bytes 1441792 | tf_op jit(solution)/shard_map/all_to_all | solution.py:62
  154.6 0.6 copy.104
  155.2 1.9 all_to_all.45
  157.1 66.8 %all-gather.5.cloned.1.call-done = bf16[2048,5632]{0,1:T(8,128)(2,1)} async-done(((bf16[2048,176]{0,1:T(8,128)(2,1)}), bf16[2048,5632]{0,1:T(8,128)(2,1)}) %all-gather.5.cloned.1.call-update) | async-done | bytes 23068688 | tf_op jit(solution)/shard_map/all_gather | solution.py:116
  223.9 9.8 %convolution_convert_fusion = bf16[2048,64]{0,1:T(8,128)(2,1)S(1)} fusion(bf16[5632,64]{0,1:T(8,128)(2,1)S(1)} %all_to_all.45, bf16[2048,5632]{0,1:T(8,128)(2,1)} %all-gather.5.cloned.1.call-done), kind=kOutput, calls=%fused_computation.14 | convolution fusion | flops 1476526080 | bytes 24051712 | tf_op jit(solution)/shard_map/dot_general | solution.py:117
  233.7 0.7 copy.120
  234.4 6.7 %all-to-all-start.3 = ((bf16[8,256,64]{1,2,0:T(8,128)(2,1)}), bf16[8,256,64]{1,2,0:T(8,128)(2,1)S(1)}, u32[]{:S(2)}, u32[]{:S(2)}) async-start(bf16[8,256,64]{1,2,0:T(8,128)(2,1)} %bitcast.63), calls=%async_computation.3 | async-start | bytes 524288 | tf_op jit(solution)/shard_map/all_to_all | solution.py:120
  241.7 11.3 %all-to-all-done.3 = bf16[8,256,64]{1,2,0:T(8,128)(2,1)S(1)} async-done(((bf16[8,256,64]{1,2,0:T(8,128)(2,1)}), bf16[8,256,64]{1,2,0:T(8,128)(2,1)S(1)}, u32[]{:S(2)}, u32[]{:S(2)}) %all-to-all-start.3) | async-done | bytes 262176 | tf_op jit(solution)/shard_map/all_to_all | solution.py:120
  253.2 3.2 %gather_fusion = bf16[1024,64]{1,0:T(8,128)(2,1)S(1)} fusion(bf16[2048,64]{1,0:T(8,128)(2,1)S(1)} %bitcast.67, s32[1024]{0:T(1024)S(1)} %broadcast_clamp_fusion), kind=kCustom, calls=%fused_computation | custom fusion | bytes 266240 | tf_op jit(solution)/shard_map/gather | solution.py:121
  256.4 2.8 %fusion.20 = bf16[512,64]{1,0:T(8,128)(2,1)S(1)} fusion(bf16[512,2,64]{2,1,0:T(2,128)(2,1)S(1)} %bitcast.73, f32[512,2]{1,0:T(8,128)S(1)} %copy.87), kind=kLoop, calls=%fused_computation.24 | loop fusion | flops 163840 | bytes 200704 | tf_op jit(solution)/shard_map/reduce_sum | solution.py:122
  259.3 0.7 copy.108
  (64 shorter events, 5.5 us)
Async XLA Ops:
  6.5 109.2 %copy-start = (bf16[1,176,2048]{2,1,0:T(8,128)(2,1)S(1)}, bf16[1,176,2048]{2,1,0:T(8,128)(2,1)}, u32[]{:S(2)}) copy-start(bf16[1,176,2048]{2,1,0:T(8,128)(2,1)} %param.18) | copy-start | bytes 2162692
  6.5 18.1 %copy-start.5 = (bf16[512,64]{0,1:T(8,128)(2,1)S(1)}, bf16[512,64]{0,1:T(8,128)(2,1)}, u32[]{:S(2)}) copy-start(bf16[512,64]{0,1:T(8,128)(2,1)} %param.11) | copy-start | bytes 196612
  8.7 18.1 %all-to-all-start.1 = ((bf16[32,2,1024]{2,1,0:T(2,128)(2,1)}), bf16[32,2,1024]{2,1,0:T(2,128)(2,1)S(1)}, u32[]{:S(2)}, u32[]{:S(2)}) async-start(bf16[32,2,1024]{2,1,0:T(2,128)(2,1)} %reshape.182), calls=%async_computation.1 | async-start | bytes 262144 | tf_op jit(solution)/shard_map/all_to_all | solution.py:61
  26.8 23.3 %all-to-all-start = ((bf16[8,260,64]{1,2,0:T(8,128)(2,1)}), bf16[8,260,64]{1,2,0:T(8,128)(2,1)S(1)}, u32[]{:S(2)}, u32[]{:S(2)}) async-start(bf16[8,260,64]{1,2,0:T(8,128)(2,1)} %pad_maximum_fusion), calls=%async_computation | async-start | bytes 786432 | tf_op jit(solution)/shard_map/all_to_all | solution.py:84
  35.0 77.9 %all-gather.3.cloned.1.call-start = ((), (), s32[]{:S(2)}) async-start(), calls=%async_computation.4 | async-start | bytes 10813440 | tf_op jit(solution)/shard_map/all_gather | solution.py:100
  53.6 170.3 %all-gather.5.cloned.1.call-start = ((), (), s32[]{:S(2)}) async-start(), calls=%async_computation.5 | async-start | bytes 23789568 | tf_op jit(solution)/shard_map/all_gather | solution.py:116
  112.9 1.6 slice-start
  115.7 5.1 %copy-start.3 = (bf16[1,176,2048]{2,1,0:T(8,128)(2,1)S(1)}, bf16[1,176,2048]{2,1,0:T(8,128)(2,1)}, u32[]{:S(2)}) copy-start(bf16[1,176,2048]{2,1,0:T(8,128)(2,1)} %param.17) | copy-start | bytes 2162692
  120.9 5.1 %copy-start.4 = (bf16[1,176,1024]{2,1,0:T(8,128)(2,1)S(1)}, bf16[1,176,1024]{2,1,0:T(8,128)(2,1)}, u32[]{:S(2)}) copy-start(bf16[1,176,1024]{2,1,0:T(8,128)(2,1)} %param.21) | copy-start | bytes 1081348
  126.0 2.2 copy-start.1
  157.1 84.4 %copy-start.2 = (f32[512,2]{0,1:T(2,128)S(1)}, f32[512,2]{0,1:T(2,128)}, u32[]{:S(2)}) copy-start(f32[512,2]{0,1:T(2,128)} %param.13) | copy-start | bytes 12292
  234.4 18.5 %all-to-all-start.3 = ((bf16[8,256,64]{1,2,0:T(8,128)(2,1)}), bf16[8,256,64]{1,2,0:T(8,128)(2,1)S(1)}, u32[]{:S(2)}, u32[]{:S(2)}) async-start(bf16[8,256,64]{1,2,0:T(8,128)(2,1)} %bitcast.63), calls=%async_computation.3 | async-start | bytes 524288 | tf_op jit(solution)/shard_map/all_to_all | solution.py:120
Sparse Core Ops, SparseCore 0:
  53.7 59.1 all-gather.2
  128.4 95.5 all-gather.4

commit v4 on v3

--- a/solution.py
+++ b/solution.py
@@ -51,15 +51,27 @@
     adapter_out,
 ):
     tok_rows, local_feat = tokens.shape
+    width = gate_weight.shape[2]
+    lora_width = adapter_out.shape[2]
     groups = lax.axis_size("expert")
-    n_mp = lax.axis_size("mp")
+    n_chip = lax.axis_size("chip")
+    n_core = lax.axis_size("core")
+    n_mp = n_chip * n_core
     capacity = 4 * tok_rows // groups
     total_slots = groups * capacity
+    half = total_slots // n_core
+    core = lax.axis_index("core")
     source_group = lax.axis_index("expert")
 
-    rank_w = adapter_in[0]
-    rank_cols_w = lax.all_to_all(rank_w, "mp", split_axis=1, concat_axis=0, tiled=True)
-    down_cols_w = lax.all_to_all(down_weight[0], "mp", split_axis=1, concat_axis=0, tiled=True)
+    rank_cols_w = lax.all_to_all(
+        adapter_in[0], ("chip", "core"), split_axis=1, concat_axis=0, tiled=True
+    )
+    own_w = jnp.concatenate([gate_weight[0], up_weight[0], down_weight[0], adapter_out[0]], axis=1)
+    partner_w = lax.ppermute(own_w, "core", [(0, 1), (1, 0)])
+    pair_w = jnp.concatenate([own_w, partner_w], axis=0)
+    down_cols_w = lax.all_to_all(
+        pair_w[:, 2 * width : 3 * width], "chip", split_axis=1, concat_axis=0, tiled=True
+    )
 
     adapter_of = token_adapters(
         request_lengths, request_adapter, request_order, source_group * tok_rows, tok_rows
@@ -94,29 +106,40 @@
     )
     part_rank = jnp.sum(part_all.reshape(row_count, ADAPTERS, RANK) * pick[:, :, None], axis=1)
     part_rows = row_count * RANK // local_feat
-    payload2 = jnp.concatenate(
-        [arrived_local, part_rank.astype(tokens.dtype).reshape(part_rows, local_feat)], axis=0
+    halves = jnp.concatenate(
+        [
+            arrived_local.reshape(n_core, half, local_feat),
+            part_rank.astype(tokens.dtype).reshape(n_core, part_rows // n_core, local_feat),
+        ],
+        axis=1,
     )
-    gathered = lax.all_gather(payload2, "mp", axis=1, tiled=True)
-    arrived = gathered[:row_count]
+    swapped = lax.all_to_all(halves, "core", split_axis=0, concat_axis=0, tiled=True)
+    pair_rows = jnp.transpose(swapped, (1, 0, 2)).reshape(swapped.shape[1], n_core * local_feat)
+    gathered = lax.all_gather(pair_rows, "chip", axis=1, tiled=True)
+    arrived = gathered[:half]
+    rank_rows = part_rows // n_core
     rank = (
-        jnp.sum(
-            gathered[row_count:].reshape(part_rows, n_mp, local_feat).astype(jnp.float32), axis=1
-        )
-        .reshape(row_count, RANK)
+        jnp.sum(gathered[half:].reshape(rank_rows, n_mp, local_feat).astype(jnp.float32), axis=1)
+        .reshape(half, RANK)
         .astype(jnp.bfloat16)
     )
-
-    gate_pre = contract_last(arrived, gate_weight[0])
-    up_base = contract_last(arrived, up_weight[0])
-    chosen = pick.astype(jnp.bfloat16)
-    expanded = (rank[:, None, :] * chosen[:, :, None]).reshape(row_count, ADAPTERS * RANK)
-    up = up_base + contract_last(expanded, adapter_out[0])
-    hidden = (jax.nn.silu(gate_pre) * up).astype(jnp.bfloat16)
-    hidden_full = lax.all_gather(hidden, "mp", axis=1, tiled=True)
-    down_local = jnp.dot(hidden_full, down_cols_w, preferred_element_type=jnp.float32).astype(
+    half_adapter = lax.dynamic_slice_in_dim(arrived_adapter, core * half, half)
+    chosen = (half_adapter[:, None] == jnp.arange(ADAPTERS, dtype=jnp.int32)[None, :]).astype(
         jnp.bfloat16
     )
+
+    gate_pre = contract_last(arrived, pair_w[:, :width])
+    up_base = contract_last(arrived, pair_w[:, width : 2 * width])
+    expanded = (rank[:, None, :] * chosen[:, :, None]).reshape(half, ADAPTERS * RANK)
+    up = up_base + contract_last(expanded, pair_w[:, 3 * width : 3 * width + lora_width])
+    hidden = (jax.nn.silu(gate_pre) * up).astype(jnp.bfloat16)
+    hidden_full = lax.all_gather(hidden, "chip", axis=1, tiled=True)
+    down_pair = jnp.dot(hidden_full, down_cols_w, preferred_element_type=jnp.float32).astype(
+        jnp.bfloat16
+    )
+    down_local = lax.all_to_all(
+        down_pair.reshape(half, n_core, local_feat), "core", split_axis=1, concat_axis=0, tiled=True
+    ).reshape(total_slots, local_feat)
     returned_rows = lax.all_to_all(down_local, "expert", split_axis=0, concat_axis=0, tiled=True)
     picked = returned_rows[slot_index].astype(jnp.float32)
     mixed = jnp.sum(route_gate[:, :, None] * picked, axis=1)
@@ -124,20 +147,25 @@
 
 
 def solution(mesh):
+    n_expert, n_mp = mesh.devices.shape
+    split = jax.sharding.Mesh(
+        mesh.devices.reshape(n_expert, n_mp // 2, 2), ("expert", "chip", "core")
+    )
+    mp = ("chip", "core")
     in_specs = (
-        P("expert", "mp"),
+        P("expert", mp),
         P("expert", None),
         P("expert", None),
         P(),
         P(),
         P(),
-        P("expert", "mp", None),
-        P("expert", "mp", None),
-        P("expert", "mp", None),
-        P("expert", "mp", None),
-        P("expert", "mp", None),
+        P("expert", mp, None),
+        P("expert", mp, None),
+        P("expert", mp, None),
+        P("expert", mp, None),
+        P("expert", mp, None),
     )
-    out_specs = P("expert", "mp")
+    out_specs = P("expert", mp)
     return jax.shard_map(
-        on_device, mesh=mesh, in_specs=in_specs, out_specs=out_specs, check_vma=False
+        on_device, mesh=split, in_specs=in_specs, out_specs=out_specs, check_vma=False
     )

time: 267 us -> 269 us (level)
  waiting for transfers between devices: 152 us -> 138 us
  blocking collectives: 25.8 us -> 38.2 us
  other arithmetic: 9.58 us -> 21.5 us
  matrix products: 25.5 us -> 15.6 us
    all_gather x2, waiting for transfers between devices: 126 us -> 107 us  [the longest x1 67.2 us: on_device(): hidden_full = lax.all_gather(hidden, 'chip', axis=1, tiled=True)]
    all_to_all x1 -> x3, blocking collectives: 25.8 us -> 38.2 us  [the longest x1 29 us: on_device(): lax.all_to_all(pair_w[:, 2 * width:3 * width], 'chip', split_axis=1, conc...]
    concatenate x1 -> x3, other arithmetic: 0.76 us -> 12.1 us  [the longest x1 10.3 us: on_device(): pair_w = jnp.concatenate([own_w, partner_w], axis=0)]
    dot_general x4, matrix products: 13.7 us -> 7.58 us  [contract_last(): lax.dot_general(left, right, (((1,), (1,)), ((), ())), preferred_element_...]
    ppermute x0 -> x1, waiting for transfers between devices: none -> 4.57 us  [on_device(): partner_w = lax.ppermute(own_w, 'core', [(0, 1), (1, 0)])]
    dot_general x1, matrix products: 9.78 us -> 6.05 us  [on_device(): jnp.dot(hidden_full, down_cols_w, preferred_element_type=jnp.float32)]
  transfers between devices with their start and end apart: 5 -> 6, of which waited for: 4 -> 5; matrix products, arithmetic and copies ran while one was open for 4% -> 8% of each run, Pallas kernels for 0% -> 0%
where the time goes in v4:
time: 269 us
  waiting for transfers between devices  138 us (51%)
  blocking collectives  38.2 us (14%)
  starting transfers between devices  23.9 us (9%)
  other arithmetic  21.5 us (8%)
  local copies, waits for them, and re-layouts  17.9 us (7%)
  matrix products  15.6 us (6%)
  between operations  13.8 us (5%)
    all_gather x1, waiting for transfers between devices, on_device(): hidden_full = lax.all_gather(hidden, 'chip', axis=1, tiled=True)  67.2 us
    all_gather x1, waiting for transfers between devices, on_device(): gathered = lax.all_gather(pair_rows, 'chip', axis=1, tiled=True)  40.2 us
    all_to_all x1, blocking collectives, on_device(): lax.all_to_all(pair_w[:, 2 * width:3 * width], 'chip', split_axis=1, conc...  29 us
    all_to_all x1, waiting for transfers between devices, on_device(): lax.all_to_all(payload.reshape(groups * chunk, local_feat), 'expert', spl...  14.9 us
    all_to_all x1, waiting for transfers between devices, on_device(): lax.all_to_all(down_local, 'expert', split_axis=0, concat_axis=0, tiled=T...  10.7 us
    concatenate x1, other arithmetic, on_device(): pair_w = jnp.concatenate([own_w, partner_w], axis=0)  10.3 us
    all_to_all x1, starting transfers between devices, on_device(): lax.all_to_all(adapter_in[0], ('chip', 'core'), split_axis=1, concat_axis...  8.58 us
    all_to_all x1, starting transfers between devices, on_device(): lax.all_to_all(payload.reshape(groups * chunk, local_feat), 'expert', spl...  8.19 us
  transfers between devices with their start and end apart: 6, of which 5 were waited for; matrix products, arithmetic and copies ran while one was open for 8% of the time, Pallas kernels for 0%

profile of v4, /device:TPU:1, one launch (start us, length us, event | category | flops | bytes accessed | tf_op | source)
XLA Modules:
  0.0 268.6 jit_solution(5500741804213924032)
XLA Ops:
  6.5 1.2 all_to_all.53
  7.9 0.8 reshape.186
  8.7 8.6 %all-to-all-start.1 = ((bf16[32,2,1024]{2,1,0:T(2,128)(2,1)}), bf16[32,2,1024]{2,1,0:T(2,128)(2,1)S(1)}, u32[]{:S(2)}, u32[]{:S(2)}) async-start(bf16[32,2,1024]{2,1,0:T(2,128)(2,1)} %reshape.186), calls=%async_computation.1 | async-start | bytes 262144 | tf_op jit(solution)/shard_map/all_to_all | solution.py:66
  17.3 0.8 copy.91
  18.5 0.9 select_reduce_fusion.2
  19.9 2.3 reduce-window.18
  23.0 0.9 fusion.5
  24.0 1.1 fusion.9
  26.1 8.2 %all-to-all-start = ((bf16[8,260,64]{1,2,0:T(8,128)(2,1)}), bf16[8,260,64]{1,2,0:T(8,128)(2,1)S(1)}, u32[]{:S(2)}, u32[]{:S(2)}) async-start(bf16[8,260,64]{1,2,0:T(8,128)(2,1)} %pad_maximum_fusion.2), calls=%async_computation | async-start | bytes 786432 | tf_op jit(solution)/shard_map/all_to_all | solution.py:96
  34.6 14.9 %all-to-all-done = bf16[8,260,64]{1,2,0:T(8,128)(2,1)S(1)} async-done(((bf16[8,260,64]{1,2,0:T(8,128)(2,1)}), bf16[8,260,64]{1,2,0:T(8,128)(2,1)S(1)}, u32[]{:S(2)}, u32[]{:S(2)}) %all-to-all-start) | async-done | bytes 266272 | tf_op jit(solution)/shard_map/all_to_all | solution.py:96
  50.2 1.3 multiply_reduce_fusion
  52.6 4.8 %all_to_all.73 = bf16[2,1280,64]{1,2,0:T(8,128)(2,1)} all-to-all(bf16[2,1280,64]{1,2,0:T(8,128)(2,1)S(1)} %copy.105), channel_id=1, replica_groups=mesh['expert'=8,'chip'=16,'core'=2] {'core'}, dimensions={0} | all-to-all | bytes 655360 | tf_op jit(solution)/shard_map/all_to_all | solution.py:116
  57.5 1.6 pad_maximum_fusion.1
  59.5 4.6 %collective-permute-done = bf16[176,7168]{1,0:T(8,128)(2,1)S(1)} collective-permute-done((bf16[176,7168]{1,0:T(8,128)(2,1)}, bf16[176,7168]{1,0:T(8,128)(2,1)S(1)}, u32[]{:S(2)}, u32[]{:S(2)}) %collective-permute-start) | collective-permute-done | bytes 2523168 | tf_op jit(solution)/shard_map/ppermute | solution.py:70
  64.1 10.3 %pad_maximum_fusion = bf16[352,7168]{1,0:T(8,128)(2,1)} fusion(bf16[176,7168]{1,0:T(8,128)(2,1)S(1)} %collective-permute-done, bf16[176,1024]{1,0:T(8,128)(2,1)} %bitcast.84, bf16[176,2048]{1,0:T(8,128)(2,1)S(1)} %bitcast.72, bf16[176,2048]{1,0:T(8,128)(2,1)} %bitcast.75, bf16[176,2048]{1,0:T(8,128)(2,1)} %bitcast.79), kind=kLoop, calls=%fused_computation.2 | loop fusion | flops 25231360 | bytes 10092544 | tf_op jit(solution)/shard_map/concatenate | solution.py:71
  74.4 40.2 %all-gather.3.cloned.1.call-done = bf16[1280,2048]{0,1:T(8,128)(2,1)} async-done(((bf16[1280,128]{0,1:T(8,128)(2,1)}), bf16[1280,2048]{0,1:T(8,128)(2,1)}) %all-gather.3.cloned.1.call-update) | async-done | bytes 5242896 | tf_op jit(solution)/shard_map/all_gather | solution.py:118
  114.6 2.3 slice.58
  116.9 1.4 reduce
  118.4 0.9 convert_element_type.95
  119.2 1.0 copy.107
  120.5 2.1 fusion.22
  122.9 1.6 copy-done.5
  124.5 1.6 fusion.1
  126.1 2.6 multiply_convert_fusion
  129.0 29.0 %all_to_all.74 = bf16[352,16,128]{2,0,1:T(8,128)(2,1)S(1)} all-to-all(bf16[352,16,128]{2,0,1:T(8,128)(2,1)S(1)} %copy_bitcast_fusion), channel_id=1, replica_groups=mesh['expert'=8,'chip'=16,'core'=2] {'chip'}, dimensions={1} | all-to-all | bytes 2883584 | tf_op jit(solution)/shard_map/all_to_all | solution.py:72
  158.0 67.2 %all-gather.5.cloned.1.call-done = bf16[1024,5632]{0,1:T(8,128)(2,1)} async-done(((bf16[1024,352]{0,1:T(8,128)(2,1)}), bf16[1024,5632]{0,1:T(8,128)(2,1)}) %all-gather.5.cloned.1.call-update) | async-done | bytes 11534352 | tf_op jit(solution)/shard_map/all_gather | solution.py:136
  225.2 6.0 %convolution_convert_fusion = bf16[1024,128]{0,1:T(8,128)(2,1)S(1)} fusion(bf16[1024,5632]{0,1:T(8,128)(2,1)} %all-gather.5.cloned.1.call-done, bf16[5632,128]{1,0:T(8,128)(2,1)S(1)} %bitcast.91), kind=kOutput, calls=%fused_computation.23 | convolution fusion | flops 1476526080 | bytes 13238272 | tf_op jit(solution)/shard_map/dot_general | solution.py:137
  231.2 4.4 %all_to_all.75 = bf16[1024,2,64]{0,2,1:T(8,128)(2,1)S(1)} all-to-all(bf16[1024,2,64]{0,2,1:T(8,128)(2,1)S(1)} %bitcast.99), channel_id=1, replica_groups=mesh['expert'=8,'chip'=16,'core'=2] {'core'}, dimensions={1} | all-to-all | bytes 524288 | tf_op jit(solution)/shard_map/all_to_all | solution.py:140
  236.8 6.7 %all-to-all-start.5 = ((bf16[8,256,64]{1,2,0:T(8,128)(2,1)}), bf16[8,256,64]{1,2,0:T(8,128)(2,1)S(1)}, u32[]{:S(2)}, u32[]{:S(2)}) async-start(bf16[8,256,64]{1,2,0:T(8,128)(2,1)} %copy.110), calls=%async_computation.5 | async-start | bytes 524288 | tf_op jit(solution)/shard_map/all_to_all | solution.py:143
  244.0 10.7 %all-to-all-done.5 = bf16[8,256,64]{1,2,0:T(8,128)(2,1)S(1)} async-done(((bf16[8,256,64]{1,2,0:T(8,128)(2,1)}), bf16[8,256,64]{1,2,0:T(8,128)(2,1)S(1)}, u32[]{:S(2)}, u32[]{:S(2)}) %all-to-all-start.5) | async-done | bytes 262176 | tf_op jit(solution)/shard_map/all_to_all | solution.py:143
  254.9 3.2 %gather_fusion = bf16[1024,64]{1,0:T(8,128)(2,1)S(1)} fusion(bf16[2048,64]{1,0:T(8,128)(2,1)S(1)} %bitcast.70, s32[1024]{0:T(1024)S(1)} %broadcast_clamp_fusion), kind=kCustom, calls=%fused_computation | custom fusion | bytes 266240 | tf_op jit(solution)/shard_map/gather | solution.py:144
  258.2 2.8 %fusion.32 = bf16[512,64]{1,0:T(8,128)(2,1)S(1)} fusion(bf16[512,2,64]{2,1,0:T(2,128)(2,1)S(1)} %bitcast.93, f32[512,2]{1,0:T(8,128)S(1)} %copy.90), kind=kLoop, calls=%fused_computation.36 | loop fusion | flops 163840 | bytes 200704 | tf_op jit(solution)/shard_map/reduce_sum | solution.py:145
  (81 shorter events, 8.7 us)
Async XLA Ops:
  6.5 17.4 %copy-start = (bf16[512,64]{0,1:T(8,128)(2,1)S(1)}, bf16[512,64]{0,1:T(8,128)(2,1)}, u32[]{:S(2)}) copy-start(bf16[512,64]{0,1:T(8,128)(2,1)} %param.11) | copy-start | bytes 196612
  6.5 16.5 %copy-start.6 = (s32[512,2]{0,1:T(2,128)S(1)}, s32[512,2]{0,1:T(2,128)}, u32[]{:S(2)}) copy-start(s32[512,2]{0,1:T(2,128)} %param.12) | copy-start | bytes 12292
  8.7 17.4 %all-to-all-start.1 = ((bf16[32,2,1024]{2,1,0:T(2,128)(2,1)}), bf16[32,2,1024]{2,1,0:T(2,128)(2,1)S(1)}, u32[]{:S(2)}, u32[]{:S(2)}) async-start(bf16[32,2,1024]{2,1,0:T(2,128)(2,1)} %reshape.186), calls=%async_computation.1 | async-start | bytes 262144 | tf_op jit(solution)/shard_map/all_to_all | solution.py:66
  26.1 23.3 %all-to-all-start = ((bf16[8,260,64]{1,2,0:T(8,128)(2,1)}), bf16[8,260,64]{1,2,0:T(8,128)(2,1)S(1)}, u32[]{:S(2)}, u32[]{:S(2)}) async-start(bf16[8,260,64]{1,2,0:T(8,128)(2,1)} %pad_maximum_fusion.2), calls=%async_computation | async-start | bytes 786432 | tf_op jit(solution)/shard_map/all_to_all | solution.py:96
  34.3 80.3 %all-gather.3.cloned.1.call-start = ((), (), s32[]{:S(2)}) async-start(), calls=%async_computation.6 | async-start | bytes 5570560 | tf_op jit(solution)/shard_map/all_gather | solution.py:118
  51.5 6.0 %copy-start.1 = (bf16[1,176,2048]{2,1,0:T(8,128)(2,1)S(1)}, bf16[1,176,2048]{2,1,0:T(8,128)(2,1)}, u32[]{:S(2)}) copy-start(bf16[1,176,2048]{2,1,0:T(8,128)(2,1)} %param.19) | copy-start | bytes 2162692
  51.5 6.0 %copy-start.2 = (bf16[1,176,2048]{2,1,0:T(8,128)(2,1)S(1)}, bf16[1,176,2048]{2,1,0:T(8,128)(2,1)}, u32[]{:S(2)}) copy-start(bf16[1,176,2048]{2,1,0:T(8,128)(2,1)} %param.18) | copy-start | bytes 2162692
  51.5 6.0 %copy-start.3 = (bf16[1,176,2048]{2,1,0:T(8,128)(2,1)S(1)}, bf16[1,176,2048]{2,1,0:T(8,128)(2,1)}, u32[]{:S(2)}) copy-start(bf16[1,176,2048]{2,1,0:T(8,128)(2,1)} %param.17) | copy-start | bytes 2162692
  51.5 6.0 %copy-start.4 = (bf16[1,176,1024]{2,1,0:T(8,128)(2,1)S(1)}, bf16[1,176,1024]{2,1,0:T(8,128)(2,1)}, u32[]{:S(2)}) copy-start(bf16[1,176,1024]{2,1,0:T(8,128)(2,1)} %param.21) | copy-start | bytes 1081348
  57.4 167.7 %all-gather.5.cloned.1.call-start = ((), (), s32[]{:S(2)}) async-start(), calls=%async_computation.7 | async-start | bytes 12255232 | tf_op jit(solution)/shard_map/all_gather | solution.py:136
  59.1 5.0 %collective-permute-start = (bf16[176,7168]{1,0:T(8,128)(2,1)}, bf16[176,7168]{1,0:T(8,128)(2,1)S(1)}, u32[]{:S(2)}, u32[]{:S(2)}) collective-permute-start(bf16[176,7168]{1,0:T(8,128)(2,1)} %pad_maximum_fusion.1), channel_id=1, source_target_pairs={{0,1},{1,0},{2,3},{3,2},{4,5},{5,4},{6,7},{7,6},{8,9},{9,8},{10,11... | collective-permute-start | bytes 7569416 | tf_op jit(solution)/shard_map/ppermute | solution.py:70
  120.3 2.3 slice-start
  120.5 2.4 slice-start.1
  120.5 4.0 %copy-start.5 = (bf16[1280,2048]{0,1:T(8,128)(2,1)S(1)}, bf16[1280,2048]{0,1:T(8,128)(2,1)}, u32[]{:S(2)}) copy-start(bf16[1280,2048]{0,1:T(8,128)(2,1)} %all-gather.3.cloned.1.call-done) | copy-start | bytes 15728644
  231.2 12.6 %copy-start.7 = (f32[512,2]{0,1:T(2,128)S(1)}, f32[512,2]{0,1:T(2,128)}, u32[]{:S(2)}) copy-start(f32[512,2]{0,1:T(2,128)} %param.13) | copy-start | bytes 12292
  236.8 17.9 %all-to-all-start.5 = ((bf16[8,256,64]{1,2,0:T(8,128)(2,1)}), bf16[8,256,64]{1,2,0:T(8,128)(2,1)S(1)}, u32[]{:S(2)}, u32[]{:S(2)}) async-start(bf16[8,256,64]{1,2,0:T(8,128)(2,1)} %copy.110), calls=%async_computation.5 | async-start | bytes 524288 | tf_op jit(solution)/shard_map/all_to_all | solution.py:143
Sparse Core Ops, SparseCore 0:
  57.6 56.9 all-gather.2
  128.9 96.2 all-gather.4

commit v5 on v4

--- a/solution.py
+++ b/solution.py
@@ -128,15 +128,15 @@
         jnp.bfloat16
     )
 
-    gate_pre = contract_last(arrived, pair_w[:, :width])
-    up_base = contract_last(arrived, pair_w[:, width : 2 * width])
+    gate_pre = contract_last(pair_w[:, :width], arrived)
+    up_base = contract_last(pair_w[:, width : 2 * width], arrived)
     expanded = (rank[:, None, :] * chosen[:, :, None]).reshape(half, ADAPTERS * RANK)
-    up = up_base + contract_last(expanded, pair_w[:, 3 * width : 3 * width + lora_width])
+    up = up_base + contract_last(pair_w[:, 3 * width : 3 * width + lora_width], expanded)
     hidden = (jax.nn.silu(gate_pre) * up).astype(jnp.bfloat16)
-    hidden_full = lax.all_gather(hidden, "chip", axis=1, tiled=True)
-    down_pair = jnp.dot(hidden_full, down_cols_w, preferred_element_type=jnp.float32).astype(
-        jnp.bfloat16
-    )
+    hidden_full = lax.all_gather(hidden, "chip", axis=0, tiled=True)
+    down_pair = lax.dot_general(
+        hidden_full, down_cols_w, (((0,), (0,)), ((), ())), preferred_element_type=jnp.float32
+    ).astype(jnp.bfloat16)
     down_local = lax.all_to_all(
         down_pair.reshape(half, n_core, local_feat), "core", split_axis=1, concat_axis=0, tiled=True
     ).reshape(total_slots, local_feat)

time: 269 us -> 269 us (level)
  no operation moved by 1% of the time
where the time goes in v5:
time: 269 us
  waiting for transfers between devices  138 us (51%)
  blocking collectives  38.2 us (14%)
  starting transfers between devices  23.9 us (9%)
  other arithmetic  21.5 us (8%)
  local copies, waits for them, and re-layouts  17.9 us (7%)
  matrix products  15.6 us (6%)
  between operations  13.8 us (5%)
    all_gather x1, waiting for transfers between devices, on_device(): hidden_full = lax.all_gather(hidden, 'chip', axis=0, tiled=True)  67.2 us
    all_gather x1, waiting for transfers between devices, on_device(): gathered = lax.all_gather(pair_rows, 'chip', axis=1, tiled=True)  40.2 us
    all_to_all x1, blocking collectives, on_device(): lax.all_to_all(pair_w[:, 2 * width:3 * width], 'chip', split_axis=1, conc...  29 us
    all_to_all x1, waiting for transfers between devices, on_device(): lax.all_to_all(payload.reshape(groups * chunk, local_feat), 'expert', spl...  14.9 us
    all_to_all x1, waiting for transfers between devices, on_device(): lax.all_to_all(down_local, 'expert', split_axis=0, concat_axis=0, tiled=T...  10.7 us
    concatenate x1, other arithmetic, on_device(): pair_w = jnp.concatenate([own_w, partner_w], axis=0)  10.3 us
    all_to_all x1, starting transfers between devices, on_device(): lax.all_to_all(adapter_in[0], ('chip', 'core'), split_axis=1, concat_axis...  8.58 us
    all_to_all x1, starting transfers between devices, on_device(): lax.all_to_all(payload.reshape(groups * chunk, local_feat), 'expert', spl...  8.19 us
  transfers between devices with their start and end apart: 6, of which 5 were waited for; matrix products, arithmetic and copies ran while one was open for 8% of the time, Pallas kernels for 0%

profile of v5, /device:TPU:1, one launch (start us, length us, event | category | flops | bytes accessed | tf_op | source)
XLA Modules:
  0.0 268.6 jit_solution(5500741804213924032)
XLA Ops:
  6.5 1.2 all_to_all.53
  7.9 0.8 reshape.186
  8.7 8.6 %all-to-all-start.1 = ((bf16[32,2,1024]{2,1,0:T(2,128)(2,1)}), bf16[32,2,1024]{2,1,0:T(2,128)(2,1)S(1)}, u32[]{:S(2)}, u32[]{:S(2)}) async-start(bf16[32,2,1024]{2,1,0:T(2,128)(2,1)} %reshape.186), calls=%async_computation.1 | async-start | bytes 262144 | tf_op jit(solution)/shard_map/all_to_all | solution.py:66
  17.3 0.8 copy.91
  18.5 0.9 select_reduce_fusion.2
  19.9 2.3 reduce-window.18
  23.0 0.9 fusion.5
  24.0 1.1 fusion.9
  26.1 8.2 %all-to-all-start = ((bf16[8,260,64]{1,2,0:T(8,128)(2,1)}), bf16[8,260,64]{1,2,0:T(8,128)(2,1)S(1)}, u32[]{:S(2)}, u32[]{:S(2)}) async-start(bf16[8,260,64]{1,2,0:T(8,128)(2,1)} %pad_maximum_fusion.2), calls=%async_computation | async-start | bytes 786432 | tf_op jit(solution)/shard_map/all_to_all | solution.py:96
  34.6 14.9 %all-to-all-done = bf16[8,260,64]{1,2,0:T(8,128)(2,1)S(1)} async-done(((bf16[8,260,64]{1,2,0:T(8,128)(2,1)}), bf16[8,260,64]{1,2,0:T(8,128)(2,1)S(1)}, u32[]{:S(2)}, u32[]{:S(2)}) %all-to-all-start) | async-done | bytes 266272 | tf_op jit(solution)/shard_map/all_to_all | solution.py:96
  50.2 1.3 multiply_reduce_fusion
  52.6 4.8 %all_to_all.73 = bf16[2,1280,64]{1,2,0:T(8,128)(2,1)} all-to-all(bf16[2,1280,64]{1,2,0:T(8,128)(2,1)S(1)} %copy.105), channel_id=1, replica_groups=mesh['expert'=8,'chip'=16,'core'=2] {'core'}, dimensions={0} | all-to-all | bytes 655360 | tf_op jit(solution)/shard_map/all_to_all | solution.py:116
  57.5 1.6 pad_maximum_fusion.1
  59.5 4.6 %collective-permute-done = bf16[176,7168]{1,0:T(8,128)(2,1)S(1)} collective-permute-done((bf16[176,7168]{1,0:T(8,128)(2,1)}, bf16[176,7168]{1,0:T(8,128)(2,1)S(1)}, u32[]{:S(2)}, u32[]{:S(2)}) %collective-permute-start) | collective-permute-done | bytes 2523168 | tf_op jit(solution)/shard_map/ppermute | solution.py:70
  64.1 10.3 %pad_maximum_fusion = bf16[352,7168]{1,0:T(8,128)(2,1)} fusion(bf16[176,7168]{1,0:T(8,128)(2,1)S(1)} %collective-permute-done, bf16[176,1024]{1,0:T(8,128)(2,1)} %bitcast.84, bf16[176,2048]{1,0:T(8,128)(2,1)S(1)} %bitcast.72, bf16[176,2048]{1,0:T(8,128)(2,1)} %bitcast.75, bf16[176,2048]{1,0:T(8,128)(2,1)} %bitcast.79), kind=kLoop, calls=%fused_computation.2 | loop fusion | flops 25231360 | bytes 10092544 | tf_op jit(solution)/shard_map/concatenate | solution.py:71
  74.4 40.2 %all-gather.3.cloned.1.call-done = bf16[1280,2048]{0,1:T(8,128)(2,1)} async-done(((bf16[1280,128]{0,1:T(8,128)(2,1)}), bf16[1280,2048]{0,1:T(8,128)(2,1)}) %all-gather.3.cloned.1.call-update) | async-done | bytes 5242896 | tf_op jit(solution)/shard_map/all_gather | solution.py:118
  114.6 2.3 slice.58
  116.9 1.4 reduce
  118.4 0.9 convert_element_type.95
  119.2 1.0 copy.107
  120.5 2.1 fusion.22
  122.9 1.6 copy-done.5
  124.5 1.6 fusion.3
  126.1 2.6 multiply_convert_fusion
  129.0 29.0 %all_to_all.74 = bf16[352,16,128]{2,0,1:T(8,128)(2,1)S(1)} all-to-all(bf16[352,16,128]{2,0,1:T(8,128)(2,1)S(1)} %copy_bitcast_fusion), channel_id=1, replica_groups=mesh['expert'=8,'chip'=16,'core'=2] {'chip'}, dimensions={1} | all-to-all | bytes 2883584 | tf_op jit(solution)/shard_map/all_to_all | solution.py:72
  158.0 67.2 %all-gather.5.cloned.1.call-done = bf16[5632,1024]{1,0:T(8,128)(2,1)} async-done(((bf16[352,1024]{1,0:T(8,128)(2,1)}), bf16[5632,1024]{1,0:T(8,128)(2,1)}) %all-gather.5.cloned.1.call-update) | async-done | bytes 11534352 | tf_op jit(solution)/shard_map/all_gather | solution.py:136
  225.2 6.0 %convolution_convert_fusion = bf16[1024,128]{0,1:T(8,128)(2,1)S(1)} fusion(bf16[5632,1024]{1,0:T(8,128)(2,1)} %all-gather.5.cloned.1.call-done, bf16[5632,128]{1,0:T(8,128)(2,1)S(1)} %bitcast.91), kind=kOutput, calls=%fused_computation.23 | convolution fusion | flops 1476526080 | bytes 13238272 | tf_op jit(solution)/shard_map/dot_general | solution.py:137
  231.2 4.4 %all_to_all.75 = bf16[1024,2,64]{0,2,1:T(8,128)(2,1)S(1)} all-to-all(bf16[1024,2,64]{0,2,1:T(8,128)(2,1)S(1)} %bitcast.99), channel_id=1, replica_groups=mesh['expert'=8,'chip'=16,'core'=2] {'core'}, dimensions={1} | all-to-all | bytes 524288 | tf_op jit(solution)/shard_map/all_to_all | solution.py:140
  236.8 6.7 %all-to-all-start.5 = ((bf16[8,256,64]{1,2,0:T(8,128)(2,1)}), bf16[8,256,64]{1,2,0:T(8,128)(2,1)S(1)}, u32[]{:S(2)}, u32[]{:S(2)}) async-start(bf16[8,256,64]{1,2,0:T(8,128)(2,1)} %copy.110), calls=%async_computation.5 | async-start | bytes 524288 | tf_op jit(solution)/shard_map/all_to_all | solution.py:143
  244.0 10.7 %all-to-all-done.5 = bf16[8,256,64]{1,2,0:T(8,128)(2,1)S(1)} async-done(((bf16[8,256,64]{1,2,0:T(8,128)(2,1)}), bf16[8,256,64]{1,2,0:T(8,128)(2,1)S(1)}, u32[]{:S(2)}, u32[]{:S(2)}) %all-to-all-start.5) | async-done | bytes 262176 | tf_op jit(solution)/shard_map/all_to_all | solution.py:143
  254.9 3.2 %gather_fusion = bf16[1024,64]{1,0:T(8,128)(2,1)S(1)} fusion(bf16[2048,64]{1,0:T(8,128)(2,1)S(1)} %bitcast.70, s32[1024]{0:T(1024)S(1)} %broadcast_clamp_fusion), kind=kCustom, calls=%fused_computation | custom fusion | bytes 266240 | tf_op jit(solution)/shard_map/gather | solution.py:144
  258.2 2.8 %fusion.32 = bf16[512,64]{1,0:T(8,128)(2,1)S(1)} fusion(bf16[512,2,64]{2,1,0:T(2,128)(2,1)S(1)} %bitcast.93, f32[512,2]{1,0:T(8,128)S(1)} %copy.90), kind=kLoop, calls=%fused_computation.36 | loop fusion | flops 163840 | bytes 200704 | tf_op jit(solution)/shard_map/reduce_sum | solution.py:145
  (81 shorter events, 8.7 us)
Async XLA Ops:
  6.5 17.4 %copy-start = (bf16[512,64]{0,1:T(8,128)(2,1)S(1)}, bf16[512,64]{0,1:T(8,128)(2,1)}, u32[]{:S(2)}) copy-start(bf16[512,64]{0,1:T(8,128)(2,1)} %param.11) | copy-start | bytes 196612
  6.5 16.5 %copy-start.6 = (s32[512,2]{0,1:T(2,128)S(1)}, s32[512,2]{0,1:T(2,128)}, u32[]{:S(2)}) copy-start(s32[512,2]{0,1:T(2,128)} %param.12) | copy-start | bytes 12292
  8.7 17.4 %all-to-all-start.1 = ((bf16[32,2,1024]{2,1,0:T(2,128)(2,1)}), bf16[32,2,1024]{2,1,0:T(2,128)(2,1)S(1)}, u32[]{:S(2)}, u32[]{:S(2)}) async-start(bf16[32,2,1024]{2,1,0:T(2,128)(2,1)} %reshape.186), calls=%async_computation.1 | async-start | bytes 262144 | tf_op jit(solution)/shard_map/all_to_all | solution.py:66
  26.1 23.3 %all-to-all-start = ((bf16[8,260,64]{1,2,0:T(8,128)(2,1)}), bf16[8,260,64]{1,2,0:T(8,128)(2,1)S(1)}, u32[]{:S(2)}, u32[]{:S(2)}) async-start(bf16[8,260,64]{1,2,0:T(8,128)(2,1)} %pad_maximum_fusion.2), calls=%async_computation | async-start | bytes 786432 | tf_op jit(solution)/shard_map/all_to_all | solution.py:96
  34.3 80.3 %all-gather.3.cloned.1.call-start = ((), (), s32[]{:S(2)}) async-start(), calls=%async_computation.6 | async-start | bytes 5570560 | tf_op jit(solution)/shard_map/all_gather | solution.py:118
  51.5 6.0 %copy-start.1 = (bf16[1,176,2048]{2,1,0:T(8,128)(2,1)S(1)}, bf16[1,176,2048]{2,1,0:T(8,128)(2,1)}, u32[]{:S(2)}) copy-start(bf16[1,176,2048]{2,1,0:T(8,128)(2,1)} %param.19) | copy-start | bytes 2162692
  51.5 6.0 %copy-start.2 = (bf16[1,176,2048]{2,1,0:T(8,128)(2,1)S(1)}, bf16[1,176,2048]{2,1,0:T(8,128)(2,1)}, u32[]{:S(2)}) copy-start(bf16[1,176,2048]{2,1,0:T(8,128)(2,1)} %param.18) | copy-start | bytes 2162692
  51.5 6.0 %copy-start.3 = (bf16[1,176,2048]{2,1,0:T(8,128)(2,1)S(1)}, bf16[1,176,2048]{2,1,0:T(8,128)(2,1)}, u32[]{:S(2)}) copy-start(bf16[1,176,2048]{2,1,0:T(8,128)(2,1)} %param.17) | copy-start | bytes 2162692
  51.5 6.0 %copy-start.4 = (bf16[1,176,1024]{2,1,0:T(8,128)(2,1)S(1)}, bf16[1,176,1024]{2,1,0:T(8,128)(2,1)}, u32[]{:S(2)}) copy-start(bf16[1,176,1024]{2,1,0:T(8,128)(2,1)} %param.21) | copy-start | bytes 1081348
  57.4 167.7 %all-gather.5.cloned.1.call-start = ((), (), s32[]{:S(2)}) async-start(), calls=%async_computation.7 | async-start | bytes 12255232 | tf_op jit(solution)/shard_map/all_gather | solution.py:136
  59.1 5.0 %collective-permute-start = (bf16[176,7168]{1,0:T(8,128)(2,1)}, bf16[176,7168]{1,0:T(8,128)(2,1)S(1)}, u32[]{:S(2)}, u32[]{:S(2)}) collective-permute-start(bf16[176,7168]{1,0:T(8,128)(2,1)} %pad_maximum_fusion.1), channel_id=1, source_target_pairs={{0,1},{1,0},{2,3},{3,2},{4,5},{5,4},{6,7},{7,6},{8,9},{9,8},{10,11... | collective-permute-start | bytes 7569416 | tf_op jit(solution)/shard_map/ppermute | solution.py:70
  120.3 2.3 slice-start
  120.5 2.4 slice-start.1
  120.5 4.0 %copy-start.5 = (bf16[1280,2048]{0,1:T(8,128)(2,1)S(1)}, bf16[1280,2048]{0,1:T(8,128)(2,1)}, u32[]{:S(2)}) copy-start(bf16[1280,2048]{0,1:T(8,128)(2,1)} %all-gather.3.cloned.1.call-done) | copy-start | bytes 15728644
  231.2 12.6 %copy-start.7 = (f32[512,2]{0,1:T(2,128)S(1)}, f32[512,2]{0,1:T(2,128)}, u32[]{:S(2)}) copy-start(f32[512,2]{0,1:T(2,128)} %param.13) | copy-start | bytes 12292
  236.8 17.9 %all-to-all-start.5 = ((bf16[8,256,64]{1,2,0:T(8,128)(2,1)}), bf16[8,256,64]{1,2,0:T(8,128)(2,1)S(1)}, u32[]{:S(2)}, u32[]{:S(2)}) async-start(bf16[8,256,64]{1,2,0:T(8,128)(2,1)} %copy.110), calls=%async_computation.5 | async-start | bytes 524288 | tf_op jit(solution)/shard_map/all_to_all | solution.py:143
Sparse Core Ops, SparseCore 0:
  57.6 56.9 all-gather.2
  128.9 96.2 all-gather.4

commit v6 on v3

--- a/solution.py
+++ b/solution.py
@@ -58,8 +58,13 @@
     source_group = lax.axis_index("expert")
 
     rank_w = adapter_in[0]
-    rank_cols_w = lax.all_to_all(rank_w, "mp", split_axis=1, concat_axis=0, tiled=True)
-    down_cols_w = lax.all_to_all(down_weight[0], "mp", split_axis=1, concat_axis=0, tiled=True)
+    rank_rows_w = rank_w.shape[0]
+    both_w = jnp.concatenate([rank_w, down_weight[0]], axis=0)
+    both_cols = lax.all_to_all(both_w, "mp", split_axis=1, concat_axis=0, tiled=True).reshape(
+        n_mp, both_w.shape[0], local_feat
+    )
+    rank_cols_w = both_cols[:, :rank_rows_w].reshape(n_mp * rank_rows_w, local_feat)
+    down_cols_w = both_cols[:, rank_rows_w:].reshape(-1, local_feat)
 
     adapter_of = token_adapters(
         request_lengths, request_adapter, request_order, source_group * tok_rows, tok_rows

time: 267 us -> 275 us (1.030)
  waiting for transfers between devices: 152 us -> 183 us
  blocking collectives: 25.8 us -> 0 us
    all_to_all x1 -> x0, blocking collectives: 25.8 us -> none  [on_device(): lax.all_to_all(down_weight[0], 'mp', split_axis=1, concat_axis=0, tiled=T...]
    all_gather x1, waiting for transfers between devices: 66.8 us -> 88.7 us  [on_device(): hidden_full = lax.all_gather(hidden, 'mp', axis=1, tiled=True)]
    all_to_all x1, waiting for transfers between devices: 0.01 us -> 15.3 us  [on_device(): lax.all_to_all(both_w, 'mp', split_axis=1, concat_axis=0, tiled=True)]
    all_to_all x4 -> x0, local copies, waits for them, and re-layouts: 3.88 us -> none  [the longest x2 2.52 us: on_device(): lax.all_to_all(down_weight[0], 'mp', split_axis=1, concat_axis=0, tiled=T...]
    all_gather x1, waiting for transfers between devices: 59.1 us -> 55.5 us  [on_device(): gathered = lax.all_gather(payload2, 'mp', axis=1, tiled=True)]
    all_to_all x1, waiting for transfers between devices: 14.9 us -> 11.9 us  [on_device(): lax.all_to_all(payload.reshape(groups * chunk, local_feat), 'expert', spl...]
  transfers between devices with their start and end apart: 5 -> 5, of which waited for: 4 -> 5; matrix products, arithmetic and copies ran while one was open for 4% -> 3% of each run, Pallas kernels for 0% -> 0%
where the time goes in v6:
time: 275 us
  waiting for transfers between devices  183 us (67%)
  matrix products  26.5 us (10%)
  starting transfers between devices  24.4 us (9%)
  local copies, waits for them, and re-layouts  15.1 us (5%)
  between operations  13.8 us (5%)
  other arithmetic  12 us (4%)
    all_gather x1, waiting for transfers between devices, on_device(): hidden_full = lax.all_gather(hidden, 'mp', axis=1, tiled=True)  88.7 us
    all_gather x1, waiting for transfers between devices, on_device(): gathered = lax.all_gather(payload2, 'mp', axis=1, tiled=True)  55.5 us
    all_to_all x1, waiting for transfers between devices, on_device(): lax.all_to_all(both_w, 'mp', split_axis=1, concat_axis=0, tiled=True)  15.3 us
    dot_general x4, matrix products, contract_last(): lax.dot_general(left, right, (((1,), (1,)), ((), ())), preferred_element_...  14.7 us
    all_to_all x1, waiting for transfers between devices, on_device(): lax.all_to_all(payload.reshape(groups * chunk, local_feat), 'expert', spl...  11.9 us
    all_to_all x1, waiting for transfers between devices, on_device(): lax.all_to_all(down_local, 'expert', split_axis=0, concat_axis=0, tiled=T...  11.3 us
    dot_general x1, matrix products, on_device(): jnp.dot(hidden_full, down_cols_w, preferred_element_type=jnp.float32)  9.78 us
    all_to_all x1, starting transfers between devices, on_device(): lax.all_to_all(payload.reshape(groups * chunk, local_feat), 'expert', spl...  9 us
  transfers between devices with their start and end apart: 5, of which 5 were waited for; matrix products, arithmetic and copies ran while one was open for 3% of the time, Pallas kernels for 0%

profile of v6, /device:TPU:1, one launch (start us, length us, event | category | flops | bytes accessed | tf_op | source)
XLA Modules:
  0.0 274.5 jit_solution(14698951272577677527)
XLA Ops:
  6.5 0.9 copy.93
  7.8 0.9 select_reduce_fusion.2
  9.2 2.3 reduce-window.18
  12.3 0.7 compare_select_fusion
  13.0 0.9 fusion.5
  14.2 1.1 fusion.11
  15.3 0.8 pad_maximum_fusion.1
  16.1 9.0 %all-to-all-start = ((bf16[8,260,64]{1,2,0:T(8,128)(2,1)}), bf16[8,260,64]{1,2,0:T(8,128)(2,1)S(1)}, u32[]{:S(2)}, u32[]{:S(2)}) async-start(bf16[8,260,64]{1,2,0:T(8,128)(2,1)} %pad_maximum_fusion.1), calls=%async_computation | async-start | bytes 786432 | tf_op jit(solution)/shard_map/all_to_all | solution.py:89
  25.1 0.5 copy.101
  25.9 1.6 pad_maximum_fusion
  27.5 11.9 %all-to-all-done = bf16[8,260,64]{1,2,0:T(8,128)(2,1)S(1)} async-done(((bf16[8,260,64]{1,2,0:T(8,128)(2,1)}), bf16[8,260,64]{1,2,0:T(8,128)(2,1)S(1)}, u32[]{:S(2)}, u32[]{:S(2)}) %all-to-all-start) | async-done | bytes 266272 | tf_op jit(solution)/shard_map/all_to_all | solution.py:89
  39.4 8.4 %all-to-all-start.1 = ((bf16[208,32,64]{0,2,1:T(8,128)(2,1)}), bf16[208,32,64]{0,2,1:T(8,128)(2,1)S(1)}, u32[]{:S(2)}, u32[]{:S(2)}) async-start(bf16[208,32,64]{0,2,1:T(8,128)(2,1)} %pad_maximum_fusion), calls=%async_computation.1 | async-start | bytes 2097152 | tf_op jit(solution)/shard_map/all_to_all | solution.py:63
  48.6 0.9 fusion.24
  49.4 15.3 %all-to-all-done.1 = bf16[208,32,64]{0,2,1:T(8,128)(2,1)S(1)} async-done(((bf16[208,32,64]{0,2,1:T(8,128)(2,1)}), bf16[208,32,64]{0,2,1:T(8,128)(2,1)S(1)}, u32[]{:S(2)}, u32[]{:S(2)}) %all-to-all-start.1) | async-done | bytes 852000 | tf_op jit(solution)/shard_map/all_to_all | solution.py:63
  65.1 2.3 multiply_reduce_fusion
  68.1 0.8 pad_maximum_fusion.2
  69.1 55.5 %all-gather.3.cloned.1.call-done = bf16[2560,2048]{0,1:T(8,128)(2,1)} async-done(((bf16[2560,64]{0,1:T(8,128)(2,1)}), bf16[2560,2048]{0,1:T(8,128)(2,1)}) %all-gather.3.cloned.1.call-update) | async-done | bytes 10485776 | tf_op jit(solution)/shard_map/all_gather | solution.py:105
  124.7 1.6 slice-done
  127.5 5.1 %fusion.2 = f32[2048,176]{0,1:T(8,128)S(1)} fusion(bf16[2560,2048]{0,1:T(8,128)(2,1)} %all-gather.3.cloned.1.call-done, bf16[1,176,2048]{2,1,0:T(8,128)(2,1)S(1)} %copy-done), kind=kOutput, calls=%fused_computation.4 | convolution fusion | flops 1476395008 | bytes 10551296 | tf_op jit(solution)/shard_map/dot_general | solution.py:35
  132.6 5.1 %fusion = f32[2048,176]{0,1:T(8,128)S(1)} fusion(bf16[2560,2048]{0,1:T(8,128)(2,1)} %all-gather.3.cloned.1.call-done, bf16[1,176,2048]{2,1,0:T(8,128)(2,1)S(1)} %copy-done.6), kind=kOutput, calls=%fused_computation.2 | convolution fusion | flops 1476395008 | bytes 10551296 | tf_op jit(solution)/shard_map/dot_general | solution.py:35
  137.8 2.1 fusion.10
  139.9 0.4 slice.42
  140.4 0.6 copy.110
  141.0 1.9 reshape.169
  142.9 88.7 %all-gather.5.cloned.1.call-done = bf16[2048,5632]{0,1:T(8,128)(2,1)} async-done(((bf16[2048,176]{0,1:T(8,128)(2,1)}), bf16[2048,5632]{0,1:T(8,128)(2,1)}) %all-gather.5.cloned.1.call-update) | async-done | bytes 23068688 | tf_op jit(solution)/shard_map/all_gather | solution.py:121
  231.6 9.8 %convolution_convert_fusion = bf16[2048,64]{0,1:T(8,128)(2,1)S(1)} fusion(bf16[5632,64]{0,1:T(8,128)(2,1)S(1)} %reshape.169, bf16[2048,5632]{0,1:T(8,128)(2,1)} %all-gather.5.cloned.1.call-done), kind=kOutput, calls=%fused_computation.14 | convolution fusion | flops 1476526080 | bytes 24051712 | tf_op jit(solution)/shard_map/dot_general | solution.py:122
  241.4 0.7 copy.125
  242.1 6.7 %all-to-all-start.2 = ((bf16[8,256,64]{1,2,0:T(8,128)(2,1)}), bf16[8,256,64]{1,2,0:T(8,128)(2,1)S(1)}, u32[]{:S(2)}, u32[]{:S(2)}) async-start(bf16[8,256,64]{1,2,0:T(8,128)(2,1)} %bitcast.59), calls=%async_computation.2 | async-start | bytes 524288 | tf_op jit(solution)/shard_map/all_to_all | solution.py:125
  249.3 11.3 %all-to-all-done.2 = bf16[8,256,64]{1,2,0:T(8,128)(2,1)S(1)} async-done(((bf16[8,256,64]{1,2,0:T(8,128)(2,1)}), bf16[8,256,64]{1,2,0:T(8,128)(2,1)S(1)}, u32[]{:S(2)}, u32[]{:S(2)}) %all-to-all-start.2) | async-done | bytes 262176 | tf_op jit(solution)/shard_map/all_to_all | solution.py:125
  260.9 3.2 %gather_fusion = bf16[1024,64]{1,0:T(8,128)(2,1)S(1)} fusion(bf16[2048,64]{1,0:T(8,128)(2,1)S(1)} %bitcast.62, s32[1024]{0:T(1024)S(1)} %broadcast_clamp_fusion), kind=kCustom, calls=%fused_computation | custom fusion | bytes 266240 | tf_op jit(solution)/shard_map/gather | solution.py:126
  264.1 2.8 %fusion.20 = bf16[512,64]{1,0:T(8,128)(2,1)S(1)} fusion(bf16[512,2,64]{2,1,0:T(2,128)(2,1)S(1)} %bitcast.70, f32[512,2]{1,0:T(8,128)S(1)} %copy.92), kind=kLoop, calls=%fused_computation.25 | loop fusion | flops 163840 | bytes 200704 | tf_op jit(solution)/shard_map/reduce_sum | solution.py:127
  267.0 0.7 copy.114
  (70 shorter events, 6.1 us)
Async XLA Ops:
  6.5 120.9 %copy-start = (bf16[1,176,2048]{2,1,0:T(8,128)(2,1)S(1)}, bf16[1,176,2048]{2,1,0:T(8,128)(2,1)}, u32[]{:S(2)}) copy-start(bf16[1,176,2048]{2,1,0:T(8,128)(2,1)} %param.18) | copy-start | bytes 2162692
  6.5 7.7 %copy-start.8 = (bf16[512,64]{0,1:T(8,128)(2,1)S(1)}, bf16[512,64]{0,1:T(8,128)(2,1)}, u32[]{:S(2)}) copy-start(bf16[512,64]{0,1:T(8,128)(2,1)} %param.11) | copy-start | bytes 196612
  13.0 12.1 %copy-start.3 = (bf16[1,176,2048]{2,1,0:T(8,128)(2,1)S(1)}, bf16[1,176,2048]{2,1,0:T(8,128)(2,1)}, u32[]{:S(2)}) copy-start(bf16[1,176,2048]{2,1,0:T(8,128)(2,1)} %param.19) | copy-start | bytes 2162692
  14.0 11.7 %copy-start.4 = (bf16[1,32,2048]{2,1,0:T(8,128)(2,1)S(1)}, bf16[1,32,2048]{2,1,0:T(8,128)(2,1)}, u32[]{:S(2)}) copy-start(bf16[1,32,2048]{2,1,0:T(8,128)(2,1)} %param.20) | copy-start | bytes 393220
  16.1 23.3 %all-to-all-start = ((bf16[8,260,64]{1,2,0:T(8,128)(2,1)}), bf16[8,260,64]{1,2,0:T(8,128)(2,1)S(1)}, u32[]{:S(2)}, u32[]{:S(2)}) async-start(bf16[8,260,64]{1,2,0:T(8,128)(2,1)} %pad_maximum_fusion.1), calls=%async_computation | async-start | bytes 786432 | tf_op jit(solution)/shard_map/all_to_all | solution.py:89
  39.4 25.4 %all-to-all-start.1 = ((bf16[208,32,64]{0,2,1:T(8,128)(2,1)}), bf16[208,32,64]{0,2,1:T(8,128)(2,1)S(1)}, u32[]{:S(2)}, u32[]{:S(2)}) async-start(bf16[208,32,64]{0,2,1:T(8,128)(2,1)} %pad_maximum_fusion), calls=%async_computation.1 | async-start | bytes 2097152 | tf_op jit(solution)/shard_map/all_to_all | solution.py:63
  47.9 76.8 %all-gather.3.cloned.1.call-start = ((), (), s32[]{:S(2)}) async-start(), calls=%async_computation.3 | async-start | bytes 10813440 | tf_op jit(solution)/shard_map/all_gather | solution.py:105
  64.8 2.7 copy-start.1
  68.9 162.7 %all-gather.5.cloned.1.call-start = ((), (), s32[]{:S(2)}) async-start(), calls=%async_computation.4 | async-start | bytes 23789568 | tf_op jit(solution)/shard_map/all_gather | solution.py:121
  124.7 1.6 slice-start
  127.5 5.1 %copy-start.6 = (bf16[1,176,2048]{2,1,0:T(8,128)(2,1)S(1)}, bf16[1,176,2048]{2,1,0:T(8,128)(2,1)}, u32[]{:S(2)}) copy-start(bf16[1,176,2048]{2,1,0:T(8,128)(2,1)} %param.17) | copy-start | bytes 2162692
  132.6 5.1 %copy-start.7 = (bf16[1,176,1024]{2,1,0:T(8,128)(2,1)S(1)}, bf16[1,176,1024]{2,1,0:T(8,128)(2,1)}, u32[]{:S(2)}) copy-start(bf16[1,176,1024]{2,1,0:T(8,128)(2,1)} %param.21) | copy-start | bytes 1081348
  137.8 2.2 copy-start.2
  142.9 106.3 %copy-start.5 = (f32[512,2]{0,1:T(2,128)S(1)}, f32[512,2]{0,1:T(2,128)}, u32[]{:S(2)}) copy-start(f32[512,2]{0,1:T(2,128)} %param.13) | copy-start | bytes 12292
  242.1 18.5 %all-to-all-start.2 = ((bf16[8,256,64]{1,2,0:T(8,128)(2,1)}), bf16[8,256,64]{1,2,0:T(8,128)(2,1)S(1)}, u32[]{:S(2)}, u32[]{:S(2)}) async-start(bf16[8,256,64]{1,2,0:T(8,128)(2,1)} %bitcast.59), calls=%async_computation.2 | async-start | bytes 524288 | tf_op jit(solution)/shard_map/all_to_all | solution.py:125
Sparse Core Ops, SparseCore 0:
  69.0 55.6 all-gather.2
  140.0 91.5 all-gather.4

commit v7 on v3

--- a/solution.py
+++ b/solution.py
@@ -5,6 +5,7 @@
 
 RANK = 16
 ADAPTERS = 64
+USED = 16
 
 
 def token_adapters(request_lengths, request_adapter, request_order, first_token, token_count):
@@ -57,8 +58,6 @@
     total_slots = groups * capacity
     source_group = lax.axis_index("expert")
 
-    rank_w = adapter_in[0]
-    rank_cols_w = lax.all_to_all(rank_w, "mp", split_axis=1, concat_axis=0, tiled=True)
     down_cols_w = lax.all_to_all(down_weight[0], "mp", split_axis=1, concat_axis=0, tiled=True)
 
     adapter_of = token_adapters(
@@ -88,35 +87,43 @@
     arrived_adapter = received[:, capacity:].reshape(total_slots).astype(jnp.int32)
     row_count = arrived_local.shape[0]
 
-    part_all = contract_last(arrived_local, rank_cols_w)
-    pick = (arrived_adapter[:, None] == jnp.arange(ADAPTERS, dtype=jnp.int32)[None, :]).astype(
+    rank_w = adapter_in[0]
+    payload2 = jnp.concatenate([jnp.transpose(arrived_local), rank_w], axis=0)
+    gathered = lax.all_gather(payload2, "mp", axis=0, tiled=False)
+    arrived_t = gathered[:, :local_feat].reshape(n_mp * local_feat, row_count)
+    rank_all_w = gathered[:, local_feat:].reshape(ADAPTERS, RANK, -1)
+
+    adapter_ids = jnp.arange(ADAPTERS, dtype=jnp.int32)
+    present = jnp.any(request_adapter[:, None] == adapter_ids[None, :], axis=0)
+    order = jnp.cumsum(present.astype(jnp.int32)) - 1
+    used_count = USED
+    used_pick = (
+        present[None, :] & (order[None, :] == jnp.arange(used_count, dtype=jnp.int32)[:, None])
+    ).astype(tokens.dtype)
+    used_w = jnp.einsum(
+        "ia,akf->ikf", used_pick, rank_all_w, preferred_element_type=jnp.float32
+    ).astype(tokens.dtype).reshape(used_count * RANK, -1)
+    rank_used = lax.dot_general(
+        arrived_t, used_w, (((0,), (1,)), ((), ())), preferred_element_type=jnp.float32
+    )
+    slot_order = jnp.where(arrived_adapter >= 0, order[jnp.clip(arrived_adapter, 0, ADAPTERS - 1)], -1)
+    slot_pick = (slot_order[:, None] == jnp.arange(used_count, dtype=jnp.int32)[None, :]).astype(
         jnp.float32
     )
-    part_rank = jnp.sum(part_all.reshape(row_count, ADAPTERS, RANK) * pick[:, :, None], axis=1)
-    part_rows = row_count * RANK // local_feat
-    payload2 = jnp.concatenate(
-        [arrived_local, part_rank.astype(tokens.dtype).reshape(part_rows, local_feat)], axis=0
-    )
-    gathered = lax.all_gather(payload2, "mp", axis=1, tiled=True)
-    arrived = gathered[:row_count]
-    rank = (
-        jnp.sum(
-            gathered[row_count:].reshape(part_rows, n_mp, local_feat).astype(jnp.float32), axis=1
-        )
-        .reshape(row_count, RANK)
-        .astype(jnp.bfloat16)
-    )
+    rank = jnp.sum(
+        rank_used.reshape(row_count, used_count, RANK) * slot_pick[:, :, None], axis=1
+    ).astype(jnp.bfloat16)
 
-    gate_pre = contract_last(arrived, gate_weight[0])
-    up_base = contract_last(arrived, up_weight[0])
-    chosen = pick.astype(jnp.bfloat16)
+    gate_pre = jnp.dot(gate_weight[0], arrived_t, preferred_element_type=jnp.float32)
+    up_base = jnp.dot(up_weight[0], arrived_t, preferred_element_type=jnp.float32)
+    chosen = (arrived_adapter[:, None] == adapter_ids[None, :]).astype(jnp.bfloat16)
     expanded = (rank[:, None, :] * chosen[:, :, None]).reshape(row_count, ADAPTERS * RANK)
-    up = up_base + contract_last(expanded, adapter_out[0])
+    up = up_base + contract_last(adapter_out[0], expanded)
     hidden = (jax.nn.silu(gate_pre) * up).astype(jnp.bfloat16)
-    hidden_full = lax.all_gather(hidden, "mp", axis=1, tiled=True)
-    down_local = jnp.dot(hidden_full, down_cols_w, preferred_element_type=jnp.float32).astype(
-        jnp.bfloat16
-    )
+    hidden_full = lax.all_gather(hidden, "mp", axis=0, tiled=True)
+    down_local = lax.dot_general(
+        hidden_full, down_cols_w, (((0,), (0,)), ((), ())), preferred_element_type=jnp.float32
+    ).astype(jnp.bfloat16)
     returned_rows = lax.all_to_all(down_local, "expert", split_axis=0, concat_axis=0, tiled=True)
     picked = returned_rows[slot_index].astype(jnp.float32)
     mixed = jnp.sum(route_gate[:, :, None] * picked, axis=1)

time: 267 us -> 273 us (1.022)
  waiting for transfers between devices: 152 us -> 99.6 us
  other arithmetic: 9.58 us -> 49.8 us
  blocking collectives: 25.8 us -> 48.2 us
  starting transfers between devices: 23.8 us -> 6.96 us
  local copies, waits for them, and re-layouts: 16.4 us -> 25.8 us
    all_gather x2, waiting for transfers between devices: 126 us -> 88.3 us  [the longest x1 66.8 us: on_device(): hidden_full = lax.all_gather(hidden, 'mp', axis=0, tiled=True)]
    select_n x0 -> x1, other arithmetic: none -> 35.1 us  [on_device(): jnp.where(arrived_adapter >= 0, order[jnp.clip(arrived_adapter, 0, ADAPTE...]
    all_to_all x0 -> x1, blocking collectives: none -> 22.4 us  [on_device(): lax.all_to_all(payload.reshape(groups * chunk, local_feat), 'expert', spl...]
    all_to_all x2 -> x0, starting transfers between devices: 16.8 us -> none  [the longest x1 8.58 us: on_device(): lax.all_to_all(rank_w, 'mp', split_axis=1, concat_axis=0, tiled=True)]
    all_to_all x2 -> x0, waiting for transfers between devices: 14.9 us -> none  [the longest x1 14.9 us: on_device(): lax.all_to_all(payload.reshape(groups * chunk, local_feat), 'expert', spl...]
    dot_general x1 -> x5, matrix products: 9.78 us -> 23.9 us  [the longest x1 9.85 us: on_device(): lax.dot_general(hidden_full, down_cols_w, (((0,), (0,)), ((), ())), prefe...]
    dot_general x4 -> x1, matrix products: 13.7 us -> 2.15 us  [contract_last(): lax.dot_general(left, right, (((1,), (1,)), ((), ())), preferred_element_...]
    slice x4 -> x3, local copies, waits for them, and re-layouts: 2.02 us -> 11 us  [the longest x1 8.25 us: on_device(): arrived_t = gathered[:, :local_feat].reshape(n_mp * local_feat, row_count)]
  transfers between devices with their start and end apart: 5 -> 3, of which waited for: 4 -> 3; matrix products, arithmetic and copies ran while one was open for 4% -> 17% of each run, Pallas kernels for 0% -> 0%
where the time goes in v7:
time: 273 us; the launch traced here: 272 us
  waiting for transfers between devices  99.6 us (36%)
  other arithmetic  49.8 us (18%)
  blocking collectives  48.2 us (18%)
  matrix products  28.1 us (10%)
  local copies, waits for them, and re-layouts  25.8 us (9%)
  between operations  13.7 us (5%)
  starting transfers between devices  6.96 us (3%)
    all_gather x1, waiting for transfers between devices, on_device(): hidden_full = lax.all_gather(hidden, 'mp', axis=0, tiled=True)  66.8 us
    select_n x1, other arithmetic, on_device(): jnp.where(arrived_adapter >= 0, order[jnp.clip(arrived_adapter, 0, ADAPTE...  35.1 us
    all_to_all x1, blocking collectives, on_device(): lax.all_to_all(down_weight[0], 'mp', split_axis=1, concat_axis=0, tiled=T...  25.8 us
    all_to_all x1, blocking collectives, on_device(): lax.all_to_all(payload.reshape(groups * chunk, local_feat), 'expert', spl...  22.4 us
    all_gather x1, waiting for transfers between devices, on_device(): gathered = lax.all_gather(payload2, 'mp', axis=0, tiled=False)  21.6 us
    all_to_all x1, waiting for transfers between devices, on_device(): lax.all_to_all(down_local, 'expert', split_axis=0, concat_axis=0, tiled=T...  11.3 us
    dot_general x1, matrix products, on_device(): lax.dot_general(hidden_full, down_cols_w, (((0,), (0,)), ((), ())), prefe...  9.85 us
    slice x1, local copies, waits for them, and re-layouts, on_device(): arrived_t = gathered[:, :local_feat].reshape(n_mp * local_feat, row_count)  8.25 us
  transfers between devices with their start and end apart: 3, of which 3 were waited for; matrix products, arithmetic and copies ran while one was open for 17% of the time, Pallas kernels for 0%

profile of v7, /device:TPU:1, one launch (start us, length us, event | category | flops | bytes accessed | tf_op | source)
XLA Modules:
  0.0 272.2 jit_solution(12056037890208920808)
XLA Ops:
  6.5 0.9 copy.114
  7.8 2.3 reduce-window.25
  10.9 0.7 compare_select_fusion.7
  11.7 0.9 select_reduce_fusion.2
  13.0 0.9 fusion.3
  14.2 1.1 fusion.13
  15.4 22.4 %all_to_all.37 = bf16[8,260,64]{1,2,0:T(8,128)(2,1)S(1)} all-to-all(bf16[8,260,64]{1,2,0:T(8,128)(2,1)S(1)} %pad_maximum_fusion), channel_id=1, replica_groups=mesh['expert'=8,'mp'=32] {'expert'}, dimensions={0} | all-to-all | bytes 532480 | tf_op jit(solution)/shard_map/all_to_all | solution.py:83
  37.8 0.8 pad_maximum_fusion.1
  39.9 0.7 fusion.40
  40.6 0.7 fusion.42
  41.2 0.7 fusion.41
  42.3 4.3 %compare_select_fusion.1 = (s32[2048,1]{0,1:T(1,128)S(1)}, s32[2048,1]{0,1:T(1,128)S(1)}) fusion(s32[]{:T(128)} %bitcast.73, s32[]{:T(128)} %bitcast.74, s32[]{:T(128)} %bitcast.75, s32[]{:T(128)} %bitcast.76, s32[]{:T(128)} %bitcast.77, s32[]{:T(128)} %bitcast.79, s32[]{:T(128)} %bitcast.78, s32[2048,1]{0,1:T(1,128)S(1)} %min.12), kind=kLoop, calls=%fused_computation.109 | loop fusion | flops 30720 | bytes 24604 | tf_op jit(solution)/shard_map/gather | solution.py:109
  46.6 1.4 compare_reduce_fusion.56
  48.0 35.1 %select_select_fusion = s32[2048]{0:T(1024)S(1)} fusion(pred[2048]{0:T(1024)(128)(4,1)S(1)} %get-tuple-element.61, pred[2048]{0:T(1024)(128)(4,1)S(1)} %get-tuple-element.60, pred[2048]{0:T(1024)(128)(4,1)S(1)} %get-tuple-element.59, pred[2048]{0:T(1024)(128)(4,1)S(1)} %get-tuple-element.58, pred[2048]{0:T(1024)(128)(4,1)S(1)} %get-tuple-element.57, ...), kind=kLoop, calls=%fused_computation.122 | loop fusion | flops 120832 | bytes 141540 | tf_op jit(solution)/shard_map/jit(_where)/select_n | solution.py:109
  83.3 21.6 %all-gather.6.cloned.1.call-done = bf16[3072,2048]{1,0:T(8,128)(2,1)} async-done(((bf16[96,2048]{1,0:T(8,128)(2,1)}), bf16[3072,2048]{1,0:T(8,128)(2,1)}) %all-gather.6.cloned.1.call-update) | async-done | bytes 12582928 | tf_op jit(solution)/shard_map/all_gather | solution.py:92
  104.8 2.5 slice.169
  107.3 8.2 %slice.168 = bf16[32,64,2048]{2,1,0:T(8,128)(2,1)} slice(bf16[32,96,2048]{2,1,0:T(8,128)(2,1)} %bitcast.148), slice={[0:32], [0:64], [0:2048]} | slice | bytes 16777216 | tf_op jit(solution)/shard_map/slice | solution.py:93
  115.6 5.2 %convolution_bitcast_fusion = f32[176,2048]{1,0:T(8,128)S(1)} fusion(bf16[2048,2048]{1,0:T(8,128)(2,1)} %bitcast.149, bf16[1,176,2048]{2,1,0:T(8,128)(2,1)S(1)} %copy-done), kind=kOutput, calls=%fused_computation.13 | convolution fusion | flops 1476395008 | bytes 10551296 | tf_op jit(solution)/shard_map/dot_general | solution.py:117
  121.5 1.7 fusion.22
  123.2 4.5 %fusion.7 = bf16[16,16,2048]{2,0,1:T(8,128)(2,1)S(1)} fusion(bf16[64,16,2048]{2,1,0:T(8,128)(2,1)S(1)} %bitcast.145, s32[64]{0:T(128)S(1)} %get-tuple-element.133, pred[64]{0:T(512)(128)(4,1)S(1)} %fusion.33), kind=kOutput, calls=%fused_computation.9 | convolution fusion | flops 67635200 | bytes 5243200 | tf_op jit(solution)/shard_map/ia,akf->ikf/dot_general | solution.py:103
  127.7 2.7 fusion.20
  131.4 2.1 fusion.12
  134.1 25.8 %all_to_all.38 = bf16[176,32,64]{0,2,1:T(8,128)(2,1)S(1)} all-to-all(bf16[176,32,64]{0,2,1:T(8,128)(2,1)S(1)} %bitcast.152), channel_id=1, replica_groups=mesh['expert'=8,'mp'=32] {'mp'}, dimensions={1} | all-to-all | bytes 1441792 | tf_op jit(solution)/shard_map/all_to_all | solution.py:61
  160.5 1.9 all_to_all.30
  162.4 66.8 %all-gather.4.cloned.1.call-done = bf16[5632,2048]{1,0:T(8,128)(2,1)} async-done(((bf16[176,2048]{1,0:T(8,128)(2,1)}), bf16[5632,2048]{1,0:T(8,128)(2,1)}) %all-gather.4.cloned.1.call-update) | async-done | bytes 23068688 | tf_op jit(solution)/shard_map/all_gather | solution.py:123
  229.2 9.9 %convolution_convert_fusion = bf16[2048,64]{0,1:T(8,128)(2,1)S(1)} fusion(bf16[5632,64]{0,1:T(8,128)(2,1)S(1)} %all_to_all.30, bf16[5632,2048]{1,0:T(8,128)(2,1)} %all-gather.4.cloned.1.call-done), kind=kOutput, calls=%fused_computation.15 | convolution fusion | flops 1476526080 | bytes 24051712 | tf_op jit(solution)/shard_map/dot_general | solution.py:124
  239.0 0.7 copy.147
  239.7 6.7 %all-to-all-start.2 = ((bf16[8,256,64]{1,2,0:T(8,128)(2,1)}), bf16[8,256,64]{1,2,0:T(8,128)(2,1)S(1)}, u32[]{:S(2)}, u32[]{:S(2)}) async-start(bf16[8,256,64]{1,2,0:T(8,128)(2,1)} %bitcast.142), calls=%async_computation.2 | async-start | bytes 524288 | tf_op jit(solution)/shard_map/all_to_all | solution.py:127
  247.0 11.3 %all-to-all-done.2 = bf16[8,256,64]{1,2,0:T(8,128)(2,1)S(1)} async-done(((bf16[8,256,64]{1,2,0:T(8,128)(2,1)}), bf16[8,256,64]{1,2,0:T(8,128)(2,1)S(1)}, u32[]{:S(2)}, u32[]{:S(2)}) %all-to-all-start.2) | async-done | bytes 262176 | tf_op jit(solution)/shard_map/all_to_all | solution.py:127
  258.6 3.2 %gather_fusion = bf16[1024,64]{1,0:T(8,128)(2,1)S(1)} fusion(bf16[2048,64]{1,0:T(8,128)(2,1)S(1)} %bitcast.146, s32[1024]{0:T(1024)S(1)} %broadcast_clamp_fusion.1), kind=kCustom, calls=%fused_computation | custom fusion | bytes 266240 | tf_op jit(solution)/shard_map/gather | solution.py:128
  261.8 2.8 %fusion.25 = bf16[512,64]{1,0:T(8,128)(2,1)S(1)} fusion(bf16[512,2,64]{2,1,0:T(2,128)(2,1)S(1)} %bitcast.156, f32[512,2]{1,0:T(8,128)S(1)} %copy.113), kind=kLoop, calls=%fused_computation.28 | loop fusion | flops 163840 | bytes 200704 | tf_op jit(solution)/shard_map/reduce_sum | solution.py:129
  264.6 0.7 copy.132
  (73 shorter events, 7.2 us)
Async XLA Ops:
  6.5 109.0 %copy-start = (bf16[1,176,2048]{2,1,0:T(8,128)(2,1)S(1)}, bf16[1,176,2048]{2,1,0:T(8,128)(2,1)}, u32[]{:S(2)}) copy-start(bf16[1,176,2048]{2,1,0:T(8,128)(2,1)} %param.17) | copy-start | bytes 2162692
  6.5 7.7 %copy-start.9 = (bf16[512,64]{0,1:T(8,128)(2,1)S(1)}, bf16[512,64]{0,1:T(8,128)(2,1)}, u32[]{:S(2)}) copy-start(bf16[512,64]{0,1:T(8,128)(2,1)} %param.11) | copy-start | bytes 196612
  6.5 98.3 %all-gather.6.cloned.1.call-start = ((), (), s32[]{:S(2)}) async-start(), calls=%async_computation.4 | async-start | bytes 12976128 | tf_op jit(solution)/shard_map/all_gather | solution.py:92
  13.0 24.8 %copy-start.4 = (bf16[1,32,2048]{2,1,0:T(8,128)(2,1)S(1)}, bf16[1,32,2048]{2,1,0:T(8,128)(2,1)}, u32[]{:S(2)}) copy-start(bf16[1,32,2048]{2,1,0:T(8,128)(2,1)} %param.20) | copy-start | bytes 393220
  14.0 24.9 %copy-start.6 = (s32[32]{0:T(128)S(1)}, s32[32]{0:T(128)}, u32[]{:S(2)}) copy-start(s32[32]{0:T(128)} %param.15) | copy-start | bytes 388
  38.7 190.5 %all-gather.4.cloned.1.call-start = ((), (), s32[]{:S(2)}) async-start(), calls=%async_computation.3 | async-start | bytes 23789568 | tf_op jit(solution)/shard_map/all_gather | solution.py:123
  115.6 5.8 %copy-start.2 = (bf16[32,64,2048]{2,1,0:T(8,128)(2,1)S(1)}, bf16[32,64,2048]{2,1,0:T(8,128)(2,1)}, u32[]{:S(2)}) copy-start(bf16[32,64,2048]{2,1,0:T(8,128)(2,1)} %slice.168) | copy-start | bytes 25165828
  115.6 5.9 %copy-start.7 = (bf16[1,176,2048]{2,1,0:T(8,128)(2,1)S(1)}, bf16[1,176,2048]{2,1,0:T(8,128)(2,1)}, u32[]{:S(2)}) copy-start(bf16[1,176,2048]{2,1,0:T(8,128)(2,1)} %param.18) | copy-start | bytes 2162692
  130.4 1.0 copy-start.8
  131.4 2.2 copy-start.3
  162.4 84.4 %copy-start.5 = (f32[512,2]{0,1:T(2,128)S(1)}, f32[512,2]{0,1:T(2,128)}, u32[]{:S(2)}) copy-start(f32[512,2]{0,1:T(2,128)} %param.13) | copy-start | bytes 12292
  229.2 36.2 %copy-start.1 = (bf16[1,176,2048]{2,1,0:T(8,128)(2,1)S(1)}, bf16[1,176,2048]{2,1,0:T(8,128)(2,1)}, u32[]{:S(2)}) copy-start(bf16[1,176,2048]{2,1,0:T(8,128)(2,1)} %param.17) | copy-start | bytes 2162692
  239.7 18.5 %all-to-all-start.2 = ((bf16[8,256,64]{1,2,0:T(8,128)(2,1)}), bf16[8,256,64]{1,2,0:T(8,128)(2,1)S(1)}, u32[]{:S(2)}, u32[]{:S(2)}) async-start(bf16[8,256,64]{1,2,0:T(8,128)(2,1)} %bitcast.142), calls=%async_computation.2 | async-start | bytes 524288 | tf_op jit(solution)/shard_map/all_to_all | solution.py:127
Sparse Core Ops, SparseCore 0:
  38.8 65.9 all-gather.5
  133.7 95.4 all-gather.3

commit v8 on v7

--- a/solution.py
+++ b/solution.py
@@ -90,33 +90,50 @@
     rank_w = adapter_in[0]
     payload2 = jnp.concatenate([jnp.transpose(arrived_local), rank_w], axis=0)
     gathered = lax.all_gather(payload2, "mp", axis=0, tiled=False)
-    arrived_t = gathered[:, :local_feat].reshape(n_mp * local_feat, row_count)
-    rank_all_w = gathered[:, local_feat:].reshape(ADAPTERS, RANK, -1)
+    block = gathered.shape[1]
+    flat = gathered.reshape(n_mp * block, row_count)
+    pad = block - local_feat
+
+    def padded(w):
+        lead = w.shape[0]
+        return jnp.concatenate(
+            [w.reshape(lead, n_mp, local_feat), jnp.zeros((lead, n_mp, pad), w.dtype)], axis=2
+        ).reshape(lead, n_mp * block)
 
     adapter_ids = jnp.arange(ADAPTERS, dtype=jnp.int32)
     present = jnp.any(request_adapter[:, None] == adapter_ids[None, :], axis=0)
     order = jnp.cumsum(present.astype(jnp.int32)) - 1
-    used_count = USED
     used_pick = (
-        present[None, :] & (order[None, :] == jnp.arange(used_count, dtype=jnp.int32)[:, None])
+        present[None, :] & (order[None, :] == jnp.arange(USED, dtype=jnp.int32)[:, None])
     ).astype(tokens.dtype)
+    groups_per_block = block // RANK
+    first_adapter_group = local_feat // RANK
+    sel = jnp.concatenate(
+        [
+            jnp.zeros((USED, n_mp, first_adapter_group), tokens.dtype),
+            used_pick.reshape(USED, n_mp, groups_per_block - first_adapter_group),
+        ],
+        axis=2,
+    )
     used_w = jnp.einsum(
-        "ia,akf->ikf", used_pick, rank_all_w, preferred_element_type=jnp.float32
-    ).astype(tokens.dtype).reshape(used_count * RANK, -1)
+        "ijg,jgkf->ikf",
+        sel,
+        gathered.reshape(n_mp, groups_per_block, RANK, row_count),
+        preferred_element_type=jnp.float32,
+    ).astype(tokens.dtype).reshape(USED * RANK, -1)
     rank_used = lax.dot_general(
-        arrived_t, used_w, (((0,), (1,)), ((), ())), preferred_element_type=jnp.float32
+        flat, padded(used_w), (((0,), (1,)), ((), ())), preferred_element_type=jnp.float32
     )
-    slot_order = jnp.where(arrived_adapter >= 0, order[jnp.clip(arrived_adapter, 0, ADAPTERS - 1)], -1)
-    slot_pick = (slot_order[:, None] == jnp.arange(used_count, dtype=jnp.int32)[None, :]).astype(
-        jnp.float32
+    chosen = (arrived_adapter[:, None] == adapter_ids[None, :]).astype(jnp.bfloat16)
+    slot_pick = lax.dot_general(
+        chosen, used_pick, (((1,), (1,)), ((), ())), preferred_element_type=jnp.float32
     )
     rank = jnp.sum(
-        rank_used.reshape(row_count, used_count, RANK) * slot_pick[:, :, None], axis=1
+        rank_used.reshape(row_count, USED, RANK) * slot_pick[:, :, None], axis=1
     ).astype(jnp.bfloat16)
 
-    gate_pre = jnp.dot(gate_weight[0], arrived_t, preferred_element_type=jnp.float32)
-    up_base = jnp.dot(up_weight[0], arrived_t, preferred_element_type=jnp.float32)
-    chosen = (arrived_adapter[:, None] == adapter_ids[None, :]).astype(jnp.bfloat16)
+    gate_pre = jnp.dot(padded(gate_weight[0]), flat, preferred_element_type=jnp.float32)
+    up_base = jnp.dot(padded(up_weight[0]), flat, preferred_element_type=jnp.float32)
     expanded = (rank[:, None, :] * chosen[:, :, None]).reshape(row_count, ADAPTERS * RANK)
     up = up_base + contract_last(adapter_out[0], expanded)
     hidden = (jax.nn.silu(gate_pre) * up).astype(jnp.bfloat16)

time: 273 us -> 294 us (1.077)
  other arithmetic: 49.8 us -> 8.98 us
  waiting for transfers between devices: 99.6 us -> 139 us
  matrix products: 28.1 us -> 51.6 us
    all_gather x1, waiting for transfers between devices: 21.6 us -> 60.4 us  [on_device(): gathered = lax.all_gather(payload2, 'mp', axis=0, tiled=False)]
    select_n x1 -> x0, other arithmetic: 35.1 us -> none  [on_device(): jnp.where(arrived_adapter >= 0, order[jnp.clip(arrived_adapter, 0, ADAPTE...]
    dot_general x4 -> x5, matrix products: 14.1 us -> 37.7 us  [the longest x1 21 us: on_device(): jnp.einsum('ijg,jgkf->ikf', sel, gathered.reshape(n_mp, groups_per_block,...]
    slice x3 -> x1, local copies, waits for them, and re-layouts: 11 us -> 0.28 us  [the longest x1 8.25 us: on_device(): arrived_t = gathered[:, :local_feat].reshape(n_mp * local_feat, row_count)]
    another operation x1 -> x4, local copies, waits for them, and re-layouts: 0.09 us -> 6.6 us  [the longest x3 6.5 us: padded(): w.reshape(lead, n_mp, local_feat)]
    gather x2 -> x0, other arithmetic: 5.75 us -> none  [on_device(): order[jnp.clip(arrived_adapter, 0, ADAPTERS - 1)]]
    dot_general x0 -> x1, local copies, waits for them, and re-layouts: none -> 3.84 us  [on_device(): lax.dot_general(flat, padded(used_w), (((0,), (1,)), ((), ())), preferred...]
  transfers between devices with their start and end apart: 3 -> 3, of which waited for: 3 -> 3; matrix products, arithmetic and copies ran while one was open for 17% -> 2% of each run, Pallas kernels for 0% -> 0%
where the time goes in v8:
time: 294 us
  waiting for transfers between devices  139 us (47%)
  matrix products  51.6 us (18%)
  blocking collectives  48.3 us (16%)
  local copies, waits for them, and re-layouts  25.6 us (9%)
  between operations  13.8 us (5%)
  other arithmetic  8.98 us (3%)
  starting transfers between devices  6.96 us (2%)
    all_gather x1, waiting for transfers between devices, on_device(): hidden_full = lax.all_gather(hidden, 'mp', axis=0, tiled=True)  66.8 us
    all_gather x1, waiting for transfers between devices, on_device(): gathered = lax.all_gather(payload2, 'mp', axis=0, tiled=False)  60.4 us
    all_to_all x1, blocking collectives, on_device(): lax.all_to_all(down_weight[0], 'mp', split_axis=1, concat_axis=0, tiled=T...  25.8 us
    all_to_all x1, blocking collectives, on_device(): lax.all_to_all(payload.reshape(groups * chunk, local_feat), 'expert', spl...  22.5 us
    dot_general x1, matrix products, on_device(): jnp.einsum('ijg,jgkf->ikf', sel, gathered.reshape(n_mp, groups_per_block,...  21 us
    all_to_all x1, waiting for transfers between devices, on_device(): lax.all_to_all(down_local, 'expert', split_axis=0, concat_axis=0, tiled=T...  11.3 us
    dot_general x1, matrix products, on_device(): lax.dot_general(hidden_full, down_cols_w, (((0,), (0,)), ((), ())), prefe...  9.79 us
    all_to_all x1, starting transfers between devices, on_device(): lax.all_to_all(down_local, 'expert', split_axis=0, concat_axis=0, tiled=T...  6.73 us
  transfers between devices with their start and end apart: 3, of which 3 were waited for; matrix products, arithmetic and copies ran while one was open for 2% of the time, Pallas kernels for 0%

profile of v8, /device:TPU:1, one launch (start us, length us, event | category | flops | bytes accessed | tf_op | source)
XLA Modules:
  0.0 293.8 jit_solution(18123372438468039729)
XLA Ops:
  6.5 0.9 copy.103
  7.8 0.9 select_reduce_fusion.2
  9.2 2.3 reduce-window.19
  12.3 0.7 compare_select_fusion
  13.0 0.9 fusion.5
  14.3 1.1 fusion.21
  15.4 22.5 %all_to_all.37 = bf16[8,260,64]{1,2,0:T(8,128)(2,1)S(1)} all-to-all(bf16[8,260,64]{1,2,0:T(8,128)(2,1)S(1)} %pad_maximum_fusion), channel_id=1, replica_groups=mesh['expert'=8,'mp'=32] {'expert'}, dimensions={0} | all-to-all | bytes 532480 | tf_op jit(solution)/shard_map/all_to_all | solution.py:83
  38.0 0.8 pad_maximum_fusion.1
  39.6 1.6 copy.111
  41.9 0.5 copy.101
  42.5 1.6 copy.102
  44.5 60.4 %all-gather.6.cloned.1.call-done = bf16[3072,2048]{1,0:T(8,128)(2,1)} async-done(((bf16[96,2048]{1,0:T(8,128)(2,1)}), bf16[3072,2048]{1,0:T(8,128)(2,1)}) %all-gather.6.cloned.1.call-update) | async-done | bytes 12582928 | tf_op jit(solution)/shard_map/all_gather | solution.py:92
  105.0 21.0 %fusion.12 = bf16[16,16,2048]{2,0,1:T(8,128)(2,1)S(1)} fusion(bf16[32,6,16,2048]{3,2,1,0:T(8,128)(2,1)} %bitcast.110, pred[16,32,2]{1,0,2:T(8,128)(4,1)S(1)} %fusion.45), kind=kOutput, calls=%fused_computation.11 | convolution fusion | flops 201850880 | bytes 13632512 | tf_op jit(solution)/shard_map/ijg,jgkf->ikf/dot_general | solution.py:118
  126.0 0.6 copy.115
  126.6 3.4 %reshape_reshape.3 = bf16[256,32,64]{2,1,0:T(8,128)(2,1)} reshape(bf16[16,16,2048]{2,1,0:T(8,128)(2,1)S(1)} %copy.115) | data formatting | bytes 2097152 | tf_op jit(solution)/shard_map/reshape;reshape | solution.py:100
  130.0 2.0 concatenate.26
  132.0 3.8 %dot_general.36 = bf16[16,16,3072]{2,1,0:T(8,128)(2,1)} reshape(bf16[256,32,96]{2,1,0:T(8,128)(2,1)S(1)} %concatenate.26) | data formatting | bytes 3145728 | tf_op jit(solution)/shard_map/dot_general | solution.py:124
  135.8 6.5 %convolution_bitcast_fusion.1 = f32[176,2048]{1,0:T(8,128)S(1)} fusion(bf16[32,96,2048]{2,1,0:T(8,128)(2,1)} %bitcast.111, bf16[176,32,64]{2,0,1:T(8,128)(2,1)} %copy.111), kind=kOutput, calls=%fused_computation.15 | convolution fusion | flops 2214592512 | bytes 14745600 | tf_op jit(solution)/shard_map/dot_general | solution.py:136
  142.4 6.5 %convolution_bitcast_fusion.2 = f32[176,2048]{1,0:T(8,128)S(1)} fusion(bf16[32,96,2048]{2,1,0:T(8,128)(2,1)} %bitcast.112, bf16[176,32,64]{2,0,1:T(8,128)(2,1)S(1)} %copy-done.2), kind=kOutput, calls=%fused_computation.16 | convolution fusion | flops 2214592512 | bytes 14745600 | tf_op jit(solution)/shard_map/dot_general | solution.py:135
  149.2 3.4 %fusion.30 = bf16[2048,16]{0,1:T(8,128)(2,1)S(1)} fusion(bf16[16,16,3072]{2,1,0:T(8,128)(2,1)S(1)} %copy-done.1, bf16[3072,2048]{1,0:T(8,128)(2,1)S(1)} %bitcast.114, f32[2048,16]{0,1:T(8,128)S(1)} %fusion.35), kind=kOutput, calls=%fused_computation.28 | convolution fusion | flops 3222241280 | bytes 14352384 | tf_op jit(solution)/shard_map/dot_general | solution.py:124
  153.0 2.2 fusion.20
  155.7 25.8 %all_to_all.38 = bf16[176,32,64]{0,2,1:T(8,128)(2,1)S(1)} all-to-all(bf16[176,32,64]{0,2,1:T(8,128)(2,1)S(1)} %bitcast.94), channel_id=1, replica_groups=mesh['expert'=8,'mp'=32] {'mp'}, dimensions={1} | all-to-all | bytes 1441792 | tf_op jit(solution)/shard_map/all_to_all | solution.py:61
  181.5 0.6 copy.119
  182.1 1.9 all_to_all.30
  184.1 66.8 %all-gather.4.cloned.1.call-done = bf16[5632,2048]{1,0:T(8,128)(2,1)} async-done(((bf16[176,2048]{1,0:T(8,128)(2,1)}), bf16[5632,2048]{1,0:T(8,128)(2,1)}) %all-gather.4.cloned.1.call-update) | async-done | bytes 23068688 | tf_op jit(solution)/shard_map/all_gather | solution.py:140
  250.9 9.8 %convolution_convert_fusion = bf16[2048,64]{0,1:T(8,128)(2,1)S(1)} fusion(bf16[5632,64]{0,1:T(8,128)(2,1)S(1)} %all_to_all.30, bf16[5632,2048]{1,0:T(8,128)(2,1)} %all-gather.4.cloned.1.call-done), kind=kOutput, calls=%fused_computation.19 | convolution fusion | flops 1476526080 | bytes 24051712 | tf_op jit(solution)/shard_map/dot_general | solution.py:141
  260.7 0.7 copy.139
  261.4 6.7 %all-to-all-start.2 = ((bf16[8,256,64]{1,2,0:T(8,128)(2,1)}), bf16[8,256,64]{1,2,0:T(8,128)(2,1)S(1)}, u32[]{:S(2)}, u32[]{:S(2)}) async-start(bf16[8,256,64]{1,2,0:T(8,128)(2,1)} %bitcast.88), calls=%async_computation.2 | async-start | bytes 524288 | tf_op jit(solution)/shard_map/all_to_all | solution.py:144
  268.6 11.3 %all-to-all-done.2 = bf16[8,256,64]{1,2,0:T(8,128)(2,1)S(1)} async-done(((bf16[8,256,64]{1,2,0:T(8,128)(2,1)}), bf16[8,256,64]{1,2,0:T(8,128)(2,1)S(1)}, u32[]{:S(2)}, u32[]{:S(2)}) %all-to-all-start.2) | async-done | bytes 262176 | tf_op jit(solution)/shard_map/all_to_all | solution.py:144
  280.2 3.2 %gather_fusion = bf16[1024,64]{1,0:T(8,128)(2,1)S(1)} fusion(bf16[2048,64]{1,0:T(8,128)(2,1)S(1)} %bitcast.91, s32[1024]{0:T(1024)S(1)} %broadcast_clamp_fusion), kind=kCustom, calls=%fused_computation | custom fusion | bytes 266240 | tf_op jit(solution)/shard_map/gather | solution.py:145
  283.4 2.8 fusion.33
  286.2 0.7 copy.123
  (80 shorter events, 6.0 us)
Async XLA Ops:
  6.5 146.5 %copy-start = (bf16[1,176,1024]{2,1,0:T(8,128)(2,1)S(1)}, bf16[1,176,1024]{2,1,0:T(8,128)(2,1)}, u32[]{:S(2)}) copy-start(bf16[1,176,1024]{2,1,0:T(8,128)(2,1)} %param.21) | copy-start | bytes 1081348
  6.5 98.4 %all-gather.6.cloned.1.call-start = ((), (), s32[]{:S(2)}) async-start(), calls=%async_computation.4 | async-start | bytes 12976128 | tf_op jit(solution)/shard_map/all_gather | solution.py:92
  7.8 6.5 %copy-start.9 = (bf16[512,64]{0,1:T(8,128)(2,1)S(1)}, bf16[512,64]{0,1:T(8,128)(2,1)}, u32[]{:S(2)}) copy-start(bf16[512,64]{0,1:T(8,128)(2,1)} %param.11) | copy-start | bytes 196612
  15.3 22.7 %copy-start.6 = (bf16[1,32,2048]{2,1,0:T(8,128)(2,1)S(1)}, bf16[1,32,2048]{2,1,0:T(8,128)(2,1)}, u32[]{:S(2)}) copy-start(bf16[1,32,2048]{2,1,0:T(8,128)(2,1)} %param.20) | copy-start | bytes 393220
  15.3 23.7 %copy-start.3 = (bf16[1,176,2048]{2,1,0:T(8,128)(2,1)S(1)}, bf16[1,176,2048]{2,1,0:T(8,128)(2,1)}, u32[]{:S(2)}) copy-start(bf16[1,176,2048]{2,1,0:T(8,128)(2,1)} %param.18) | copy-start | bytes 2162692
  38.8 2.4 copy-start.8
  38.8 3.1 %copy-start.4 = (bf16[1,176,2048]{2,1,0:T(8,128)(2,1)S(1)}, bf16[1,176,2048]{2,1,0:T(8,128)(2,1)}, u32[]{:S(2)}) copy-start(bf16[1,176,2048]{2,1,0:T(8,128)(2,1)} %param.17) | copy-start | bytes 2162692
  38.8 212.0 %all-gather.4.cloned.1.call-start = ((), (), s32[]{:S(2)}) async-start(), calls=%async_computation.3 | async-start | bytes 23789568 | tf_op jit(solution)/shard_map/all_gather | solution.py:140
  135.8 6.5 %copy-start.2 = (bf16[176,32,64]{2,0,1:T(8,128)(2,1)S(1)}, bf16[176,32,64]{2,0,1:T(8,128)(2,1)}, u32[]{:S(2)}) copy-start(bf16[176,32,64]{2,0,1:T(8,128)(2,1)} %copy.102) | copy-start | bytes 2162692
  135.8 13.1 %slice-start = ((s8[12582912]{0:T(1024)(128)(4,1)}), s8[4194304]{0:T(1024)(128)(4,1)S(1)}, s32[]{:S(2)}) async-start(s8[12582912]{0:T(1024)(128)(4,1)} %bitcast.113), calls=%async_computation.5 | async-start | bytes 8388608
  135.8 13.1 %slice-start.1 = ((s8[12582912]{0:T(1024)(128)(4,1)}), s8[4194304]{0:T(1024)(128)(4,1)S(1)}, s32[]{:S(2)}) async-start(s8[12582912]{0:T(1024)(128)(4,1)} %bitcast.113), calls=%async_computation.6 | async-start | bytes 8388608
  142.4 6.5 %copy-start.1 = (bf16[16,16,3072]{2,1,0:T(8,128)(2,1)S(1)}, bf16[16,16,3072]{2,1,0:T(8,128)(2,1)}, u32[]{:S(2)}) copy-start(bf16[16,16,3072]{2,1,0:T(8,128)(2,1)} %dot_general.36) | copy-start | bytes 4718596
  142.4 6.8 %slice-start.2 = ((s8[12582912]{0:T(1024)(128)(4,1)}), s8[4194304]{0:T(1024)(128)(4,1)S(1)}, s32[]{:S(2)}) async-start(s8[12582912]{0:T(1024)(128)(4,1)} %bitcast.113), calls=%async_computation.7 | async-start | bytes 8388608
  153.0 2.2 copy-start.5
  184.0 84.4 %copy-start.7 = (f32[512,2]{0,1:T(2,128)S(1)}, f32[512,2]{0,1:T(2,128)}, u32[]{:S(2)}) copy-start(f32[512,2]{0,1:T(2,128)} %param.13) | copy-start | bytes 12292
  261.4 18.5 %all-to-all-start.2 = ((bf16[8,256,64]{1,2,0:T(8,128)(2,1)}), bf16[8,256,64]{1,2,0:T(8,128)(2,1)S(1)}, u32[]{:S(2)}, u32[]{:S(2)}) async-start(bf16[8,256,64]{1,2,0:T(8,128)(2,1)} %bitcast.88), calls=%async_computation.2 | async-start | bytes 524288 | tf_op jit(solution)/shard_map/all_to_all | solution.py:144
Sparse Core Ops, SparseCore 0:
  38.9 65.9 all-gather.5
  155.3 95.5 all-gather.3

commit v9 on v3

--- a/solution.py
+++ b/solution.py
@@ -118,8 +118,11 @@
         jnp.bfloat16
     )
     returned_rows = lax.all_to_all(down_local, "expert", split_axis=0, concat_axis=0, tiled=True)
-    picked = returned_rows[slot_index].astype(jnp.float32)
-    mixed = jnp.sum(route_gate[:, :, None] * picked, axis=1)
+    mixed = jnp.zeros((tok_rows, local_feat), jnp.float32)
+    for choice in range(slot_index.shape[1]):
+        hit = (slot_index[:, choice][:, None] == slot_ids[:, 0][None, :]).astype(returned_rows.dtype)
+        picked = jnp.dot(hit, returned_rows, preferred_element_type=jnp.float32)
+        mixed = mixed + route_gate[:, choice][:, None] * picked
     return mixed.astype(jnp.bfloat16)
 
 

time: 267 us -> 263 us (0.985)
  local copies, waits for them, and re-layouts: 16.4 us -> 11.7 us
  other arithmetic: 9.58 us -> 6.75 us
    gather x1 -> x0, local copies, waits for them, and re-layouts: 3.21 us -> none  [on_device(): picked = returned_rows[slot_index].astype(jnp.float32)]
    reduce_sum x1 -> x0, other arithmetic: 2.83 us -> none  [on_device(): mixed = jnp.sum(route_gate[:, :, None] * picked, axis=1)]
where the time goes in v9:
time: 263 us; the launch traced here: 262 us
  waiting for transfers between devices  153 us (58%)
  matrix products  28 us (11%)
  blocking collectives  25.8 us (10%)
  starting transfers between devices  23.8 us (9%)
  between operations  13.8 us (5%)
  local copies, waits for them, and re-layouts  11.7 us (4%)
  other arithmetic  6.75 us (3%)
    all_gather x1, waiting for transfers between devices, on_device(): hidden_full = lax.all_gather(hidden, 'mp', axis=1, tiled=True)  66.8 us
    all_gather x1, waiting for transfers between devices, on_device(): gathered = lax.all_gather(payload2, 'mp', axis=1, tiled=True)  59.1 us
    all_to_all x1, blocking collectives, on_device(): lax.all_to_all(down_weight[0], 'mp', split_axis=1, concat_axis=0, tiled=T...  25.8 us
    all_to_all x1, waiting for transfers between devices, on_device(): lax.all_to_all(payload.reshape(groups * chunk, local_feat), 'expert', spl...  14.9 us
    dot_general x4, matrix products, contract_last(): lax.dot_general(left, right, (((1,), (1,)), ((), ())), preferred_element_...  13.7 us
    all_to_all x1, waiting for transfers between devices, on_device(): lax.all_to_all(down_local, 'expert', split_axis=0, concat_axis=0, tiled=T...  11.7 us
    dot_general x1, matrix products, on_device(): jnp.dot(hidden_full, down_cols_w, preferred_element_type=jnp.float32)  9.78 us
    all_to_all x1, starting transfers between devices, on_device(): lax.all_to_all(rank_w, 'mp', split_axis=1, concat_axis=0, tiled=True)  8.58 us
  transfers between devices with their start and end apart: 5, of which 4 were waited for; matrix products, arithmetic and copies ran while one was open for 4% of the time, Pallas kernels for 0%

profile of v9, /device:TPU:1, one launch (start us, length us, event | category | flops | bytes accessed | tf_op | source)
XLA Modules:
  0.0 262.3 jit_solution(6632444539328532173)
XLA Ops:
  6.5 1.2 all_to_all.39
  7.9 0.8 reshape.170
  8.7 8.6 %all-to-all-start.1 = ((bf16[32,2,1024]{2,1,0:T(2,128)(2,1)}), bf16[32,2,1024]{2,1,0:T(2,128)(2,1)S(1)}, u32[]{:S(2)}, u32[]{:S(2)}) async-start(bf16[32,2,1024]{2,1,0:T(2,128)(2,1)} %reshape.170), calls=%async_computation.1 | async-start | bytes 262144 | tf_op jit(solution)/shard_map/all_to_all | solution.py:61
  17.3 0.8 copy.95
  18.5 0.9 select_reduce_fusion.2
  19.9 2.3 reduce-window.18
  23.0 0.7 multiply_add_fusion
  23.7 0.9 fusion.7
  24.7 1.1 fusion.13
  26.0 0.8 pad_maximum_fusion
  26.8 8.2 %all-to-all-start = ((bf16[8,260,64]{1,2,0:T(8,128)(2,1)}), bf16[8,260,64]{1,2,0:T(8,128)(2,1)S(1)}, u32[]{:S(2)}, u32[]{:S(2)}) async-start(bf16[8,260,64]{1,2,0:T(8,128)(2,1)} %pad_maximum_fusion), calls=%async_computation | async-start | bytes 786432 | tf_op jit(solution)/shard_map/all_to_all | solution.py:84
  35.3 14.9 %all-to-all-done = bf16[8,260,64]{1,2,0:T(8,128)(2,1)S(1)} async-done(((bf16[8,260,64]{1,2,0:T(8,128)(2,1)}), bf16[8,260,64]{1,2,0:T(8,128)(2,1)S(1)}, u32[]{:S(2)}, u32[]{:S(2)}) %all-to-all-start) | async-done | bytes 266272 | tf_op jit(solution)/shard_map/all_to_all | solution.py:84
  50.8 1.3 multiply_reduce_fusion
  52.8 0.8 pad_maximum_fusion.1
  53.8 59.1 %all-gather.3.cloned.1.call-done = bf16[2560,2048]{0,1:T(8,128)(2,1)} async-done(((bf16[2560,64]{0,1:T(8,128)(2,1)}), bf16[2560,2048]{0,1:T(8,128)(2,1)}) %all-gather.3.cloned.1.call-update) | async-done | bytes 10485776 | tf_op jit(solution)/shard_map/all_gather | solution.py:100
  112.9 1.6 slice-done
  114.5 0.3 reduce
  115.4 0.3 broadcast_multiply_fusion
  115.7 5.1 %fusion.2 = f32[2048,176]{0,1:T(8,128)S(1)} fusion(bf16[2560,2048]{0,1:T(8,128)(2,1)} %all-gather.3.cloned.1.call-done, bf16[1,176,2048]{2,1,0:T(8,128)(2,1)S(1)} %copy-done), kind=kOutput, calls=%fused_computation.3 | convolution fusion | flops 1476395008 | bytes 10551296 | tf_op jit(solution)/shard_map/dot_general | solution.py:35
  120.9 5.1 %fusion = f32[2048,176]{0,1:T(8,128)S(1)} fusion(bf16[2560,2048]{0,1:T(8,128)(2,1)} %all-gather.3.cloned.1.call-done, bf16[1,176,2048]{2,1,0:T(8,128)(2,1)S(1)} %copy-done.3), kind=kOutput, calls=%fused_computation.1 | convolution fusion | flops 1476395008 | bytes 10551296 | tf_op jit(solution)/shard_map/dot_general | solution.py:35
  126.0 2.2 fusion.12
  128.2 0.5 copy.110
  128.8 25.8 %all_to_all.53 = bf16[176,32,64]{0,2,1:T(8,128)(2,1)S(1)} all-to-all(bf16[176,32,64]{0,2,1:T(8,128)(2,1)S(1)} %bitcast.71), channel_id=1, replica_groups=mesh['expert'=8,'mp'=32] {'mp'}, dimensions={1} | all-to-all | bytes 1441792 | tf_op jit(solution)/shard_map/all_to_all | solution.py:62
  154.6 0.6 copy.111
  155.2 1.9 all_to_all.45
  157.1 66.8 %all-gather.5.cloned.1.call-done = bf16[2048,5632]{0,1:T(8,128)(2,1)} async-done(((bf16[2048,176]{0,1:T(8,128)(2,1)}), bf16[2048,5632]{0,1:T(8,128)(2,1)}) %all-gather.5.cloned.1.call-update) | async-done | bytes 23068688 | tf_op jit(solution)/shard_map/all_gather | solution.py:116
  223.9 9.8 %convolution_convert_fusion = bf16[2048,64]{0,1:T(8,128)(2,1)S(1)} fusion(bf16[5632,64]{0,1:T(8,128)(2,1)S(1)} %all_to_all.45, bf16[2048,5632]{0,1:T(8,128)(2,1)} %all-gather.5.cloned.1.call-done), kind=kOutput, calls=%fused_computation.17 | convolution fusion | flops 1476526080 | bytes 24051712 | tf_op jit(solution)/shard_map/dot_general | solution.py:117
  233.7 0.7 copy.126
  234.4 6.7 %all-to-all-start.3 = ((bf16[8,256,64]{1,2,0:T(8,128)(2,1)}), bf16[8,256,64]{1,2,0:T(8,128)(2,1)S(1)}, u32[]{:S(2)}, u32[]{:S(2)}) async-start(bf16[8,256,64]{1,2,0:T(8,128)(2,1)} %bitcast.66), calls=%async_computation.3 | async-start | bytes 524288 | tf_op jit(solution)/shard_map/all_to_all | solution.py:120
  241.2 11.7 %all-to-all-done.3 = bf16[8,256,64]{1,2,0:T(8,128)(2,1)S(1)} async-done(((bf16[8,256,64]{1,2,0:T(8,128)(2,1)}), bf16[8,256,64]{1,2,0:T(8,128)(2,1)S(1)}, u32[]{:S(2)}, u32[]{:S(2)}) %all-to-all-start.3) | async-done | bytes 262176 | tf_op jit(solution)/shard_map/all_to_all | solution.py:120
  252.9 0.9 fusion.24
  253.9 1.6 fusion.25
  (60 shorter events, 4.5 us)
Async XLA Ops:
  6.5 109.2 %copy-start = (bf16[1,176,2048]{2,1,0:T(8,128)(2,1)S(1)}, bf16[1,176,2048]{2,1,0:T(8,128)(2,1)}, u32[]{:S(2)}) copy-start(bf16[1,176,2048]{2,1,0:T(8,128)(2,1)} %param.18) | copy-start | bytes 2162692
  6.5 18.1 %copy-start.5 = (bf16[512,64]{0,1:T(8,128)(2,1)S(1)}, bf16[512,64]{0,1:T(8,128)(2,1)}, u32[]{:S(2)}) copy-start(bf16[512,64]{0,1:T(8,128)(2,1)} %param.11) | copy-start | bytes 196612
  8.7 18.1 %all-to-all-start.1 = ((bf16[32,2,1024]{2,1,0:T(2,128)(2,1)}), bf16[32,2,1024]{2,1,0:T(2,128)(2,1)S(1)}, u32[]{:S(2)}, u32[]{:S(2)}) async-start(bf16[32,2,1024]{2,1,0:T(2,128)(2,1)} %reshape.170), calls=%async_computation.1 | async-start | bytes 262144 | tf_op jit(solution)/shard_map/all_to_all | solution.py:61
  26.8 23.3 %all-to-all-start = ((bf16[8,260,64]{1,2,0:T(8,128)(2,1)}), bf16[8,260,64]{1,2,0:T(8,128)(2,1)S(1)}, u32[]{:S(2)}, u32[]{:S(2)}) async-start(bf16[8,260,64]{1,2,0:T(8,128)(2,1)} %pad_maximum_fusion), calls=%async_computation | async-start | bytes 786432 | tf_op jit(solution)/shard_map/all_to_all | solution.py:84
  35.0 77.9 %all-gather.3.cloned.1.call-start = ((), (), s32[]{:S(2)}) async-start(), calls=%async_computation.4 | async-start | bytes 10813440 | tf_op jit(solution)/shard_map/all_gather | solution.py:100
  53.6 170.3 %all-gather.5.cloned.1.call-start = ((), (), s32[]{:S(2)}) async-start(), calls=%async_computation.5 | async-start | bytes 23789568 | tf_op jit(solution)/shard_map/all_gather | solution.py:116
  112.9 1.6 slice-start
  115.7 5.1 %copy-start.3 = (bf16[1,176,2048]{2,1,0:T(8,128)(2,1)S(1)}, bf16[1,176,2048]{2,1,0:T(8,128)(2,1)}, u32[]{:S(2)}) copy-start(bf16[1,176,2048]{2,1,0:T(8,128)(2,1)} %param.17) | copy-start | bytes 2162692
  120.9 5.1 %copy-start.4 = (bf16[1,176,1024]{2,1,0:T(8,128)(2,1)S(1)}, bf16[1,176,1024]{2,1,0:T(8,128)(2,1)}, u32[]{:S(2)}) copy-start(bf16[1,176,1024]{2,1,0:T(8,128)(2,1)} %param.21) | copy-start | bytes 1081348
  126.0 2.2 copy-start.1
  157.1 84.1 %copy-start.2 = (f32[512,2]{0,1:T(2,128)S(1)}, f32[512,2]{0,1:T(2,128)}, u32[]{:S(2)}) copy-start(f32[512,2]{0,1:T(2,128)} %param.13) | copy-start | bytes 12292
  234.4 18.5 %all-to-all-start.3 = ((bf16[8,256,64]{1,2,0:T(8,128)(2,1)}), bf16[8,256,64]{1,2,0:T(8,128)(2,1)S(1)}, u32[]{:S(2)}, u32[]{:S(2)}) async-start(bf16[8,256,64]{1,2,0:T(8,128)(2,1)} %bitcast.66), calls=%async_computation.3 | async-start | bytes 524288 | tf_op jit(solution)/shard_map/all_to_all | solution.py:120
Sparse Core Ops, SparseCore 0:
  53.7 59.1 all-gather.2
  128.4 95.5 all-gather.4

commit v10 on v9

--- a/solution.py
+++ b/solution.py
@@ -59,6 +59,7 @@
 
     rank_w = adapter_in[0]
     rank_cols_w = lax.all_to_all(rank_w, "mp", split_axis=1, concat_axis=0, tiled=True)
+    gate_up_w = jnp.concatenate([gate_weight[0], up_weight[0]], axis=0)
     down_cols_w = lax.all_to_all(down_weight[0], "mp", split_axis=1, concat_axis=0, tiled=True)
 
     adapter_of = token_adapters(
@@ -107,8 +108,10 @@
         .astype(jnp.bfloat16)
     )
 
-    gate_pre = contract_last(arrived, gate_weight[0])
-    up_base = contract_last(arrived, up_weight[0])
+    units = gate_weight.shape[1]
+    gate_up = contract_last(arrived, gate_up_w)
+    gate_pre = gate_up[:, :units]
+    up_base = gate_up[:, units:]
     chosen = pick.astype(jnp.bfloat16)
     expanded = (rank[:, None, :] * chosen[:, :, None]).reshape(row_count, ADAPTERS * RANK)
     up = up_base + contract_last(expanded, adapter_out[0])

time: 263 us -> 259 us (0.985)
  matrix products: 28 us -> 23.3 us
    dot_general x4 -> x3, matrix products: 13.7 us -> 8.96 us  [contract_last(): lax.dot_general(left, right, (((1,), (1,)), ((), ())), preferred_element_...]
where the time goes in v10:
time: 259 us; the launch traced here: 258 us
  waiting for transfers between devices  153 us (59%)
  blocking collectives  25.8 us (10%)
  starting transfers between devices  23.6 us (9%)
  matrix products  23.3 us (9%)
  between operations  13.7 us (5%)
  local copies, waits for them, and re-layouts  12.1 us (5%)
  other arithmetic  6.75 us (3%)
    all_gather x1, waiting for transfers between devices, on_device(): hidden_full = lax.all_gather(hidden, 'mp', axis=1, tiled=True)  66.8 us
    all_gather x1, waiting for transfers between devices, on_device(): gathered = lax.all_gather(payload2, 'mp', axis=1, tiled=True)  59.3 us
    all_to_all x1, blocking collectives, on_device(): lax.all_to_all(down_weight[0], 'mp', split_axis=1, concat_axis=0, tiled=T...  25.8 us
    all_to_all x1, waiting for transfers between devices, on_device(): lax.all_to_all(payload.reshape(groups * chunk, local_feat), 'expert', spl...  14.9 us
    all_to_all x1, waiting for transfers between devices, on_device(): lax.all_to_all(down_local, 'expert', split_axis=0, concat_axis=0, tiled=T...  11.7 us
    dot_general x1, matrix products, on_device(): jnp.dot(hidden_full, down_cols_w, preferred_element_type=jnp.float32)  9.78 us
    dot_general x3, matrix products, contract_last(): lax.dot_general(left, right, (((1,), (1,)), ((), ())), preferred_element_...  8.96 us
    all_to_all x1, starting transfers between devices, on_device(): lax.all_to_all(rank_w, 'mp', split_axis=1, concat_axis=0, tiled=True)  8.58 us
  transfers between devices with their start and end apart: 5, of which 4 were waited for; matrix products, arithmetic and copies ran while one was open for 4% of the time, Pallas kernels for 0%

profile of v10, /device:TPU:1, one launch (start us, length us, event | category | flops | bytes accessed | tf_op | source)
XLA Modules:
  0.0 258.0 jit_solution(2947236605131702755)
XLA Ops:
  6.5 1.2 all_to_all.39
  7.9 0.8 reshape.170
  8.7 8.6 %all-to-all-start.1 = ((bf16[32,2,1024]{2,1,0:T(2,128)(2,1)}), bf16[32,2,1024]{2,1,0:T(2,128)(2,1)S(1)}, u32[]{:S(2)}, u32[]{:S(2)}) async-start(bf16[32,2,1024]{2,1,0:T(2,128)(2,1)} %reshape.170), calls=%async_computation.1 | async-start | bytes 262144 | tf_op jit(solution)/shard_map/all_to_all | solution.py:61
  17.3 0.8 copy.95
  18.5 0.9 select_reduce_fusion.2
  19.9 2.3 reduce-window.18
  23.0 0.7 multiply_add_fusion
  23.7 0.9 fusion.5
  24.7 1.1 fusion.11
  26.0 0.8 pad_maximum_fusion
  26.8 8.2 %all-to-all-start = ((bf16[8,260,64]{1,2,0:T(8,128)(2,1)}), bf16[8,260,64]{1,2,0:T(8,128)(2,1)S(1)}, u32[]{:S(2)}, u32[]{:S(2)}) async-start(bf16[8,260,64]{1,2,0:T(8,128)(2,1)} %pad_maximum_fusion), calls=%async_computation | async-start | bytes 786432 | tf_op jit(solution)/shard_map/all_to_all | solution.py:85
  35.3 14.9 %all-to-all-done = bf16[8,260,64]{1,2,0:T(8,128)(2,1)S(1)} async-done(((bf16[8,260,64]{1,2,0:T(8,128)(2,1)}), bf16[8,260,64]{1,2,0:T(8,128)(2,1)S(1)}, u32[]{:S(2)}, u32[]{:S(2)}) %all-to-all-start) | async-done | bytes 266272 | tf_op jit(solution)/shard_map/all_to_all | solution.py:85
  50.8 1.3 multiply_reduce_fusion
  52.4 0.3 convert_element_type.93
  52.8 0.8 pad_maximum_fusion.1
  53.6 59.3 %all-gather.3.cloned.1.call-done = bf16[2560,2048]{0,1:T(8,128)(2,1)} async-done(((bf16[2560,64]{0,1:T(8,128)(2,1)}), bf16[2560,2048]{0,1:T(8,128)(2,1)}) %all-gather.3.cloned.1.call-update) | async-done | bytes 10485776 | tf_op jit(solution)/shard_map/all_gather | solution.py:101
  112.9 1.8 slice-done
  114.7 0.3 reduce
  115.6 0.3 broadcast_multiply_fusion
  116.1 5.5 %fusion = f32[2048,352]{0,1:T(8,128)S(1)} fusion(bf16[2560,2048]{0,1:T(8,128)(2,1)} %all-gather.3.cloned.1.call-done, bf16[176,2048]{1,0:T(8,128)(2,1)S(1)} %bitcast.90, bf16[176,2048]{1,0:T(8,128)(2,1)S(1)} %bitcast.91), kind=kOutput, calls=%fused_computation | convolution fusion | flops 2955673600 | bytes 12713984 | tf_op jit(solution)/shard_map/dot_general | solution.py:35
  121.7 2.2 fusion.10
  123.9 0.5 copy.110
  124.4 25.8 %all_to_all.53 = bf16[176,32,64]{0,2,1:T(8,128)(2,1)S(1)} all-to-all(bf16[176,32,64]{0,2,1:T(8,128)(2,1)S(1)} %bitcast.67), channel_id=1, replica_groups=mesh['expert'=8,'mp'=32] {'mp'}, dimensions={1} | all-to-all | bytes 1441792 | tf_op jit(solution)/shard_map/all_to_all | solution.py:63
  150.2 0.6 copy.111
  150.8 1.9 all_to_all.45
  152.8 66.8 %all-gather.5.cloned.1.call-done = bf16[2048,5632]{0,1:T(8,128)(2,1)} async-done(((bf16[2048,176]{0,1:T(8,128)(2,1)}), bf16[2048,5632]{0,1:T(8,128)(2,1)}) %all-gather.5.cloned.1.call-update) | async-done | bytes 23068688 | tf_op jit(solution)/shard_map/all_gather | solution.py:119
  219.6 9.8 %convolution_convert_fusion = bf16[2048,64]{0,1:T(8,128)(2,1)S(1)} fusion(bf16[5632,64]{0,1:T(8,128)(2,1)S(1)} %all_to_all.45, bf16[2048,5632]{0,1:T(8,128)(2,1)} %all-gather.5.cloned.1.call-done), kind=kOutput, calls=%fused_computation.15 | convolution fusion | flops 1476526080 | bytes 24051712 | tf_op jit(solution)/shard_map/dot_general | solution.py:120
  229.4 0.7 copy.126
  230.1 6.7 %all-to-all-start.3 = ((bf16[8,256,64]{1,2,0:T(8,128)(2,1)}), bf16[8,256,64]{1,2,0:T(8,128)(2,1)S(1)}, u32[]{:S(2)}, u32[]{:S(2)}) async-start(bf16[8,256,64]{1,2,0:T(8,128)(2,1)} %bitcast.62), calls=%async_computation.3 | async-start | bytes 524288 | tf_op jit(solution)/shard_map/all_to_all | solution.py:123
  236.8 11.7 %all-to-all-done.3 = bf16[8,256,64]{1,2,0:T(8,128)(2,1)S(1)} async-done(((bf16[8,256,64]{1,2,0:T(8,128)(2,1)}), bf16[8,256,64]{1,2,0:T(8,128)(2,1)S(1)}, u32[]{:S(2)}, u32[]{:S(2)}) %all-to-all-start.3) | async-done | bytes 262176 | tf_op jit(solution)/shard_map/all_to_all | solution.py:123
  248.6 0.9 fusion.25
  249.5 1.6 fusion.26
  (59 shorter events, 4.2 us)
Async XLA Ops:
  6.5 115.1 %copy-start = (bf16[1,176,1024]{2,1,0:T(8,128)(2,1)S(1)}, bf16[1,176,1024]{2,1,0:T(8,128)(2,1)}, u32[]{:S(2)}) copy-start(bf16[1,176,1024]{2,1,0:T(8,128)(2,1)} %param.21) | copy-start | bytes 1081348
  6.5 18.1 %copy-start.5 = (bf16[512,64]{0,1:T(8,128)(2,1)S(1)}, bf16[512,64]{0,1:T(8,128)(2,1)}, u32[]{:S(2)}) copy-start(bf16[512,64]{0,1:T(8,128)(2,1)} %param.11) | copy-start | bytes 196612
  8.7 18.1 %all-to-all-start.1 = ((bf16[32,2,1024]{2,1,0:T(2,128)(2,1)}), bf16[32,2,1024]{2,1,0:T(2,128)(2,1)S(1)}, u32[]{:S(2)}, u32[]{:S(2)}) async-start(bf16[32,2,1024]{2,1,0:T(2,128)(2,1)} %reshape.170), calls=%async_computation.1 | async-start | bytes 262144 | tf_op jit(solution)/shard_map/all_to_all | solution.py:61
  26.8 23.3 %all-to-all-start = ((bf16[8,260,64]{1,2,0:T(8,128)(2,1)}), bf16[8,260,64]{1,2,0:T(8,128)(2,1)S(1)}, u32[]{:S(2)}, u32[]{:S(2)}) async-start(bf16[8,260,64]{1,2,0:T(8,128)(2,1)} %pad_maximum_fusion), calls=%async_computation | async-start | bytes 786432 | tf_op jit(solution)/shard_map/all_to_all | solution.py:85
  35.0 77.9 %all-gather.3.cloned.1.call-start = ((), (), s32[]{:S(2)}) async-start(), calls=%async_computation.4 | async-start | bytes 10813440 | tf_op jit(solution)/shard_map/all_gather | solution.py:101
  53.6 166.0 %all-gather.5.cloned.1.call-start = ((), (), s32[]{:S(2)}) async-start(), calls=%async_computation.5 | async-start | bytes 23789568 | tf_op jit(solution)/shard_map/all_gather | solution.py:119
  112.9 1.8 slice-start
  112.9 3.0 %copy-start.3 = (bf16[1,176,2048]{2,1,0:T(8,128)(2,1)S(1)}, bf16[1,176,2048]{2,1,0:T(8,128)(2,1)}, u32[]{:S(2)}) copy-start(bf16[1,176,2048]{2,1,0:T(8,128)(2,1)} %param.18) | copy-start | bytes 2162692
  115.0 1.1 copy-start.4
  121.7 2.2 copy-start.1
  152.7 84.1 %copy-start.2 = (f32[512,2]{0,1:T(2,128)S(1)}, f32[512,2]{0,1:T(2,128)}, u32[]{:S(2)}) copy-start(f32[512,2]{0,1:T(2,128)} %param.13) | copy-start | bytes 12292
  230.1 18.5 %all-to-all-start.3 = ((bf16[8,256,64]{1,2,0:T(8,128)(2,1)}), bf16[8,256,64]{1,2,0:T(8,128)(2,1)S(1)}, u32[]{:S(2)}, u32[]{:S(2)}) async-start(bf16[8,256,64]{1,2,0:T(8,128)(2,1)} %bitcast.62), calls=%async_computation.3 | async-start | bytes 524288 | tf_op jit(solution)/shard_map/all_to_all | solution.py:123
Sparse Core Ops, SparseCore 0:
  53.7 59.1 all-gather.2
  124.0 95.5 all-gather.4

commit v11 on v10

--- a/solution.py
+++ b/solution.py
@@ -26,7 +26,13 @@
     one_hot = (flat_routes[:, None] == jnp.arange(groups, dtype=jnp.int32)[None, :]).astype(
         jnp.int32
     )
-    before = jnp.cumsum(one_hot, axis=0, dtype=jnp.int32) - one_hot
+    count = flat_routes.shape[0]
+    earlier = (
+        jnp.arange(count, dtype=jnp.int32)[None, :] < jnp.arange(count, dtype=jnp.int32)[:, None]
+    ).astype(jnp.bfloat16)
+    before = jnp.dot(
+        earlier, one_hot.astype(jnp.bfloat16), preferred_element_type=jnp.float32
+    ).astype(jnp.int32)
     seat_index = jnp.sum(before * one_hot, axis=1, dtype=jnp.int32)
     return (flat_routes * capacity + seat_index).reshape(routes.shape)
 

time: 259 us -> 256 us (0.988)
  transfers between devices with their start and end apart: 5 -> 5, of which waited for: 4 -> 5; matrix products, arithmetic and copies ran while one was open for 4% -> 3% of each run, Pallas kernels for 0% -> 0%
where the time goes in v11:
time: 256 us; the launch traced here: 255 us
  waiting for transfers between devices  153 us (60%)
  blocking collectives  25.8 us (10%)
  matrix products  23.8 us (9%)
  starting transfers between devices  23.6 us (9%)
  between operations  13.7 us (5%)
  local copies, waits for them, and re-layouts  11.6 us (5%)
  other arithmetic  4.21 us (2%)
    all_gather x1, waiting for transfers between devices, on_device(): hidden_full = lax.all_gather(hidden, 'mp', axis=1, tiled=True)  66.8 us
    all_gather x1, waiting for transfers between devices, on_device(): gathered = lax.all_gather(payload2, 'mp', axis=1, tiled=True)  58.6 us
    all_to_all x1, blocking collectives, on_device(): lax.all_to_all(down_weight[0], 'mp', split_axis=1, concat_axis=0, tiled=T...  25.8 us
    all_to_all x1, waiting for transfers between devices, on_device(): lax.all_to_all(payload.reshape(groups * chunk, local_feat), 'expert', spl...  14.9 us
    all_to_all x1, waiting for transfers between devices, on_device(): lax.all_to_all(down_local, 'expert', split_axis=0, concat_axis=0, tiled=T...  11.7 us
    dot_general x1, matrix products, on_device(): jnp.dot(hidden_full, down_cols_w, preferred_element_type=jnp.float32)  9.78 us
    dot_general x3, matrix products, contract_last(): lax.dot_general(left, right, (((1,), (1,)), ((), ())), preferred_element_...  8.96 us
    all_to_all x1, starting transfers between devices, on_device(): lax.all_to_all(rank_w, 'mp', split_axis=1, concat_axis=0, tiled=True)  8.58 us
  transfers between devices with their start and end apart: 5, of which 5 were waited for; matrix products, arithmetic and copies ran while one was open for 3% of the time, Pallas kernels for 0%

profile of v11, /device:TPU:1, one launch (start us, length us, event | category | flops | bytes accessed | tf_op | source)
XLA Modules:
  0.0 255.4 jit_solution(1396880073404984713)
XLA Ops:
  6.5 1.2 all_to_all.39
  7.9 0.8 reshape.152
  8.7 8.6 %all-to-all-start.1 = ((bf16[32,2,1024]{2,1,0:T(2,128)(2,1)}), bf16[32,2,1024]{2,1,0:T(2,128)(2,1)S(1)}, u32[]{:S(2)}, u32[]{:S(2)}) async-start(bf16[32,2,1024]{2,1,0:T(2,128)(2,1)} %reshape.152), calls=%async_computation.1 | async-start | bytes 262144 | tf_op jit(solution)/shard_map/all_to_all | solution.py:67
  17.3 0.9 select_reduce_fusion.2
  18.7 0.8 copy.90
  19.7 0.5 fusion.30
  20.5 0.7 multiply_add_fusion
  21.2 0.9 fusion.6
  22.1 1.1 fusion.12
  23.5 0.8 pad_maximum_fusion
  24.3 0.7 all-to-all-done.1
  25.0 8.2 %all-to-all-start = ((bf16[8,260,64]{1,2,0:T(8,128)(2,1)}), bf16[8,260,64]{1,2,0:T(8,128)(2,1)S(1)}, u32[]{:S(2)}, u32[]{:S(2)}) async-start(bf16[8,260,64]{1,2,0:T(8,128)(2,1)} %pad_maximum_fusion), calls=%async_computation | async-start | bytes 786432 | tf_op jit(solution)/shard_map/all_to_all | solution.py:91
  33.4 14.9 %all-to-all-done = bf16[8,260,64]{1,2,0:T(8,128)(2,1)S(1)} async-done(((bf16[8,260,64]{1,2,0:T(8,128)(2,1)}), bf16[8,260,64]{1,2,0:T(8,128)(2,1)S(1)}, u32[]{:S(2)}, u32[]{:S(2)}) %all-to-all-start) | async-done | bytes 266272 | tf_op jit(solution)/shard_map/all_to_all | solution.py:91
  49.0 1.3 multiply_reduce_fusion
  51.0 0.8 pad_maximum_fusion.1
  51.8 58.6 %all-gather.3.cloned.1.call-done = bf16[2560,2048]{0,1:T(8,128)(2,1)} async-done(((bf16[2560,64]{0,1:T(8,128)(2,1)}), bf16[2560,2048]{0,1:T(8,128)(2,1)}) %all-gather.3.cloned.1.call-update) | async-done | bytes 10485776 | tf_op jit(solution)/shard_map/all_gather | solution.py:107
  110.4 1.8 slice-done
  112.2 0.3 reduce
  113.1 0.3 broadcast_multiply_fusion
  113.6 5.5 %fusion = f32[2048,352]{0,1:T(8,128)S(1)} fusion(bf16[2560,2048]{0,1:T(8,128)(2,1)} %all-gather.3.cloned.1.call-done, bf16[176,2048]{1,0:T(8,128)(2,1)S(1)} %bitcast.70, bf16[176,2048]{1,0:T(8,128)(2,1)S(1)} %bitcast.71), kind=kOutput, calls=%fused_computation | convolution fusion | flops 2955673600 | bytes 12713984 | tf_op jit(solution)/shard_map/dot_general | solution.py:41
  119.2 2.2 fusion.11
  121.4 0.5 copy.104
  121.9 25.8 %all_to_all.53 = bf16[176,32,64]{0,2,1:T(8,128)(2,1)S(1)} all-to-all(bf16[176,32,64]{0,2,1:T(8,128)(2,1)S(1)} %bitcast.48), channel_id=1, replica_groups=mesh['expert'=8,'mp'=32] {'mp'}, dimensions={1} | all-to-all | bytes 1441792 | tf_op jit(solution)/shard_map/all_to_all | solution.py:69
  147.7 0.6 copy.105
  148.3 1.9 all_to_all.45
  150.2 66.8 %all-gather.5.cloned.1.call-done = bf16[2048,5632]{0,1:T(8,128)(2,1)} async-done(((bf16[2048,176]{0,1:T(8,128)(2,1)}), bf16[2048,5632]{0,1:T(8,128)(2,1)}) %all-gather.5.cloned.1.call-update) | async-done | bytes 23068688 | tf_op jit(solution)/shard_map/all_gather | solution.py:125
  217.1 9.8 %convolution_convert_fusion = bf16[2048,64]{0,1:T(8,128)(2,1)S(1)} fusion(bf16[5632,64]{0,1:T(8,128)(2,1)S(1)} %all_to_all.45, bf16[2048,5632]{0,1:T(8,128)(2,1)} %all-gather.5.cloned.1.call-done), kind=kOutput, calls=%fused_computation.17 | convolution fusion | flops 1476526080 | bytes 24051712 | tf_op jit(solution)/shard_map/dot_general | solution.py:126
  226.8 0.7 copy.118
  227.6 6.7 %all-to-all-start.3 = ((bf16[8,256,64]{1,2,0:T(8,128)(2,1)}), bf16[8,256,64]{1,2,0:T(8,128)(2,1)S(1)}, u32[]{:S(2)}, u32[]{:S(2)}) async-start(bf16[8,256,64]{1,2,0:T(8,128)(2,1)} %bitcast.44), calls=%async_computation.3 | async-start | bytes 524288 | tf_op jit(solution)/shard_map/all_to_all | solution.py:129
  234.3 11.7 %all-to-all-done.3 = bf16[8,256,64]{1,2,0:T(8,128)(2,1)S(1)} async-done(((bf16[8,256,64]{1,2,0:T(8,128)(2,1)}), bf16[8,256,64]{1,2,0:T(8,128)(2,1)S(1)}, u32[]{:S(2)}, u32[]{:S(2)}) %all-to-all-start.3) | async-done | bytes 262176 | tf_op jit(solution)/shard_map/all_to_all | solution.py:129
  246.1 0.9 fusion.26
  247.0 1.6 fusion.27
  (53 shorter events, 3.8 us)
Async XLA Ops:
  6.5 112.6 %copy-start = (bf16[1,176,1024]{2,1,0:T(8,128)(2,1)S(1)}, bf16[1,176,1024]{2,1,0:T(8,128)(2,1)}, u32[]{:S(2)}) copy-start(bf16[1,176,1024]{2,1,0:T(8,128)(2,1)} %param.21) | copy-start | bytes 1081348
  6.5 15.6 %copy-start.5 = (bf16[512,64]{0,1:T(8,128)(2,1)S(1)}, bf16[512,64]{0,1:T(8,128)(2,1)}, u32[]{:S(2)}) copy-start(bf16[512,64]{0,1:T(8,128)(2,1)} %param.11) | copy-start | bytes 196612
  8.7 16.3 %all-to-all-start.1 = ((bf16[32,2,1024]{2,1,0:T(2,128)(2,1)}), bf16[32,2,1024]{2,1,0:T(2,128)(2,1)S(1)}, u32[]{:S(2)}, u32[]{:S(2)}) async-start(bf16[32,2,1024]{2,1,0:T(2,128)(2,1)} %reshape.152), calls=%async_computation.1 | async-start | bytes 262144 | tf_op jit(solution)/shard_map/all_to_all | solution.py:67
  25.0 23.3 %all-to-all-start = ((bf16[8,260,64]{1,2,0:T(8,128)(2,1)}), bf16[8,260,64]{1,2,0:T(8,128)(2,1)S(1)}, u32[]{:S(2)}, u32[]{:S(2)}) async-start(bf16[8,260,64]{1,2,0:T(8,128)(2,1)} %pad_maximum_fusion), calls=%async_computation | async-start | bytes 786432 | tf_op jit(solution)/shard_map/all_to_all | solution.py:91
  33.2 77.2 %all-gather.3.cloned.1.call-start = ((), (), s32[]{:S(2)}) async-start(), calls=%async_computation.4 | async-start | bytes 10813440 | tf_op jit(solution)/shard_map/all_gather | solution.py:107
  51.8 165.3 %all-gather.5.cloned.1.call-start = ((), (), s32[]{:S(2)}) async-start(), calls=%async_computation.5 | async-start | bytes 23789568 | tf_op jit(solution)/shard_map/all_gather | solution.py:125
  110.4 1.8 slice-start
  110.4 3.0 %copy-start.3 = (bf16[1,176,2048]{2,1,0:T(8,128)(2,1)S(1)}, bf16[1,176,2048]{2,1,0:T(8,128)(2,1)}, u32[]{:S(2)}) copy-start(bf16[1,176,2048]{2,1,0:T(8,128)(2,1)} %param.18) | copy-start | bytes 2162692
  112.5 1.1 copy-start.4
  119.2 2.2 copy-start.1
  150.2 84.1 %copy-start.2 = (f32[512,2]{0,1:T(2,128)S(1)}, f32[512,2]{0,1:T(2,128)}, u32[]{:S(2)}) copy-start(f32[512,2]{0,1:T(2,128)} %param.13) | copy-start | bytes 12292
  227.6 18.5 %all-to-all-start.3 = ((bf16[8,256,64]{1,2,0:T(8,128)(2,1)}), bf16[8,256,64]{1,2,0:T(8,128)(2,1)S(1)}, u32[]{:S(2)}, u32[]{:S(2)}) async-start(bf16[8,256,64]{1,2,0:T(8,128)(2,1)} %bitcast.44), calls=%async_computation.3 | async-start | bytes 524288 | tf_op jit(solution)/shard_map/all_to_all | solution.py:129
Sparse Core Ops, SparseCore 0:
  51.9 58.4 all-gather.2
  121.5 95.5 all-gather.4

commit v12 on v11

--- a/solution.py
+++ b/solution.py
@@ -76,10 +76,10 @@
     seat = (
         (slot_index[None, :, 0] == slot_ids) | (slot_index[None, :, 1] == slot_ids)
     ).astype(tokens.dtype)
-    send_rows = jnp.dot(seat, tokens, preferred_element_type=jnp.float32).astype(tokens.dtype)
-    id_plus = jnp.dot(
-        seat, (adapter_of + 1).astype(tokens.dtype), preferred_element_type=jnp.float32
-    ) - 1.0
+    with_ids = jnp.concatenate([tokens, (adapter_of + 1).astype(tokens.dtype)[:, None]], axis=1)
+    seated = jnp.dot(seat, with_ids, preferred_element_type=jnp.float32)
+    send_rows = seated[:, :local_feat].astype(tokens.dtype)
+    id_plus = seated[:, local_feat] - 1.0
     payload = jnp.concatenate(
         [
             send_rows.reshape(groups, capacity, local_feat),

time: 256 us -> 256 us (level)
  no operation moved by 1% of the time
where the time goes in v12:
time: 256 us; the launch traced here: 255 us
  waiting for transfers between devices  153 us (60%)
  blocking collectives  25.8 us (10%)
  starting transfers between devices  23.6 us (9%)
  matrix products  23.6 us (9%)
  between operations  13.7 us (5%)
  local copies, waits for them, and re-layouts  11.7 us (5%)
  other arithmetic  4.23 us (2%)
    all_gather x1, waiting for transfers between devices, on_device(): hidden_full = lax.all_gather(hidden, 'mp', axis=1, tiled=True)  66.8 us
    all_gather x1, waiting for transfers between devices, on_device(): gathered = lax.all_gather(payload2, 'mp', axis=1, tiled=True)  58.5 us
    all_to_all x1, blocking collectives, on_device(): lax.all_to_all(down_weight[0], 'mp', split_axis=1, concat_axis=0, tiled=T...  25.8 us
    all_to_all x1, waiting for transfers between devices, on_device(): lax.all_to_all(payload.reshape(groups * chunk, local_feat), 'expert', spl...  14.9 us
    all_to_all x1, waiting for transfers between devices, on_device(): lax.all_to_all(down_local, 'expert', split_axis=0, concat_axis=0, tiled=T...  11.7 us
    dot_general x1, matrix products, on_device(): jnp.dot(hidden_full, down_cols_w, preferred_element_type=jnp.float32)  9.78 us
    dot_general x3, matrix products, contract_last(): lax.dot_general(left, right, (((1,), (1,)), ((), ())), preferred_element_...  8.96 us
    all_to_all x1, starting transfers between devices, on_device(): lax.all_to_all(rank_w, 'mp', split_axis=1, concat_axis=0, tiled=True)  8.58 us
  transfers between devices with their start and end apart: 5, of which 5 were waited for; matrix products, arithmetic and copies ran while one was open for 3% of the time, Pallas kernels for 0%

profile of v12, /device:TPU:1, one launch (start us, length us, event | category | flops | bytes accessed | tf_op | source)
XLA Modules:
  0.0 255.4 jit_solution(9792328285877058332)
XLA Ops:
  6.5 1.2 all_to_all.39
  7.9 0.8 reshape.165
  8.7 8.6 %all-to-all-start.1 = ((bf16[32,2,1024]{2,1,0:T(2,128)(2,1)}), bf16[32,2,1024]{2,1,0:T(2,128)(2,1)S(1)}, u32[]{:S(2)}, u32[]{:S(2)}) async-start(bf16[32,2,1024]{2,1,0:T(2,128)(2,1)} %reshape.165), calls=%async_computation.1 | async-start | bytes 262144 | tf_op jit(solution)/shard_map/all_to_all | solution.py:67
  17.3 0.8 copy.91
  18.3 0.5 fusion.23
  19.1 0.7 multiply_add_fusion
  19.8 0.9 select_reduce_fusion.2
  21.2 1.9 fusion.6
  23.4 0.8 pad_maximum_fusion
  24.2 0.8 all-to-all-done.1
  25.0 8.2 %all-to-all-start = ((bf16[8,260,64]{1,2,0:T(8,128)(2,1)}), bf16[8,260,64]{1,2,0:T(8,128)(2,1)S(1)}, u32[]{:S(2)}, u32[]{:S(2)}) async-start(bf16[8,260,64]{1,2,0:T(8,128)(2,1)} %pad_maximum_fusion), calls=%async_computation | async-start | bytes 786432 | tf_op jit(solution)/shard_map/all_to_all | solution.py:91
  33.4 14.9 %all-to-all-done = bf16[8,260,64]{1,2,0:T(8,128)(2,1)S(1)} async-done(((bf16[8,260,64]{1,2,0:T(8,128)(2,1)}), bf16[8,260,64]{1,2,0:T(8,128)(2,1)S(1)}, u32[]{:S(2)}, u32[]{:S(2)}) %all-to-all-start) | async-done | bytes 266272 | tf_op jit(solution)/shard_map/all_to_all | solution.py:91
  49.0 1.3 multiply_reduce_fusion
  50.5 0.3 convert_element_type.110
  51.0 0.8 pad_maximum_fusion.1
  51.8 58.5 %all-gather.3.cloned.1.call-done = bf16[2560,2048]{0,1:T(8,128)(2,1)} async-done(((bf16[2560,64]{0,1:T(8,128)(2,1)}), bf16[2560,2048]{0,1:T(8,128)(2,1)}) %all-gather.3.cloned.1.call-update) | async-done | bytes 10485776 | tf_op jit(solution)/shard_map/all_gather | solution.py:107
  110.3 1.8 slice-done
  112.1 0.3 reduce
  113.0 0.3 broadcast_multiply_fusion
  113.5 5.5 %fusion = f32[2048,352]{0,1:T(8,128)S(1)} fusion(bf16[2560,2048]{0,1:T(8,128)(2,1)} %all-gather.3.cloned.1.call-done, bf16[176,2048]{1,0:T(8,128)(2,1)S(1)} %bitcast.64, bf16[176,2048]{1,0:T(8,128)(2,1)S(1)} %bitcast.65), kind=kOutput, calls=%fused_computation | convolution fusion | flops 2955673600 | bytes 12713984 | tf_op jit(solution)/shard_map/dot_general | solution.py:41
  119.1 2.2 fusion.9
  121.3 0.5 copy.105
  121.8 25.8 %all_to_all.53 = bf16[176,32,64]{0,2,1:T(8,128)(2,1)S(1)} all-to-all(bf16[176,32,64]{0,2,1:T(8,128)(2,1)S(1)} %bitcast.45), channel_id=1, replica_groups=mesh['expert'=8,'mp'=32] {'mp'}, dimensions={1} | all-to-all | bytes 1441792 | tf_op jit(solution)/shard_map/all_to_all | solution.py:69
  147.6 0.6 copy.106
  148.2 1.9 all_to_all.45
  150.1 66.8 %all-gather.5.cloned.1.call-done = bf16[2048,5632]{0,1:T(8,128)(2,1)} async-done(((bf16[2048,176]{0,1:T(8,128)(2,1)}), bf16[2048,5632]{0,1:T(8,128)(2,1)}) %all-gather.5.cloned.1.call-update) | async-done | bytes 23068688 | tf_op jit(solution)/shard_map/all_gather | solution.py:125
  217.0 9.8 %convolution_convert_fusion = bf16[2048,64]{0,1:T(8,128)(2,1)S(1)} fusion(bf16[5632,64]{0,1:T(8,128)(2,1)S(1)} %all_to_all.45, bf16[2048,5632]{0,1:T(8,128)(2,1)} %all-gather.5.cloned.1.call-done), kind=kOutput, calls=%fused_computation.16 | convolution fusion | flops 1476526080 | bytes 24051712 | tf_op jit(solution)/shard_map/dot_general | solution.py:126
  226.8 0.7 copy.119
  227.5 6.7 %all-to-all-start.3 = ((bf16[8,256,64]{1,2,0:T(8,128)(2,1)}), bf16[8,256,64]{1,2,0:T(8,128)(2,1)S(1)}, u32[]{:S(2)}, u32[]{:S(2)}) async-start(bf16[8,256,64]{1,2,0:T(8,128)(2,1)} %bitcast.41), calls=%async_computation.3 | async-start | bytes 524288 | tf_op jit(solution)/shard_map/all_to_all | solution.py:129
  234.2 11.7 %all-to-all-done.3 = bf16[8,256,64]{1,2,0:T(8,128)(2,1)S(1)} async-done(((bf16[8,256,64]{1,2,0:T(8,128)(2,1)}), bf16[8,256,64]{1,2,0:T(8,128)(2,1)S(1)}, u32[]{:S(2)}, u32[]{:S(2)}) %all-to-all-start.3) | async-done | bytes 262176 | tf_op jit(solution)/shard_map/all_to_all | solution.py:129
  246.0 0.9 fusion.19
  246.9 1.6 fusion.20
  (51 shorter events, 3.5 us)
Async XLA Ops:
  6.5 112.5 %copy-start = (bf16[1,176,1024]{2,1,0:T(8,128)(2,1)S(1)}, bf16[1,176,1024]{2,1,0:T(8,128)(2,1)}, u32[]{:S(2)}) copy-start(bf16[1,176,1024]{2,1,0:T(8,128)(2,1)} %param.21) | copy-start | bytes 1081348
  8.7 16.3 %all-to-all-start.1 = ((bf16[32,2,1024]{2,1,0:T(2,128)(2,1)}), bf16[32,2,1024]{2,1,0:T(2,128)(2,1)S(1)}, u32[]{:S(2)}, u32[]{:S(2)}) async-start(bf16[32,2,1024]{2,1,0:T(2,128)(2,1)} %reshape.165), calls=%async_computation.1 | async-start | bytes 262144 | tf_op jit(solution)/shard_map/all_to_all | solution.py:67
  25.0 23.3 %all-to-all-start = ((bf16[8,260,64]{1,2,0:T(8,128)(2,1)}), bf16[8,260,64]{1,2,0:T(8,128)(2,1)S(1)}, u32[]{:S(2)}, u32[]{:S(2)}) async-start(bf16[8,260,64]{1,2,0:T(8,128)(2,1)} %pad_maximum_fusion), calls=%async_computation | async-start | bytes 786432 | tf_op jit(solution)/shard_map/all_to_all | solution.py:91
  33.2 77.1 %all-gather.3.cloned.1.call-start = ((), (), s32[]{:S(2)}) async-start(), calls=%async_computation.4 | async-start | bytes 10813440 | tf_op jit(solution)/shard_map/all_gather | solution.py:107
  51.8 165.2 %all-gather.5.cloned.1.call-start = ((), (), s32[]{:S(2)}) async-start(), calls=%async_computation.5 | async-start | bytes 23789568 | tf_op jit(solution)/shard_map/all_gather | solution.py:125
  110.3 1.8 slice-start
  110.3 3.0 %copy-start.3 = (bf16[1,176,2048]{2,1,0:T(8,128)(2,1)S(1)}, bf16[1,176,2048]{2,1,0:T(8,128)(2,1)}, u32[]{:S(2)}) copy-start(bf16[1,176,2048]{2,1,0:T(8,128)(2,1)} %param.18) | copy-start | bytes 2162692
  112.4 1.1 copy-start.4
  119.1 2.2 copy-start.1
  150.1 84.1 %copy-start.2 = (f32[512,2]{0,1:T(2,128)S(1)}, f32[512,2]{0,1:T(2,128)}, u32[]{:S(2)}) copy-start(f32[512,2]{0,1:T(2,128)} %param.13) | copy-start | bytes 12292
  227.5 18.5 %all-to-all-start.3 = ((bf16[8,256,64]{1,2,0:T(8,128)(2,1)}), bf16[8,256,64]{1,2,0:T(8,128)(2,1)S(1)}, u32[]{:S(2)}, u32[]{:S(2)}) async-start(bf16[8,256,64]{1,2,0:T(8,128)(2,1)} %bitcast.41), calls=%async_computation.3 | async-start | bytes 524288 | tf_op jit(solution)/shard_map/all_to_all | solution.py:129
Sparse Core Ops, SparseCore 0:
  51.9 58.3 all-gather.2
  121.4 95.5 all-gather.4

commit v13 on v11

--- a/solution.py
+++ b/solution.py
@@ -63,8 +63,6 @@
     total_slots = groups * capacity
     source_group = lax.axis_index("expert")
 
-    rank_w = adapter_in[0]
-    rank_cols_w = lax.all_to_all(rank_w, "mp", split_axis=1, concat_axis=0, tiled=True)
     gate_up_w = jnp.concatenate([gate_weight[0], up_weight[0]], axis=0)
     down_cols_w = lax.all_to_all(down_weight[0], "mp", split_axis=1, concat_axis=0, tiled=True)
 
@@ -72,6 +70,8 @@
         request_lengths, request_adapter, request_order, source_group * tok_rows, tok_rows
     )
     slot_index = expert_slots(expert_route, groups, capacity)
+    slot_index, rank_w = lax.optimization_barrier((slot_index, adapter_in[0]))
+    rank_cols_w = lax.all_to_all(rank_w, "mp", split_axis=1, concat_axis=0, tiled=True)
     slot_ids = jnp.arange(total_slots, dtype=jnp.int32)[:, None]
     seat = (
         (slot_index[None, :, 0] == slot_ids) | (slot_index[None, :, 1] == slot_ids)

time: 256 us -> 256 us (level)
  transfers between devices with their start and end apart: 5 -> 5, of which waited for: 5 -> 5; matrix products, arithmetic and copies ran while one was open for 3% -> 2% of each run, Pallas kernels for 0% -> 0%
where the time goes in v13:
time: 256 us; the launch traced here: 255 us
  waiting for transfers between devices  153 us (60%)
  blocking collectives  25.8 us (10%)
  matrix products  23.8 us (9%)
  starting transfers between devices  23.6 us (9%)
  between operations  13.7 us (5%)
  local copies, waits for them, and re-layouts  11.6 us (5%)
  other arithmetic  4.21 us (2%)
    all_gather x1, waiting for transfers between devices, on_device(): hidden_full = lax.all_gather(hidden, 'mp', axis=1, tiled=True)  66.8 us
    all_gather x1, waiting for transfers between devices, on_device(): gathered = lax.all_gather(payload2, 'mp', axis=1, tiled=True)  56.1 us
    all_to_all x1, blocking collectives, on_device(): lax.all_to_all(down_weight[0], 'mp', split_axis=1, concat_axis=0, tiled=T...  25.8 us
    all_to_all x1, waiting for transfers between devices, on_device(): lax.all_to_all(payload.reshape(groups * chunk, local_feat), 'expert', spl...  14.9 us
    all_to_all x1, waiting for transfers between devices, on_device(): lax.all_to_all(down_local, 'expert', split_axis=0, concat_axis=0, tiled=T...  11.7 us
    dot_general x1, matrix products, on_device(): jnp.dot(hidden_full, down_cols_w, preferred_element_type=jnp.float32)  9.78 us
    dot_general x3, matrix products, contract_last(): lax.dot_general(left, right, (((1,), (1,)), ((), ())), preferred_element_...  8.96 us
    all_to_all x1, starting transfers between devices, on_device(): lax.all_to_all(rank_w, 'mp', split_axis=1, concat_axis=0, tiled=True)  8.58 us
  transfers between devices with their start and end apart: 5, of which 5 were waited for; matrix products, arithmetic and copies ran while one was open for 2% of the time, Pallas kernels for 0%

profile of v13, /device:TPU:1, one launch (start us, length us, event | category | flops | bytes accessed | tf_op | source)
XLA Modules:
  0.0 255.4 jit_solution(17025278439713077966)
XLA Ops:
  6.5 0.9 copy.90
  7.6 0.5 fusion.30
  8.4 0.7 multiply_add_fusion
  9.1 1.2 all_to_all.39
  10.4 0.8 reshape.151
  11.2 8.6 %all-to-all-start.1 = ((bf16[32,2,1024]{2,1,0:T(2,128)(2,1)}), bf16[32,2,1024]{2,1,0:T(2,128)(2,1)S(1)}, u32[]{:S(2)}, u32[]{:S(2)}) async-start(bf16[32,2,1024]{2,1,0:T(2,128)(2,1)} %reshape.151), calls=%async_computation.1 | async-start | bytes 262144 | tf_op jit(solution)/shard_map/all_to_all | solution.py:74
  19.8 0.9 select_reduce_fusion.2
  21.2 0.9 fusion.6
  22.1 1.1 fusion.12
  23.5 0.8 pad_maximum_fusion
  24.3 3.2 %all-to-all-done.1 = bf16[32,2,1024]{2,1,0:T(2,128)(2,1)S(1)} async-done(((bf16[32,2,1024]{2,1,0:T(2,128)(2,1)}), bf16[32,2,1024]{2,1,0:T(2,128)(2,1)S(1)}, u32[]{:S(2)}, u32[]{:S(2)}) %all-to-all-start.1) | async-done | bytes 131104 | tf_op jit(solution)/shard_map/all_to_all | solution.py:74
  27.5 8.2 %all-to-all-start = ((bf16[8,260,64]{1,2,0:T(8,128)(2,1)}), bf16[8,260,64]{1,2,0:T(8,128)(2,1)S(1)}, u32[]{:S(2)}, u32[]{:S(2)}) async-start(bf16[8,260,64]{1,2,0:T(8,128)(2,1)} %pad_maximum_fusion), calls=%async_computation | async-start | bytes 786432 | tf_op jit(solution)/shard_map/all_to_all | solution.py:91
  36.0 14.9 %all-to-all-done = bf16[8,260,64]{1,2,0:T(8,128)(2,1)S(1)} async-done(((bf16[8,260,64]{1,2,0:T(8,128)(2,1)}), bf16[8,260,64]{1,2,0:T(8,128)(2,1)S(1)}, u32[]{:S(2)}, u32[]{:S(2)}) %all-to-all-start) | async-done | bytes 266272 | tf_op jit(solution)/shard_map/all_to_all | solution.py:91
  51.5 1.3 multiply_reduce_fusion
  53.5 0.8 pad_maximum_fusion.1
  54.3 56.1 %all-gather.3.cloned.1.call-done = bf16[2560,2048]{0,1:T(8,128)(2,1)} async-done(((bf16[2560,64]{0,1:T(8,128)(2,1)}), bf16[2560,2048]{0,1:T(8,128)(2,1)}) %all-gather.3.cloned.1.call-update) | async-done | bytes 10485776 | tf_op jit(solution)/shard_map/all_gather | solution.py:107
  110.4 1.8 slice-done
  112.2 0.3 reduce
  113.1 0.3 broadcast_multiply_fusion
  113.6 5.5 %fusion = f32[2048,352]{0,1:T(8,128)S(1)} fusion(bf16[2560,2048]{0,1:T(8,128)(2,1)} %all-gather.3.cloned.1.call-done, bf16[176,2048]{1,0:T(8,128)(2,1)S(1)} %bitcast.72, bf16[176,2048]{1,0:T(8,128)(2,1)S(1)} %bitcast.73), kind=kOutput, calls=%fused_computation | convolution fusion | flops 2955673600 | bytes 12713984 | tf_op jit(solution)/shard_map/dot_general | solution.py:41
  119.2 2.2 fusion.11
  121.4 0.5 copy.104
  121.9 25.8 %all_to_all.53 = bf16[176,32,64]{0,2,1:T(8,128)(2,1)S(1)} all-to-all(bf16[176,32,64]{0,2,1:T(8,128)(2,1)S(1)} %bitcast.49), channel_id=1, replica_groups=mesh['expert'=8,'mp'=32] {'mp'}, dimensions={1} | all-to-all | bytes 1441792 | tf_op jit(solution)/shard_map/all_to_all | solution.py:67
  147.7 0.6 copy.105
  148.3 1.9 all_to_all.45
  150.2 66.8 %all-gather.5.cloned.1.call-done = bf16[2048,5632]{0,1:T(8,128)(2,1)} async-done(((bf16[2048,176]{0,1:T(8,128)(2,1)}), bf16[2048,5632]{0,1:T(8,128)(2,1)}) %all-gather.5.cloned.1.call-update) | async-done | bytes 23068688 | tf_op jit(solution)/shard_map/all_gather | solution.py:125
  217.1 9.8 %convolution_convert_fusion = bf16[2048,64]{0,1:T(8,128)(2,1)S(1)} fusion(bf16[5632,64]{0,1:T(8,128)(2,1)S(1)} %all_to_all.45, bf16[2048,5632]{0,1:T(8,128)(2,1)} %all-gather.5.cloned.1.call-done), kind=kOutput, calls=%fused_computation.17 | convolution fusion | flops 1476526080 | bytes 24051712 | tf_op jit(solution)/shard_map/dot_general | solution.py:126
  226.8 0.7 copy.118
  227.6 6.7 %all-to-all-start.3 = ((bf16[8,256,64]{1,2,0:T(8,128)(2,1)}), bf16[8,256,64]{1,2,0:T(8,128)(2,1)S(1)}, u32[]{:S(2)}, u32[]{:S(2)}) async-start(bf16[8,256,64]{1,2,0:T(8,128)(2,1)} %bitcast.45), calls=%async_computation.3 | async-start | bytes 524288 | tf_op jit(solution)/shard_map/all_to_all | solution.py:129
  234.3 11.7 %all-to-all-done.3 = bf16[8,256,64]{1,2,0:T(8,128)(2,1)S(1)} async-done(((bf16[8,256,64]{1,2,0:T(8,128)(2,1)}), bf16[8,256,64]{1,2,0:T(8,128)(2,1)S(1)}, u32[]{:S(2)}, u32[]{:S(2)}) %all-to-all-start.3) | async-done | bytes 262176 | tf_op jit(solution)/shard_map/all_to_all | solution.py:129
  246.1 0.9 fusion.26
  247.0 1.6 fusion.27
  (53 shorter events, 3.8 us)
Async XLA Ops:
  6.5 112.6 %copy-start = (bf16[1,176,1024]{2,1,0:T(8,128)(2,1)S(1)}, bf16[1,176,1024]{2,1,0:T(8,128)(2,1)}, u32[]{:S(2)}) copy-start(bf16[1,176,1024]{2,1,0:T(8,128)(2,1)} %param.21) | copy-start | bytes 1081348
  6.5 15.6 %copy-start.5 = (bf16[512,64]{0,1:T(8,128)(2,1)S(1)}, bf16[512,64]{0,1:T(8,128)(2,1)}, u32[]{:S(2)}) copy-start(bf16[512,64]{0,1:T(8,128)(2,1)} %param.11) | copy-start | bytes 196612
  11.2 16.3 %all-to-all-start.1 = ((bf16[32,2,1024]{2,1,0:T(2,128)(2,1)}), bf16[32,2,1024]{2,1,0:T(2,128)(2,1)S(1)}, u32[]{:S(2)}, u32[]{:S(2)}) async-start(bf16[32,2,1024]{2,1,0:T(2,128)(2,1)} %reshape.151), calls=%async_computation.1 | async-start | bytes 262144 | tf_op jit(solution)/shard_map/all_to_all | solution.py:74
  27.5 23.3 %all-to-all-start = ((bf16[8,260,64]{1,2,0:T(8,128)(2,1)}), bf16[8,260,64]{1,2,0:T(8,128)(2,1)S(1)}, u32[]{:S(2)}, u32[]{:S(2)}) async-start(bf16[8,260,64]{1,2,0:T(8,128)(2,1)} %pad_maximum_fusion), calls=%async_computation | async-start | bytes 786432 | tf_op jit(solution)/shard_map/all_to_all | solution.py:91
  35.7 74.7 %all-gather.3.cloned.1.call-start = ((), (), s32[]{:S(2)}) async-start(), calls=%async_computation.4 | async-start | bytes 10813440 | tf_op jit(solution)/shard_map/all_gather | solution.py:107
  54.3 162.8 %all-gather.5.cloned.1.call-start = ((), (), s32[]{:S(2)}) async-start(), calls=%async_computation.5 | async-start | bytes 23789568 | tf_op jit(solution)/shard_map/all_gather | solution.py:125
  110.4 1.8 slice-start
  110.4 3.0 %copy-start.3 = (bf16[1,176,2048]{2,1,0:T(8,128)(2,1)S(1)}, bf16[1,176,2048]{2,1,0:T(8,128)(2,1)}, u32[]{:S(2)}) copy-start(bf16[1,176,2048]{2,1,0:T(8,128)(2,1)} %param.18) | copy-start | bytes 2162692
  112.5 1.1 copy-start.4
  119.2 2.2 copy-start.1
  150.2 84.1 %copy-start.2 = (f32[512,2]{0,1:T(2,128)S(1)}, f32[512,2]{0,1:T(2,128)}, u32[]{:S(2)}) copy-start(f32[512,2]{0,1:T(2,128)} %param.13) | copy-start | bytes 12292
  227.6 18.5 %all-to-all-start.3 = ((bf16[8,256,64]{1,2,0:T(8,128)(2,1)}), bf16[8,256,64]{1,2,0:T(8,128)(2,1)S(1)}, u32[]{:S(2)}, u32[]{:S(2)}) async-start(bf16[8,256,64]{1,2,0:T(8,128)(2,1)} %bitcast.45), calls=%async_computation.3 | async-start | bytes 524288 | tf_op jit(solution)/shard_map/all_to_all | solution.py:129
Sparse Core Ops, SparseCore 0:
  54.4 55.9 all-gather.2
  121.5 95.5 all-gather.4
